TPU v7x, 128 devices: a whole 4x4x4 slice. The times are simulated.
128 devices in a mesh: fsdp: 8 (over x, core), dp: 16 (over z, y).
Axes of the slice: x: 4, y: 4, z: 4, core: 2. Of those that a mesh axis runs over, the one named last changes fastest.
Arguments:
- patch_states: bfloat16 [131072, 1280], P(('fsdp', 'dp')), may hold values from -6 to 6
- segment_ids: int32 [131072], P(('fsdp', 'dp')), may hold values from 0 to 63, as said below
- first_gain: float32 [1280], replicated, may hold values from 0.1 to 1.9
- first_shift: float32 [1280], replicated, may hold values from -3 to 3
- qkv_weight: bfloat16 [3840, 1280], P(('fsdp', 'dp')), may hold values from -1.5 to 1.5
- qkv_bias: float32 [3840], replicated, may hold values from -3 to 3
- out_weight: bfloat16 [1280, 1280], P(('fsdp', 'dp')), may hold values from -0.15625 to 0.15625
- out_bias: float32 [1280], replicated, may hold values from -3 to 3
- second_gain: float32 [1280], replicated, may hold values from 0.1 to 1.9
- second_shift: float32 [1280], replicated, may hold values from -3 to 3
- merge_weight: bfloat16 [1280, 5120], P(('fsdp', 'dp')), may hold values from -0.078125 to 0.078125
- merge_bias: float32 [1280], replicated, may hold values from -3 to 3
- dest_device: int32 [32768], P(('fsdp', 'dp')), may hold values from 0 to 127, as said below
- dest_slot: int32 [32768], P(('fsdp', 'dp')), may hold values from 0 to 255, as said below
Outputs:
- requests: bfloat16 [32768, 1280], P(('fsdp', 'dp'))
Inputs may be any that keep to these rules, and one draw needn't show every extreme that they name: `segment_ids`: within each device's 1024 tokens the ids start at 0, never fall, and change only between aligned groups of 4 tokens. `dest_device`: every device receives exactly 256 merged rows; the rows from one device to one device number 0, 2 or 4, and 4 for some pairs. The pairs of dest_device and dest_slot are all different.
All inputs are finite; a program needn't handle non-finite values.
Results may differ from a plain program's by a relative error of at most 0.0062.
Values may be sent and summed in bfloat16 or wider, within the bound.
No kernel may reach another device: no remote copies, remote signals or barrier semaphores. Data moves between devices by JAX's collectives and lax.ppermute only.
A program may use at most 128 MiB of HBM per device.

v0:
```python
import math

import jax
import jax.numpy as jnp
from jax import lax
from jax.sharding import PartitionSpec as P

D = 1280
H = 16
HD = 80


EPSILON = 1e-06


def layer_norm(states, gain, shift):
    values = states.astype(jnp.float32)
    center = jnp.mean(values, axis=-1, keepdims=True)
    spread = jnp.mean(jnp.square(values - center), axis=-1, keepdims=True)
    return (values - center) * lax.rsqrt(spread + EPSILON) * gain + shift


def times_rows(left, piece):
    return lax.dot_general(
        left, piece, (((1,), (1,)), ((), ())), preferred_element_type=jnp.float32
    )


def project(weight, apply_rows):
    whole = lax.all_gather(weight, ("fsdp", "dp"), axis=0, tiled=True)
    result = apply_rows(whole, 0)
    return result


def softmax_rows(scores, query_ids, key_ids):
    same = query_ids[:, None] == key_ids[None, :]
    masked = jnp.where(same[None], scores, -jnp.inf)
    top = jnp.max(masked, axis=-1, keepdims=True)
    expo = jnp.exp(masked - top)
    return (expo / jnp.sum(expo, axis=-1, keepdims=True)).astype(jnp.bfloat16)


def attend_block(query_rows, key_rows, value_rows, query_ids, key_ids, scale):
    scores = (
        jnp.einsum("qhd,khd->hqk", query_rows, key_rows, preferred_element_type=jnp.float32) * scale
    )
    probs = softmax_rows(scores, query_ids, key_ids)
    total = jnp.einsum("hqk,khd->qhd", probs, value_rows, preferred_element_type=jnp.float32)
    return total


def per_device(
    patch_states,
    segment_ids,
    first_gain,
    first_shift,
    qkv_weight,
    qkv_bias,
    out_weight,
    out_bias,
    second_gain,
    second_shift,
    merge_weight,
    merge_bias,
    dest_device,
    dest_slot,
):
    tokens = patch_states.shape[0]
    width = D
    head_dim = HD
    group = min(4, H)
    group_count = H // group
    group_width = group * head_dim
    block = min(512, tokens)
    scale = 1.0 / math.sqrt(head_dim)
    normed = layer_norm(patch_states, first_gain, first_shift).astype(jnp.bfloat16)

    def joined_rows(piece, start):
        term = times_rows(normed, piece) + qkv_bias
        return term.astype(jnp.bfloat16)

    joined = project(qkv_weight, joined_rows)

    def per_group(group_index):
        offset = group_index * group_width
        query_cols = lax.dynamic_slice_in_dim(joined, offset, group_width, 1).reshape(
            tokens, group, head_dim
        )
        key_cols = lax.dynamic_slice_in_dim(joined, width + offset, group_width, 1).reshape(
            tokens, group, head_dim
        )
        value_cols = lax.dynamic_slice_in_dim(joined, 2 * width + offset, group_width, 1).reshape(
            tokens, group, head_dim
        )
        outputs = []
        for number in range(tokens // block):
            lower = number * block
            result = attend_block(
                query_cols[lower : lower + block],
                key_cols,
                value_cols,
                segment_ids[lower : lower + block],
                segment_ids,
                scale,
            )
            outputs.append(result.reshape(block, group_width).astype(jnp.bfloat16))
        return jnp.concatenate(outputs, axis=0)

    grouped_out = lax.map(per_group, jnp.arange(group_count, dtype=jnp.int32))
    attended = jnp.moveaxis(grouped_out, 0, 1).reshape(tokens, width)

    def hidden_rows(piece, start):
        residual = patch_states.astype(jnp.float32)
        term = times_rows(attended, piece) + out_bias + residual
        return term.astype(jnp.bfloat16)

    hidden = project(out_weight, hidden_rows)
    merged = (
        layer_norm(hidden, second_gain, second_shift)
        .astype(jnp.bfloat16)
        .reshape(tokens // 4, 4 * width)
    )

    def merged_rows(piece, start):
        term = times_rows(merged, piece) + merge_bias
        return term.astype(jnp.bfloat16)

    projected = project(merge_weight, merged_rows)
    fsdp_count = lax.axis_size("fsdp")
    dp_count = lax.axis_size("dp")
    count_dev = fsdp_count * dp_count
    row_count = tokens // 4
    capacity = 2 * (row_count // count_dev)
    matches = (dest_device[:, None] == jnp.arange(count_dev, dtype=jnp.int32)[None, :]).astype(
        jnp.int32
    )
    earlier = jnp.cumsum(matches, axis=0) - matches
    rank = jnp.sum(earlier * matches, axis=1)
    position = dest_device * capacity + rank
    rows_out = jnp.zeros((count_dev * capacity, width), jnp.bfloat16).at[position].set(projected)
    slots_out = jnp.full((count_dev * capacity,), row_count, jnp.int32).at[position].set(dest_slot)
    got_rows, got_slots = (
        lax.all_to_all(
            rows_out.reshape(count_dev, capacity, width),
            ("fsdp", "dp"),
            split_axis=0,
            concat_axis=0,
            tiled=True,
        ),
        lax.all_to_all(
            slots_out.reshape(count_dev, capacity),
            ("fsdp", "dp"),
            split_axis=0,
            concat_axis=0,
            tiled=True,
        ),
    )
    requests = (
        jnp.zeros((row_count, width), jnp.bfloat16)
        .at[got_slots.reshape(-1)]
        .set(got_rows.reshape(-1, width), mode="drop")
    )
    return requests


def solution(mesh):
    in_specs = (
        P(("fsdp", "dp"), None),
        P(("fsdp", "dp")),
        P(),
        P(),
        P(("fsdp", "dp"), None),
        P(),
        P(("fsdp", "dp"), None),
        P(),
        P(),
        P(),
        P(("fsdp", "dp"), None),
        P(),
        P(("fsdp", "dp")),
        P(("fsdp", "dp")),
    )
    out_specs = P(("fsdp", "dp"), None)
    return jax.shard_map(
        per_device, mesh=mesh, in_specs=in_specs, out_specs=out_specs, check_vma=False
    )
```

profile of v0, /device:TPU:1, one launch (start us, length us, event | category | flops | bytes accessed | tf_op | source)
XLA Modules:
  0.0 383.7 jit_solution(8263721826374111492)
XLA Ops:
  11.4 1.6 scatter_custom_fusion
  13.7 12.0 %all-to-all-start = ((s32[128,1,4]{2,1,0:T(1,128)}), s32[128,1,4]{2,1,0:T(1,128)}, u32[]{:S(2)}, u32[]{:S(2)}) async-start(s32[128,1,4]{2,1,0:T(1,128)} %bitcast.14), calls=%async_computation | async-start | bytes 131072 | tf_op jit(solution)/shard_map/all_to_all | solution.py:150
  25.7 2.2 convert_reduce_fusion
  28.7 52.8 %all-gather.9.cloned.1.call-done = bf16[128,10,1280]{2,1,0:T(8,128)(2,1)} async-done(((bf16[1,10,1280]{2,1,0:T(8,128)(2,1)}), bf16[128,10,1280]{2,1,0:T(8,128)(2,1)}) %all-gather.9.cloned.1.call-update) | async-done | bytes 3276816 | tf_op jit(solution)/shard_map/all_gather | solution.py:30
  81.5 7.0 %reshape.219 = bf16[1280,1280]{1,0:T(8,128)(2,1)} reshape(bf16[128,10,1280]{2,1,0:T(8,128)(2,1)} %all-gather.9.cloned.1.call-done) | data formatting | bytes 6553600
  88.5 65.3 %all-gather.7.cloned.1.call-done = bf16[128,30,1280]{2,1,0:T(8,128)(2,1)} async-done(((bf16[1,30,1280]{2,1,0:T(8,128)(2,1)}), bf16[128,30,1280]{2,1,0:T(8,128)(2,1)}) %all-gather.7.cloned.1.call-update) | async-done | bytes 9830416 | tf_op jit(solution)/shard_map/all_gather | solution.py:30
  153.8 13.6 %reshape.217 = bf16[3840,1280]{1,0:T(8,128)(2,1)} reshape(bf16[128,30,1280]{2,1,0:T(8,128)(2,1)} %all-gather.7.cloned.1.call-done) | data formatting | bytes 19660800
  167.5 16.8 %add_convert_fusion = bf16[1024,3840]{1,0:T(8,128)(2,1)} fusion(bf16[3840,1280]{1,0:T(8,128)(2,1)} %reshape.217, f32[3840]{0:T(1024)S(1)} %copy-done.6, bf16[1024,1280]{1,0:T(8,128)(2,1)S(1)} %copy-done, f32[1280]{0:T(1024)S(1)} %copy-done.7, f32[1280]{0:T(1024)S(1)} %copy-done.8, f32[1024]{0:T(1024)S(1)} %add_rsqrt_fusion.1, ...), kind=kOutput, calls=%fused_computation.36 | convolution fusion | flops 10082058240 | bytes 20349952 | tf_op jit(solution)/shard_map/dot_general | solution.py:24
  184.3 10.7 %copy.22 = bf16[1024,3840]{0,1:T(8,128)(2,1)} copy(bf16[1024,3840]{1,0:T(8,128)(2,1)} %add_convert_fusion) | data formatting | bytes 15728640 | tf_op jit(solution)/shard_map/while | solution.py:109
  195.0 103.7 %while.12 = (s32[]{:T(128)}, bf16[4,1024,320]{1,2,0:T(8,128)(2,1)}, s32[4]{0:T(128)S(1)}, bf16[1024,3840]{0,1:T(8,128)(2,1)}, s32[1024]{0:T(1024)S(1)}, /*index=...) while((s32[]{:T(128)}, bf16[4,1024,320]{1,2,0:T(8,128)(2,1)}, ...), condition=%wide.region_11.12_spmd, body=%wide.region_6.11_spmd.sunk | while | flops 1370032128 | bytes 44876600 | solution.py:109
  196.2 1.4 constant_dynamic-slice_fusion.5
  197.6 1.1 constant_dynamic-slice_fusion.6
  199.4 5.3 %fusion.92 = (f32[4,512]{1,0:T(4,128)S(1)}, f32[4,512,1024]{2,1,0:T(8,128)}) fusion(pred[512,1024]{1,0:T(8,128)(4,1)S(1)} %get-tuple-element.162, bf16[512,4,80]{0,2,1:T(8,128)(2,1)S(1)} %bitcast.86, bf16[1024,4,80]{0,2,1:T(8,128)(2,1)S(1)} %bitcast.82), kind=kOutput, calls=%fused_computation.85.clone.1 | convolution fusion | flops 343933952 | bytes 9904128 | tf_op jit(solution)/shard_map/while/body/eval_jaxpr/sub | solution.py:39
  204.7 5.0 %fusion.93 = bf16[4,80,512]{2,1,0:T(8,128)(2,1)S(1)} fusion(bf16[1024,4,80]{0,2,1:T(8,128)(2,1)S(1)} %bitcast.80, f32[4,512,1024]{2,1,0:T(8,128)} %get-tuple-element.164, f32[4,512]{1,0:T(4,128)S(1)} %get-tuple-element.165), kind=kOutput, calls=%fused_computation.22.clone.1 | convolution fusion | flops 339902464 | bytes 9379840 | tf_op jit(solution)/shard_map/while/body/eval_jaxpr/hqk,khd->qhd/dot_general | solution.py:48
  209.7 5.3 %fusion.90 = (f32[4,512]{1,0:T(4,128)S(1)}, f32[4,512,1024]{2,1,0:T(8,128)}) fusion(pred[512,1024]{1,0:T(8,128)(4,1)S(1)} %get-tuple-element.157, bf16[512,4,80]{0,2,1:T(8,128)(2,1)S(1)} %bitcast.84, bf16[1024,4,80]{0,2,1:T(8,128)(2,1)S(1)} %bitcast.83), kind=kOutput, calls=%fused_computation.84.clone.1 | convolution fusion | flops 343933952 | bytes 9904128 | tf_op jit(solution)/shard_map/while/body/eval_jaxpr/sub | solution.py:39
  215.1 5.3 %fusion.91 = bf16[4,80,512]{2,1,0:T(8,128)(2,1)S(1)} fusion(bf16[1024,4,80]{0,2,1:T(8,128)(2,1)S(1)} %bitcast.81, f32[4,512,1024]{2,1,0:T(8,128)} %get-tuple-element.160, f32[4,512]{1,0:T(4,128)S(1)} %get-tuple-element.161), kind=kOutput, calls=%fused_computation.21.clone.1 | convolution fusion | flops 339902464 | bytes 9379840 | tf_op jit(solution)/shard_map/while/body/eval_jaxpr/hqk,khd->qhd/dot_general | solution.py:48
  220.3 0.9 fusion.94
  222.4 1.4 constant_dynamic-slice_fusion.5
  223.8 1.2 constant_dynamic-slice_fusion.6
  225.7 5.3 %fusion.92 = (f32[4,512]{1,0:T(4,128)S(1)}, f32[4,512,1024]{2,1,0:T(8,128)}) fusion(pred[512,1024]{1,0:T(8,128)(4,1)S(1)} %get-tuple-element.162, bf16[512,4,80]{0,2,1:T(8,128)(2,1)S(1)} %bitcast.86, bf16[1024,4,80]{0,2,1:T(8,128)(2,1)S(1)} %bitcast.82), kind=kOutput, calls=%fused_computation.85.clone.1 | convolution fusion | flops 343933952 | bytes 9904128 | tf_op jit(solution)/shard_map/while/body/eval_jaxpr/sub | solution.py:39
  231.0 5.1 %fusion.93 = bf16[4,80,512]{2,1,0:T(8,128)(2,1)S(1)} fusion(bf16[1024,4,80]{0,2,1:T(8,128)(2,1)S(1)} %bitcast.80, f32[4,512,1024]{2,1,0:T(8,128)} %get-tuple-element.164, f32[4,512]{1,0:T(4,128)S(1)} %get-tuple-element.165), kind=kOutput, calls=%fused_computation.22.clone.1 | convolution fusion | flops 339902464 | bytes 9379840 | tf_op jit(solution)/shard_map/while/body/eval_jaxpr/hqk,khd->qhd/dot_general | solution.py:48
  236.2 5.3 %fusion.90 = (f32[4,512]{1,0:T(4,128)S(1)}, f32[4,512,1024]{2,1,0:T(8,128)}) fusion(pred[512,1024]{1,0:T(8,128)(4,1)S(1)} %get-tuple-element.157, bf16[512,4,80]{0,2,1:T(8,128)(2,1)S(1)} %bitcast.84, bf16[1024,4,80]{0,2,1:T(8,128)(2,1)S(1)} %bitcast.83), kind=kOutput, calls=%fused_computation.84.clone.1 | convolution fusion | flops 343933952 | bytes 9904128 | tf_op jit(solution)/shard_map/while/body/eval_jaxpr/sub | solution.py:39
  241.5 4.8 %fusion.91 = bf16[4,80,512]{2,1,0:T(8,128)(2,1)S(1)} fusion(bf16[1024,4,80]{0,2,1:T(8,128)(2,1)S(1)} %bitcast.81, f32[4,512,1024]{2,1,0:T(8,128)} %get-tuple-element.160, f32[4,512]{1,0:T(4,128)S(1)} %get-tuple-element.161), kind=kOutput, calls=%fused_computation.21.clone.1 | convolution fusion | flops 339902464 | bytes 9379840 | tf_op jit(solution)/shard_map/while/body/eval_jaxpr/hqk,khd->qhd/dot_general | solution.py:48
  246.4 1.0 fusion.94
  248.5 1.4 constant_dynamic-slice_fusion.5
  249.9 1.1 constant_dynamic-slice_fusion.6
  251.7 5.3 %fusion.92 = (f32[4,512]{1,0:T(4,128)S(1)}, f32[4,512,1024]{2,1,0:T(8,128)}) fusion(pred[512,1024]{1,0:T(8,128)(4,1)S(1)} %get-tuple-element.162, bf16[512,4,80]{0,2,1:T(8,128)(2,1)S(1)} %bitcast.86, bf16[1024,4,80]{0,2,1:T(8,128)(2,1)S(1)} %bitcast.82), kind=kOutput, calls=%fused_computation.85.clone.1 | convolution fusion | flops 343933952 | bytes 9904128 | tf_op jit(solution)/shard_map/while/body/eval_jaxpr/sub | solution.py:39
  257.0 4.8 %fusion.93 = bf16[4,80,512]{2,1,0:T(8,128)(2,1)S(1)} fusion(bf16[1024,4,80]{0,2,1:T(8,128)(2,1)S(1)} %bitcast.80, f32[4,512,1024]{2,1,0:T(8,128)} %get-tuple-element.164, f32[4,512]{1,0:T(4,128)S(1)} %get-tuple-element.165), kind=kOutput, calls=%fused_computation.22.clone.1 | convolution fusion | flops 339902464 | bytes 9379840 | tf_op jit(solution)/shard_map/while/body/eval_jaxpr/hqk,khd->qhd/dot_general | solution.py:48
  261.9 5.3 %fusion.90 = (f32[4,512]{1,0:T(4,128)S(1)}, f32[4,512,1024]{2,1,0:T(8,128)}) fusion(pred[512,1024]{1,0:T(8,128)(4,1)S(1)} %get-tuple-element.157, bf16[512,4,80]{0,2,1:T(8,128)(2,1)S(1)} %bitcast.84, bf16[1024,4,80]{0,2,1:T(8,128)(2,1)S(1)} %bitcast.83), kind=kOutput, calls=%fused_computation.84.clone.1 | convolution fusion | flops 343933952 | bytes 9904128 | tf_op jit(solution)/shard_map/while/body/eval_jaxpr/sub | solution.py:39
  267.2 4.8 %fusion.91 = bf16[4,80,512]{2,1,0:T(8,128)(2,1)S(1)} fusion(bf16[1024,4,80]{0,2,1:T(8,128)(2,1)S(1)} %bitcast.81, f32[4,512,1024]{2,1,0:T(8,128)} %get-tuple-element.160, f32[4,512]{1,0:T(4,128)S(1)} %get-tuple-element.161), kind=kOutput, calls=%fused_computation.21.clone.1 | convolution fusion | flops 339902464 | bytes 9379840 | tf_op jit(solution)/shard_map/while/body/eval_jaxpr/hqk,khd->qhd/dot_general | solution.py:48
  272.0 1.0 fusion.94
  274.2 1.4 constant_dynamic-slice_fusion.5
  275.6 1.1 constant_dynamic-slice_fusion.6
  277.4 5.3 %fusion.92 = (f32[4,512]{1,0:T(4,128)S(1)}, f32[4,512,1024]{2,1,0:T(8,128)}) fusion(pred[512,1024]{1,0:T(8,128)(4,1)S(1)} %get-tuple-element.162, bf16[512,4,80]{0,2,1:T(8,128)(2,1)S(1)} %bitcast.86, bf16[1024,4,80]{0,2,1:T(8,128)(2,1)S(1)} %bitcast.82), kind=kOutput, calls=%fused_computation.85.clone.1 | convolution fusion | flops 343933952 | bytes 9904128 | tf_op jit(solution)/shard_map/while/body/eval_jaxpr/sub | solution.py:39
  282.7 4.8 %fusion.93 = bf16[4,80,512]{2,1,0:T(8,128)(2,1)S(1)} fusion(bf16[1024,4,80]{0,2,1:T(8,128)(2,1)S(1)} %bitcast.80, f32[4,512,1024]{2,1,0:T(8,128)} %get-tuple-element.164, f32[4,512]{1,0:T(4,128)S(1)} %get-tuple-element.165), kind=kOutput, calls=%fused_computation.22.clone.1 | convolution fusion | flops 339902464 | bytes 9379840 | tf_op jit(solution)/shard_map/while/body/eval_jaxpr/hqk,khd->qhd/dot_general | solution.py:48
  287.5 5.3 %fusion.90 = (f32[4,512]{1,0:T(4,128)S(1)}, f32[4,512,1024]{2,1,0:T(8,128)}) fusion(pred[512,1024]{1,0:T(8,128)(4,1)S(1)} %get-tuple-element.157, bf16[512,4,80]{0,2,1:T(8,128)(2,1)S(1)} %bitcast.84, bf16[1024,4,80]{0,2,1:T(8,128)(2,1)S(1)} %bitcast.83), kind=kOutput, calls=%fused_computation.84.clone.1 | convolution fusion | flops 343933952 | bytes 9904128 | tf_op jit(solution)/shard_map/while/body/eval_jaxpr/sub | solution.py:39
  292.9 4.8 %fusion.91 = bf16[4,80,512]{2,1,0:T(8,128)(2,1)S(1)} fusion(bf16[1024,4,80]{0,2,1:T(8,128)(2,1)S(1)} %bitcast.81, f32[4,512,1024]{2,1,0:T(8,128)} %get-tuple-element.160, f32[4,512]{1,0:T(4,128)S(1)} %get-tuple-element.161), kind=kOutput, calls=%fused_computation.21.clone.1 | convolution fusion | flops 339902464 | bytes 9379840 | tf_op jit(solution)/shard_map/while/body/eval_jaxpr/hqk,khd->qhd/dot_general | solution.py:48
  298.7 7.3 %convert_reduce_fusion.1 = (f32[1024]{0:T(1024)S(1)}, bf16[1024,1280]{1,0:T(8,128)(2,1)S(1)}) fusion(bf16[1024,1280]{1,0:T(8,128)(2,1)} %param.16, f32[1280]{0:T(1024)S(1)} %copy-done.9, bf16[1024,1280]{0,1:T(8,128)(2,1)} %bitcast.18, bf16[1280,1280]{1,0:T(8,128)(2,1)} %reshape.219), kind=kOutput, calls=%fused_computation.41 | convolution fusion | flops 3363306496 | bytes 11150336 | tf_op jit(solution)/shard_map/dot_general | solution.py:24
  306.9 1.0 fusion.34
  307.9 2.9 reshape.187
  310.8 24.6 %reshape.221 = bf16[1280,5120]{1,0:T(8,128)(2,1)} reshape(bf16[128,10,5120]{2,1,0:T(8,128)(2,1)} %all-gather.11.cloned.1.call-done) | data formatting | bytes 26214400
  335.4 6.7 %fusion.41 = bf16[256,1280]{1,0:T(8,128)(2,1)S(1)} fusion(bf16[256,5120]{1,0:T(8,128)(2,1)S(1)} %copy-done.1, bf16[1280,5120]{1,0:T(8,128)(2,1)} %reshape.221, f32[1280]{0:T(1024)S(1)} %copy-done.10), kind=kOutput, calls=%fused_computation.60 | convolution fusion | flops 3356098560 | bytes 16389120 | tf_op jit(solution)/shard_map/dot_general | solution.py:24
  342.2 2.3 scatter_custom_fusion.1
  344.5 1.2 reshape.188
  345.7 6.3 %all-to-all-start.1 = ((bf16[128,4,1280]{2,1,0:T(4,128)(2,1)}), bf16[128,4,1280]{2,1,0:T(4,128)(2,1)S(1)}, u32[]{:S(2)}, u32[]{:S(2)}) async-start(bf16[128,4,1280]{2,1,0:T(4,128)(2,1)} %reshape.188), calls=%async_computation.1 | async-start | bytes 2621440 | tf_op jit(solution)/shard_map/all_to_all | solution.py:143
  352.5 1.6 reduce.3
  354.2 19.1 %all-to-all-done.1 = bf16[128,4,1280]{2,1,0:T(4,128)(2,1)S(1)} async-done(((bf16[128,4,1280]{2,1,0:T(4,128)(2,1)}), bf16[128,4,1280]{2,1,0:T(4,128)(2,1)S(1)}, u32[]{:S(2)}, u32[]{:S(2)}) %all-to-all-start.1) | async-done | bytes 1310752 | tf_op jit(solution)/shard_map/all_to_all | solution.py:143
  373.7 3.5 scatter_custom_fusion.2
  (66 shorter events, 14.1 us)
Async XLA Ops:
  6.5 21.3 %copy-start = (bf16[1024,1280]{1,0:T(8,128)(2,1)S(1)}, bf16[1024,1280]{1,0:T(8,128)(2,1)}, u32[]{:S(2)}) copy-start(bf16[1024,1280]{1,0:T(8,128)(2,1)} %param.16) | copy-start | bytes 7864324
  6.5 75.0 %all-gather.9.cloned.1.call-start = ((), (), s32[]{:S(2)}) async-start(), calls=%async_computation.3 | async-start | bytes 5283840 | tf_op jit(solution)/shard_map/all_gather | solution.py:30
  7.3 146.6 %all-gather.7.cloned.1.call-start = ((), (), s32[]{:S(2)}) async-start(), calls=%async_computation.2 | async-start | bytes 10567680 | tf_op jit(solution)/shard_map/all_gather | solution.py:30
  8.0 302.8 %all-gather.11.cloned.1.call-start = ((), (), s32[]{:S(2)}) async-start(), calls=%async_computation.4 | async-start | bytes 21135360 | tf_op jit(solution)/shard_map/all_gather | solution.py:30
  11.4 16.4 %copy-start.5 = (s32[256]{0:T(256)}, s32[256]{0:T(256)S(1)}, u32[]{:S(2)}) copy-start(s32[256]{0:T(256)S(1)} %compare_select_fusion.1) | copy-start | bytes 3076
  13.7 332.0 %all-to-all-start = ((s32[128,1,4]{2,1,0:T(1,128)}), s32[128,1,4]{2,1,0:T(1,128)}, u32[]{:S(2)}, u32[]{:S(2)}) async-start(s32[128,1,4]{2,1,0:T(1,128)} %bitcast.14), calls=%async_computation | async-start | bytes 131072 | tf_op jit(solution)/shard_map/all_to_all | solution.py:150
  88.5 78.9 %copy-start.6 = (f32[3840]{0:T(1024)S(1)}, f32[3840]{0:T(1024)}, u32[]{:S(2)}) copy-start(f32[3840]{0:T(1024)} %param.21) | copy-start | bytes 46084
  88.5 78.9 %copy-start.7 = (f32[1280]{0:T(1024)S(1)}, f32[1280]{0:T(1024)}, u32[]{:S(2)}) copy-start(f32[1280]{0:T(1024)} %param.19) | copy-start | bytes 15364
  88.5 78.9 %copy-start.8 = (f32[1280]{0:T(1024)S(1)}, f32[1280]{0:T(1024)}, u32[]{:S(2)}) copy-start(f32[1280]{0:T(1024)} %param.18) | copy-start | bytes 15364
  184.3 10.7 %copy-start.2 = (s32[1024]{0:T(1024)S(1)}, s32[1024]{0:T(1024)}, u32[]{:S(2)}) copy-start(s32[1024]{0:T(1024)} %param.17) | copy-start | bytes 12292
  195.0 103.7 %copy-start.9 = (f32[1280]{0:T(1024)S(1)}, f32[1280]{0:T(1024)}, u32[]{:S(2)}) copy-start(f32[1280]{0:T(1024)} %param.23) | copy-start | bytes 15364
  298.7 8.2 %copy-start.3 = (f32[1280]{0:T(1024)S(1)}, f32[1280]{0:T(1024)}, u32[]{:S(2)}) copy-start(f32[1280]{0:T(1024)} %param.25) | copy-start | bytes 15364
  298.7 8.2 %copy-start.4 = (f32[1280]{0:T(1024)S(1)}, f32[1280]{0:T(1024)}, u32[]{:S(2)}) copy-start(f32[1280]{0:T(1024)} %param.24) | copy-start | bytes 15364
  310.8 24.6 %copy-start.1 = (bf16[256,5120]{1,0:T(8,128)(2,1)S(1)}, bf16[256,5120]{1,0:T(8,128)(2,1)}, u32[]{:S(2)}) copy-start(bf16[256,5120]{1,0:T(8,128)(2,1)} %reshape.187) | copy-start | bytes 7864324
  310.8 24.6 %copy-start.10 = (f32[1280]{0:T(1024)S(1)}, f32[1280]{0:T(1024)}, u32[]{:S(2)}) copy-start(f32[1280]{0:T(1024)} %param.27) | copy-start | bytes 15364
  345.7 27.6 %all-to-all-start.1 = ((bf16[128,4,1280]{2,1,0:T(4,128)(2,1)}), bf16[128,4,1280]{2,1,0:T(4,128)(2,1)S(1)}, u32[]{:S(2)}, u32[]{:S(2)}) async-start(bf16[128,4,1280]{2,1,0:T(4,128)(2,1)} %reshape.188), calls=%async_computation.1 | async-start | bytes 2621440 | tf_op jit(solution)/shard_map/all_to_all | solution.py:143
Sparse Core Ops, SparseCore 0:
  10.3 71.1 all-gather.8
  84.6 69.1 all-gather.6
  156.8 85.2 all-gather.10
where the time goes:
time: 386 us; the launch traced here: 384 us
  waiting for transfers between devices  139 us (36%)
  matrix products  113 us (29%)
  local copies, waits for them, and re-layouts  82.4 us (21%)
  starting transfers between devices  18.3 us (5%)
  other arithmetic  14.7 us (4%)
  between operations  13.3 us (3%)
    all_gather x3, waiting for transfers between devices, project(): whole = lax.all_gather(weight, ('fsdp', 'dp'), axis=0, tiled=True)  118 us
    unnamed x26, local copies, waits for them, and re-layouts  45.3 us
    sub x8, matrix products, softmax_rows(): expo = jnp.exp(masked - top)  42.8 us
    dot_general x8, matrix products, attend_block(): jnp.einsum('hqk,khd->qhd', probs, value_rows, preferred_element_type=jnp....  39.5 us
    dot_general x3, matrix products, times_rows(): lax.dot_general(left, piece, (((1,), (1,)), ((), ())), preferred_element_...  30.8 us
    all_to_all x1, waiting for transfers between devices, per_device(): lax.all_to_all(rows_out.reshape(count_dev, capacity, width), ('fsdp', 'dp...  19.1 us
    all_to_all x1, starting transfers between devices, per_device(): lax.all_to_all(slots_out.reshape(count_dev, capacity), ('fsdp', 'dp'), sp...  12 us
    while x1, local copies, waits for them, and re-layouts, per_device(): grouped_out = lax.map(per_group, jnp.arange(group_count, dtype=jnp.int32))  10.7 us
  transfers between devices with their start and end apart: 5, of which 3 were waited for; matrix products, arithmetic and copies ran while one was open for 54% of the time, Pallas kernels for 0%

commit v1 on v0

v1 whole, which is shorter than its diff:
```python
import functools
import math

import jax
import jax.numpy as jnp
from jax import lax
from jax.experimental import pallas as pl
from jax.experimental.pallas import tpu as pltpu
from jax.sharding import PartitionSpec as P

D = 1280
H = 16
HD = 80


EPSILON = 1e-06


def layer_norm(states, gain, shift):
    values = states.astype(jnp.float32)
    center = jnp.mean(values, axis=-1, keepdims=True)
    spread = jnp.mean(jnp.square(values - center), axis=-1, keepdims=True)
    return (values - center) * lax.rsqrt(spread + EPSILON) * gain + shift


def times_rows(left, piece):
    return lax.dot_general(
        left, piece, (((1,), (1,)), ((), ())), preferred_element_type=jnp.float32
    )


def attention_kernel(scale, q_ref, k_ref, v_ref, qid_ref, kid_ref, o_ref):
    q = q_ref[...]
    k = k_ref[...]
    v = v_ref[...]
    scores = lax.dot_general(
        q, k, (((0,), (0,)), ((), ())), preferred_element_type=jnp.float32
    )
    scores = scores * scale
    same = qid_ref[...] == kid_ref[...]
    masked = jnp.where(same, scores, -jnp.inf)
    top = jnp.max(masked, axis=-1, keepdims=True)
    expo = jnp.exp(masked - top)
    total = jnp.sum(expo, axis=-1, keepdims=True)
    probs = (expo / total).astype(jnp.bfloat16)
    out = lax.dot_general(
        v, probs, (((1,), (1,)), ((), ())), preferred_element_type=jnp.float32
    )
    o_ref[...] = out.astype(o_ref.dtype)


def attention(joined_t, segment_ids, block_q):
    tokens = joined_t.shape[1]
    scale = 1.0 / math.sqrt(HD)
    qid = segment_ids.reshape(tokens, 1)
    kid = segment_ids.reshape(1, tokens)
    flops = 4 * H * tokens * tokens * HD
    cost = pl.CostEstimate(
        flops=flops,
        transcendentals=H * tokens * tokens,
        bytes_accessed=joined_t.size * 2 + tokens * D * 2,
    )
    return pl.pallas_call(
        functools.partial(attention_kernel, scale),
        out_shape=jax.ShapeDtypeStruct((D, tokens), jnp.bfloat16),
        grid=(H, tokens // block_q),
        in_specs=[
            pl.BlockSpec((HD, block_q), lambda h, i: (h, i)),
            pl.BlockSpec((HD, tokens), lambda h, i: (H + h, 0)),
            pl.BlockSpec((HD, tokens), lambda h, i: (2 * H + h, 0)),
            pl.BlockSpec((block_q, 1), lambda h, i: (i, 0)),
            pl.BlockSpec((1, tokens), lambda h, i: (0, 0)),
        ],
        out_specs=pl.BlockSpec((HD, block_q), lambda h, i: (h, i)),
        cost_estimate=cost,
    )(joined_t, joined_t, joined_t, qid, kid)


def per_device(
    patch_states,
    segment_ids,
    first_gain,
    first_shift,
    qkv_weight,
    qkv_bias,
    out_weight,
    out_bias,
    second_gain,
    second_shift,
    merge_weight,
    merge_bias,
    dest_device,
    dest_slot,
):
    tokens = patch_states.shape[0]
    width = D
    axes = ("fsdp", "dp")

    qkv_full = lax.all_gather(qkv_weight, axes, axis=0, tiled=True)
    out_rows = out_weight.shape[0]
    merge_rows = merge_weight.shape[0]
    lanes = 128
    flat = jnp.concatenate(
        [out_weight.reshape(-1, lanes), merge_weight.reshape(-1, lanes)], axis=0
    )[None]
    qkv_full, flat = lax.optimization_barrier((qkv_full, flat))
    rest = lax.all_gather(flat, axes, axis=0, tiled=True)
    devices = rest.shape[0]
    out_cut = out_rows * width // lanes
    out_full = rest[:, :out_cut].reshape(devices * out_rows, width)
    merge_full = rest[:, out_cut:].reshape(devices * merge_rows, 4 * width)

    normed = layer_norm(patch_states, first_gain, first_shift).astype(jnp.bfloat16)
    joined_t = lax.dot_general(
        qkv_full, normed, (((1,), (1,)), ((), ())), preferred_element_type=jnp.float32
    )
    joined_t = (joined_t + qkv_bias[:, None]).astype(jnp.bfloat16)

    attended_t = attention(joined_t, segment_ids, 512)

    projected_att = lax.dot_general(
        attended_t, out_full, (((0,), (1,)), ((), ())), preferred_element_type=jnp.float32
    )
    hidden = (patch_states.astype(jnp.float32) + projected_att + out_bias).astype(
        jnp.bfloat16
    )
    merged = (
        layer_norm(hidden, second_gain, second_shift)
        .astype(jnp.bfloat16)
        .reshape(tokens // 4, 4 * width)
    )
    projected = (times_rows(merged, merge_full) + merge_bias).astype(jnp.bfloat16)

    fsdp_count = lax.axis_size("fsdp")
    dp_count = lax.axis_size("dp")
    count_dev = fsdp_count * dp_count
    row_count = tokens // 4
    capacity = 2 * (row_count // count_dev)
    matches = (dest_device[:, None] == jnp.arange(count_dev, dtype=jnp.int32)[None, :]).astype(
        jnp.int32
    )
    earlier = jnp.cumsum(matches, axis=0) - matches
    rank = jnp.sum(earlier * matches, axis=1)
    position = dest_device * capacity + rank
    rows_out = jnp.zeros((count_dev * capacity, width), jnp.bfloat16).at[position].set(projected)
    slots_out = jnp.full((count_dev * capacity,), row_count, jnp.int32).at[position].set(dest_slot)
    got_rows, got_slots = (
        lax.all_to_all(
            rows_out.reshape(count_dev, capacity, width),
            axes,
            split_axis=0,
            concat_axis=0,
            tiled=True,
        ),
        lax.all_to_all(
            slots_out.reshape(count_dev, capacity),
            axes,
            split_axis=0,
            concat_axis=0,
            tiled=True,
        ),
    )
    requests = (
        jnp.zeros((row_count, width), jnp.bfloat16)
        .at[got_slots.reshape(-1)]
        .set(got_rows.reshape(-1, width), mode="drop")
    )
    return requests


def solution(mesh):
    in_specs = (
        P(("fsdp", "dp"), None),
        P(("fsdp", "dp")),
        P(),
        P(),
        P(("fsdp", "dp"), None),
        P(),
        P(("fsdp", "dp"), None),
        P(),
        P(),
        P(),
        P(("fsdp", "dp"), None),
        P(),
        P(("fsdp", "dp")),
        P(("fsdp", "dp")),
    )
    out_specs = P(("fsdp", "dp"), None)
    return jax.shard_map(
        per_device, mesh=mesh, in_specs=in_specs, out_specs=out_specs, check_vma=False
    )
```

time: 386 us -> 279 us (0.72)
  matrix products: 113 us -> 31.4 us
  Pallas kernels: 0 us -> 45.4 us
  waiting for transfers between devices: 139 us -> 101 us
  local copies, waits for them, and re-layouts: 82.4 us -> 68.4 us
  other arithmetic: 14.7 us -> 5.04 us
  starting transfers between devices: 18.3 us -> 13.3 us
    pallas_call x0 -> x1, Pallas kernels: none -> 45.4 us  [attention(): pl.pallas_call(functools.partial(attention_kernel, scale), out_shape=jax....]
    unnamed x26 -> x23, local copies, waits for them, and re-layouts: 45.3 us -> 0.05 us
    sub x8 -> x0, matrix products: 42.8 us -> none  [softmax_rows(): expo = jnp.exp(masked - top)]
    all_gather x3 -> x2, waiting for transfers between devices: 118 us -> 80 us  [the longest x1 76 us: per_device(): qkv_full = lax.all_gather(qkv_weight, axes, axis=0, tiled=True)]
    reshape x0 -> x5, local copies, waits for them, and re-layouts: none -> 27.2 us  [the longest x1 19.7 us: per_device(): merge_full = rest[:, out_cut:].reshape(devices * merge_rows, 4 * width)]
    dot_general x3 -> x1, matrix products: 30.8 us -> 6.72 us  [times_rows(): lax.dot_general(left, piece, (((1,), (1,)), ((), ())), preferred_element_...]
    dot_general x8 -> x2, matrix products: 39.5 us -> 24.7 us  [the longest x1 17.4 us: per_device(): lax.dot_general(qkv_full, normed, (((1,), (1,)), ((), ())), preferred_ele...]
    optimization_barrier x0 -> x1, local copies, waits for them, and re-layouts: none -> 13.6 us  [per_device(): qkv_full, flat = lax.optimization_barrier((qkv_full, flat))]
  transfers between devices with their start and end apart: 5 -> 4, of which waited for: 3 -> 3; matrix products, arithmetic and copies ran while one was open for 54% -> 30% of each run, Pallas kernels for 0% -> 16%
where the time goes in v1:
time: 279 us; the launch traced here: 278 us
  waiting for transfers between devices  101 us (36%)
  local copies, waits for them, and re-layouts  68.4 us (25%)
  Pallas kernels  45.4 us (16%)
  matrix products  31.4 us (11%)
  between operations  13.6 us (5%)
  starting transfers between devices  13.3 us (5%)
  other arithmetic  5.04 us (2%)
    all_gather x1, waiting for transfers between devices, per_device(): qkv_full = lax.all_gather(qkv_weight, axes, axis=0, tiled=True)  76 us
    pallas_call x1, Pallas kernels, attention(): pl.pallas_call(functools.partial(attention_kernel, scale), out_shape=jax....  45.4 us
    all_to_all x1, waiting for transfers between devices, per_device(): lax.all_to_all(rows_out.reshape(count_dev, capacity, width), axes, split_...  19.9 us
    reshape x1, local copies, waits for them, and re-layouts, per_device(): merge_full = rest[:, out_cut:].reshape(devices * merge_rows, 4 * width)  19.7 us
    dot_general x1, matrix products, per_device(): lax.dot_general(qkv_full, normed, (((1,), (1,)), ((), ())), preferred_ele...  17.4 us
    optimization_barrier x1, local copies, waits for them, and re-layouts, per_device(): qkv_full, flat = lax.optimization_barrier((qkv_full, flat))  13.6 us
    slice x1, local copies, waits for them, and re-layouts, per_device(): merge_full = rest[:, out_cut:].reshape(devices * merge_rows, 4 * width)  12.4 us
    dot_general x1, matrix products, per_device(): lax.dot_general(attended_t, out_full, (((0,), (1,)), ((), ())), preferred...  7.33 us
  transfers between devices with their start and end apart: 4, of which 3 were waited for; matrix products, arithmetic and copies ran while one was open for 30% of the time, Pallas kernels for 16%

profile of v1, /device:TPU:1, one launch (start us, length us, event | category | flops | bytes accessed | tf_op | source)
XLA Modules:
  0.0 277.8 jit_solution(358819465433723233)
XLA Ops:
  6.5 0.0 all-gather.6.cloned.1.call-start
  6.5 0.7 all-gather.6.cloned.1.call-update
  7.3 0.0 all-gather.4.cloned.1.call-start
  7.3 1.0 reshape.113
  8.3 0.8 reshape.112
  9.1 0.7 maximum_bitcast_fusion
  9.8 76.0 %all-gather.6.cloned.1.call-done = bf16[128,30,1280]{2,1,0:T(8,128)(2,1)} async-done(((bf16[1,30,1280]{2,1,0:T(8,128)(2,1)}), bf16[128,30,1280]{2,1,0:T(8,128)(2,1)}) %all-gather.6.cloned.1.call-update) | async-done | bytes 9830416 | tf_op jit(solution)/shard_map/all_gather | solution.py:99
  85.8 13.6 %reshape.148 = bf16[3840,1280]{1,0:T(8,128)(2,1)} reshape(bf16[128,30,1280]{2,1,0:T(8,128)(2,1)} %all-gather.6.cloned.1.call-done) | data formatting | bytes 19660800 | tf_op jit(solution)/shard_map/optimization_barrier | solution.py:106
  99.5 0.0 all-gather.4.cloned.1.call-update
  99.5 0.0 copy-done.2
  99.5 0.1 copy.18
  99.6 0.2 fusion.24
  99.9 0.2 fusion.26
  100.1 1.6 scatter_custom_fusion
  101.7 0.7 all_to_all.9
  102.4 6.0 %all-to-all-start = ((s32[128,1,4]{2,1,0:T(1,128)}), s32[128,1,4]{2,1,0:T(1,128)S(1)}, u32[]{:S(2)}, u32[]{:S(2)}) async-start(s32[128,1,4]{2,1,0:T(1,128)} %bitcast.4), calls=%async_computation | async-start | bytes 131072 | tf_op jit(solution)/shard_map/all_to_all | solution.py:155
  108.4 0.0 copy-done.5
  108.4 1.0 copy.21.qid_ref
  109.4 0.0 copy-done
  109.4 0.4 convert_reduce_fusion
  109.9 0.8 fusion.4
  110.7 0.0 copy-done.6
  110.7 0.0 copy-done.7
  110.7 0.0 copy-done.8
  110.7 17.4 %add_convert_fusion.q_ref.k_ref.v_ref = bf16[3840,1024]{1,0:T(8,128)(2,1)} fusion(bf16[3840,1280]{1,0:T(8,128)(2,1)} %reshape.148, f32[3840]{0:T(1024)S(1)} %copy-done.6, bf16[1024,1280]{1,0:T(8,128)(2,1)S(1)} %copy-done, f32[1280]{0:T(1024)S(1)} %copy-done.7, f32[1280]{0:T(1024)S(1)} %copy-done.8, f32[1024]{0:T(1024)S(1)} %add_rsqrt_fusion.1, ...), kind=kOutput, calls=%fused_computation.3 | convolution fusion | flops 10082058240 | bytes 20349952 | tf_op jit(solution)/shard_map/dot_general | solution.py:114
  128.1 45.4 %shard_map.136 = bf16[1280,1024]{1,0:T(8,128)(2,1)} custom-call(bf16[3840,1024]{1,0:T(8,128)(2,1)} %add_convert_fusion.q_ref.k_ref.v_ref, bf16[3840,1024]{1,0:T(8,128)(2,1)} %add_convert_fusion.q_ref.k_ref.v_ref, bf16[3840,1024]{1,0:T(8,128)(2,1)} %add_convert_fusion.q_ref.k_ref.v_ref, s32[1024,1]{1,0:T(8,128)} %copy.21.qid_ref, s32[1,1024]{1,0:T(1,128)} %bitcast.31), custom_call_target="tpu_custom_call" | custom-call | flops 5368709120 | bytes 10485760 | tf_op jit(solution)/shard_map/pallas_call | solution.py:63
  173.5 4.0 %all-gather.4.cloned.1.call-done = bf16[128,500,128]{2,1,0:T(8,128)(2,1)} async-done(((bf16[1,500,128]{2,1,0:T(8,128)(2,1)}), bf16[128,500,128]{2,1,0:T(8,128)(2,1)}) %all-gather.4.cloned.1.call-update) | async-done | bytes 16384016 | tf_op jit(solution)/shard_map/all_gather | solution.py:107
  177.5 2.0 slice-done
  179.5 4.6 %reshape.116 = bf16[1280,1280]{1,0:T(8,128)(2,1)} reshape(bf16[128,100,128]{2,1,0:T(8,128)(2,1)S(1)} %slice-done) | data formatting | bytes 6553600 | tf_op jit(solution)/shard_map/reshape | solution.py:110
  184.1 0.0 copy-done.9
  184.1 7.3 %convert_reduce_fusion.1 = (f32[1024]{0:T(1024)S(1)}, bf16[1024,1280]{1,0:T(8,128)(2,1)S(1)}) fusion(f32[1280]{0:T(1024)S(1)} %copy-done.9, bf16[1280,1024]{1,0:T(8,128)(2,1)} %shard_map.136, bf16[1280,1280]{1,0:T(8,128)(2,1)} %reshape.116, bf16[1024,1280]{1,0:T(8,128)(2,1)} %param.14), kind=kOutput, calls=%fused_computation.8 | convolution fusion | flops 3363306496 | bytes 11150336 | tf_op jit(solution)/shard_map/dot_general | solution.py:121
  191.5 0.8 fusion.8
  192.3 1.0 fusion.11
  193.4 2.9 %reshape.117 = bf16[256,5120]{1,0:T(8,128)(2,1)} reshape(bf16[1024,1280]{1,0:T(8,128)(2,1)S(1)} %fusion.11) | data formatting | bytes 5242880 | tf_op jit(solution)/shard_map/reshape | solution.py:130
  196.3 12.4 %slice.18 = bf16[128,400,128]{2,1,0:T(8,128)(2,1)} slice(bf16[128,500,128]{2,1,0:T(8,128)(2,1)} %all-gather.4.cloned.1.call-done), slice={[0:128], [100:500], [0:128]} | slice | bytes 26214400 | tf_op jit(solution)/shard_map/slice | solution.py:111
  208.7 19.7 %reshape.118 = bf16[1280,5120]{1,0:T(8,128)(2,1)} reshape(bf16[128,400,128]{2,1,0:T(8,128)(2,1)} %slice.18) | data formatting | bytes 26214400 | tf_op jit(solution)/shard_map/reshape | solution.py:111
  228.3 0.0 copy-done.1
  228.3 6.7 %fusion.19 = bf16[256,1280]{1,0:T(8,128)(2,1)S(1)} fusion(bf16[256,5120]{1,0:T(8,128)(2,1)S(1)} %copy-done.1, bf16[1280,5120]{1,0:T(8,128)(2,1)} %reshape.118, f32[1280]{0:T(1024)S(1)} %copy-done.10), kind=kOutput, calls=%fused_computation.28 | convolution fusion | flops 3356098560 | bytes 16389120 | tf_op jit(solution)/shard_map/dot_general | solution.py:27
  235.1 2.1 scatter_custom_fusion.1
  237.2 1.2 reshape.119
  238.4 0.0 all-to-all-done
  238.4 7.3 %all-to-all-start.1 = ((bf16[128,4,1280]{2,1,0:T(4,128)(2,1)}), bf16[128,4,1280]{2,1,0:T(4,128)(2,1)S(1)}, u32[]{:S(2)}, u32[]{:S(2)}) async-start(bf16[128,4,1280]{2,1,0:T(4,128)(2,1)} %reshape.119), calls=%async_computation.1 | async-start | bytes 2621440 | tf_op jit(solution)/shard_map/all_to_all | solution.py:148
  245.7 0.5 broadcast.111
  246.2 0.8 reduce.3
  247.0 0.1 reshape.111
  247.2 19.9 %all-to-all-done.1 = bf16[128,4,1280]{2,1,0:T(4,128)(2,1)S(1)} async-done(((bf16[128,4,1280]{2,1,0:T(4,128)(2,1)}), bf16[128,4,1280]{2,1,0:T(4,128)(2,1)S(1)}, u32[]{:S(2)}, u32[]{:S(2)}) %all-to-all-start.1) | async-done | bytes 1310752 | tf_op jit(solution)/shard_map/all_to_all | solution.py:148
  267.1 0.3 reshape.141
  267.4 3.5 %scatter_custom_fusion.2 = bf16[256,1280]{1,0:T(8,128)(2,1)} fusion(s32[512]{0:T(512)S(1)} %bitcast.33, bf16[512,1280]{1,0:T(8,128)(2,1)S(1)} %reshape.141, bf16[]{:T(256)} %constant.8.clone.1), kind=kCustom, calls=%fused_computation.31 | custom fusion | bytes 655362 | tf_op jit(solution)/shard_map/scatter | solution.py:166
  (27 shorter events, 0.1 us)
Async XLA Ops:
  6.5 79.3 %all-gather.6.cloned.1.call-start = ((), (), s32[]{:S(2)}) async-start(), calls=%async_computation.3 | async-start | bytes 10567680 | tf_op jit(solution)/shard_map/all_gather | solution.py:99
  7.3 170.3 %all-gather.4.cloned.1.call-start = ((), (), s32[]{:S(2)}) async-start(), calls=%async_computation.2 | async-start | bytes 16644096 | tf_op jit(solution)/shard_map/all_gather | solution.py:107
  9.8 89.7 %copy-start.2 = (s32[256]{0:T(256)S(1)}, s32[256]{0:T(256)}, u32[]{:S(2)}) copy-start(s32[256]{0:T(256)} %param.26) | copy-start | bytes 3076
  9.8 98.6 %copy-start.5 = (s32[1024]{0:T(1024)S(1)}, s32[1024]{0:T(1024)}, u32[]{:S(2)}) copy-start(s32[1024]{0:T(1024)} %param.15) | copy-start | bytes 12292
  9.8 99.6 %copy-start = (bf16[1024,1280]{1,0:T(8,128)(2,1)S(1)}, bf16[1024,1280]{1,0:T(8,128)(2,1)}, u32[]{:S(2)}) copy-start(bf16[1024,1280]{1,0:T(8,128)(2,1)} %param.14) | copy-start | bytes 7864324
  99.5 11.2 %copy-start.6 = (f32[3840]{0:T(1024)S(1)}, f32[3840]{0:T(1024)}, u32[]{:S(2)}) copy-start(f32[3840]{0:T(1024)} %param.19) | copy-start | bytes 46084
  99.5 11.2 %copy-start.7 = (f32[1280]{0:T(1024)S(1)}, f32[1280]{0:T(1024)}, u32[]{:S(2)}) copy-start(f32[1280]{0:T(1024)} %param.17) | copy-start | bytes 15364
  99.5 11.3 %copy-start.8 = (f32[1280]{0:T(1024)S(1)}, f32[1280]{0:T(1024)}, u32[]{:S(2)}) copy-start(f32[1280]{0:T(1024)} %param.16) | copy-start | bytes 15364
  102.4 136.1 %all-to-all-start = ((s32[128,1,4]{2,1,0:T(1,128)}), s32[128,1,4]{2,1,0:T(1,128)S(1)}, u32[]{:S(2)}, u32[]{:S(2)}) async-start(s32[128,1,4]{2,1,0:T(1,128)} %bitcast.4), calls=%async_computation | async-start | bytes 131072 | tf_op jit(solution)/shard_map/all_to_all | solution.py:155
  173.5 10.6 %copy-start.9 = (f32[1280]{0:T(1024)S(1)}, f32[1280]{0:T(1024)}, u32[]{:S(2)}) copy-start(f32[1280]{0:T(1024)} %param.21) | copy-start | bytes 15364
  177.5 2.0 slice-start
  184.1 8.2 %copy-start.3 = (f32[1280]{0:T(1024)S(1)}, f32[1280]{0:T(1024)}, u32[]{:S(2)}) copy-start(f32[1280]{0:T(1024)} %param.23) | copy-start | bytes 15364
  184.1 8.2 %copy-start.4 = (f32[1280]{0:T(1024)S(1)}, f32[1280]{0:T(1024)}, u32[]{:S(2)}) copy-start(f32[1280]{0:T(1024)} %param.22) | copy-start | bytes 15364
  208.7 19.7 %copy-start.1 = (bf16[256,5120]{1,0:T(8,128)(2,1)S(1)}, bf16[256,5120]{1,0:T(8,128)(2,1)}, u32[]{:S(2)}) copy-start(bf16[256,5120]{1,0:T(8,128)(2,1)} %reshape.117) | copy-start | bytes 7864324
  208.7 19.7 %copy-start.10 = (f32[1280]{0:T(1024)S(1)}, f32[1280]{0:T(1024)}, u32[]{:S(2)}) copy-start(f32[1280]{0:T(1024)} %param.25) | copy-start | bytes 15364
  238.4 28.6 %all-to-all-start.1 = ((bf16[128,4,1280]{2,1,0:T(4,128)(2,1)}), bf16[128,4,1280]{2,1,0:T(4,128)(2,1)S(1)}, u32[]{:S(2)}, u32[]{:S(2)}) async-start(bf16[128,4,1280]{2,1,0:T(4,128)(2,1)} %reshape.119), calls=%async_computation.1 | async-start | bytes 2621440 | tf_op jit(solution)/shard_map/all_to_all | solution.py:148
Sparse Core Ops, SparseCore 0:
  10.5 75.2 all-gather.5
  99.6 77.8 all-gather.3

commit v2 on v1

--- a/solution.py
+++ b/solution.py
@@ -96,19 +96,34 @@
     width = D
     axes = ("fsdp", "dp")
 
-    qkv_full = lax.all_gather(qkv_weight, axes, axis=0, tiled=True)
+    qkv_full = lax.all_gather(qkv_weight, axes, axis=0, tiled=False)
     out_rows = out_weight.shape[0]
     merge_rows = merge_weight.shape[0]
-    lanes = 128
-    flat = jnp.concatenate(
-        [out_weight.reshape(-1, lanes), merge_weight.reshape(-1, lanes)], axis=0
-    )[None]
-    qkv_full, flat = lax.optimization_barrier((qkv_full, flat))
-    rest = lax.all_gather(flat, axes, axis=0, tiled=True)
-    devices = rest.shape[0]
-    out_cut = out_rows * width // lanes
-    out_full = rest[:, :out_cut].reshape(devices * out_rows, width)
-    merge_full = rest[:, out_cut:].reshape(devices * merge_rows, 4 * width)
+    tile_rows = 16
+    wide = 4 * width
+    out_pad_rows = -(-out_rows * width // wide) * (wide // width)
+    out_packed = jnp.concatenate(
+        [out_weight, jnp.zeros((out_pad_rows - out_rows, width), out_weight.dtype)], axis=0
+    ).reshape(-1, wide)
+    packed_rows = out_packed.shape[0]
+    second = jnp.concatenate(
+        [
+            merge_weight,
+            out_packed,
+            jnp.zeros((tile_rows - merge_rows - packed_rows, wide), merge_weight.dtype),
+        ],
+        axis=0,
+    )
+    qkv_full, second = lax.optimization_barrier((qkv_full, second))
+    second_parts = lax.all_gather(second, axes, axis=0, tiled=False)
+    devices = second_parts.shape[0]
+    qkv_full = qkv_full.reshape(devices * qkv_weight.shape[0], width)
+    out_full = (
+        second_parts[:, merge_rows : merge_rows + packed_rows]
+        .reshape(devices, out_pad_rows, width)[:, :out_rows]
+        .reshape(devices * out_rows, width)
+    )
+    merge_full = second_parts.reshape(devices * tile_rows, wide)
 
     normed = layer_norm(patch_states, first_gain, first_shift).astype(jnp.bfloat16)
     joined_t = lax.dot_general(
@@ -129,7 +144,9 @@
         .astype(jnp.bfloat16)
         .reshape(tokens // 4, 4 * width)
     )
-    projected = (times_rows(merged, merge_full) + merge_bias).astype(jnp.bfloat16)
+    projected_padded = lax.optimization_barrier(times_rows(merged, merge_full))
+    projected = projected_padded.reshape(tokens // 4, devices, tile_rows)[:, :, :merge_rows]
+    projected = (projected.reshape(tokens // 4, width) + merge_bias).astype(jnp.bfloat16)
 
     fsdp_count = lax.axis_size("fsdp")
     dp_count = lax.axis_size("dp")

time: 279 us -> 285 us (1.022)
  waiting for transfers between devices: 101 us -> 96.5 us
  other arithmetic: 5.04 us -> 9.36 us
  matrix products: 31.4 us -> 35.7 us
    slice x3 -> x4, local copies, waits for them, and re-layouts: 14.3 us -> 27.6 us  [per_device(): second_parts[:, merge_rows:merge_rows + packed_rows]]
    optimization_barrier x1, local copies, waits for them, and re-layouts: 13.6 us -> 1.93 us  [per_device(): projected_padded = lax.optimization_barrier(times_rows(merged, merge_full))]
    reshape x4, local copies, waits for them, and re-layouts: 26.1 us -> 21 us  [the longest x1 13.6 us: per_device(): qkv_full = qkv_full.reshape(devices * qkv_weight.shape[0], width)]
    dot_general x1, matrix products: 6.72 us -> 11.6 us  [times_rows(): lax.dot_general(left, piece, (((1,), (1,)), ((), ())), preferred_element_...]
    all_gather x2, waiting for transfers between devices: 80 us -> 75.9 us  [the longest x1 75.9 us: per_device(): qkv_full = lax.all_gather(qkv_weight, axes, axis=0, tiled=False)]
  transfers between devices with their start and end apart: 4 -> 4, of which waited for: 3 -> 2; matrix products, arithmetic and copies ran while one was open for 30% -> 38% of each run, Pallas kernels for 16% -> 16%
where the time goes in v2:
time: 285 us; the launch traced here: 284 us
  waiting for transfers between devices  96.5 us (34%)
  local copies, waits for them, and re-layouts  67.6 us (24%)
  Pallas kernels  45.4 us (16%)
  matrix products  35.7 us (13%)
  starting transfers between devices  15.8 us (6%)
  between operations  13.6 us (5%)
  other arithmetic  9.36 us (3%)
    all_gather x1, waiting for transfers between devices, per_device(): qkv_full = lax.all_gather(qkv_weight, axes, axis=0, tiled=False)  75.9 us
    pallas_call x1, Pallas kernels, attention(): pl.pallas_call(functools.partial(attention_kernel, scale), out_shape=jax....  45.4 us
    slice x4, local copies, waits for them, and re-layouts, per_device(): second_parts[:, merge_rows:merge_rows + packed_rows]  27.6 us
    all_to_all x1, waiting for transfers between devices, per_device(): lax.all_to_all(rows_out.reshape(count_dev, capacity, width), axes, split_...  19.9 us
    dot_general x1, matrix products, per_device(): lax.dot_general(qkv_full, normed, (((1,), (1,)), ((), ())), preferred_ele...  17.5 us
    reshape x1, local copies, waits for them, and re-layouts, per_device(): qkv_full = qkv_full.reshape(devices * qkv_weight.shape[0], width)  13.6 us
    dot_general x1, matrix products, times_rows(): lax.dot_general(left, piece, (((1,), (1,)), ((), ())), preferred_element_...  11.6 us
    all_to_all x1, starting transfers between devices, per_device(): lax.all_to_all(rows_out.reshape(count_dev, capacity, width), axes, split_...  9.71 us
  transfers between devices with their start and end apart: 4, of which 2 were waited for; matrix products, arithmetic and copies ran while one was open for 38% of the time, Pallas kernels for 16%

profile of v2, /device:TPU:1, one launch (start us, length us, event | category | flops | bytes accessed | tf_op | source)
XLA Modules:
  0.0 283.9 jit_solution(9228214560262916033)
XLA Ops:
  6.5 0.7 all-gather.8.cloned.1.call-update
  7.3 0.0 all-gather.6.cloned.1.call-start
  7.3 0.8 concatenate.6
  8.2 0.1 pad.3.clone
  8.2 1.7 maximum_maximum_fusion
  9.9 75.9 %all-gather.8.cloned.1.call-done = bf16[128,30,1280]{2,1,0:T(8,128)(2,1)} async-done(((bf16[1,30,1280]{2,1,0:T(8,128)(2,1)}), bf16[128,30,1280]{2,1,0:T(8,128)(2,1)}) %all-gather.8.cloned.1.call-update) | async-done | bytes 9830416 | tf_op jit(solution)/shard_map/all_gather | solution.py:99
  85.8 0.0 all-gather.6.cloned.1.call-update
  85.8 0.8 copy.27
  86.6 0.2 fusion.23
  86.9 0.9 fusion.25
  87.7 0.7 compare_select_fusion.1
  88.4 1.6 scatter_custom_fusion
  90.0 0.7 all_to_all.9
  90.7 6.0 %all-to-all-start = ((s32[128,1,4]{2,1,0:T(1,128)}), s32[128,1,4]{2,1,0:T(1,128)S(1)}, u32[]{:S(2)}, u32[]{:S(2)}) async-start(s32[128,1,4]{2,1,0:T(1,128)} %bitcast.4), calls=%async_computation | async-start | bytes 131072 | tf_op jit(solution)/shard_map/all_to_all | solution.py:172
  96.7 1.7 copy.30.qid_ref
  98.4 2.1 convert_reduce_fusion
  100.6 0.8 fusion.4
  101.5 0.0 copy-start.5
  101.5 0.0 copy-start.6
  101.5 0.0 copy-start.7
  101.5 13.6 %reshape.122 = bf16[3840,1280]{1,0:T(8,128)(2,1)} reshape(bf16[128,30,1280]{2,1,0:T(8,128)(2,1)} %all-gather.8.cloned.1.call-done) | data formatting | bytes 19660800 | tf_op jit(solution)/shard_map/reshape | solution.py:120
  115.1 17.5 %add_convert_fusion.q_ref.k_ref.v_ref = bf16[3840,1024]{1,0:T(8,128)(2,1)} fusion(bf16[3840,1280]{1,0:T(8,128)(2,1)} %reshape.122, f32[3840]{0:T(1024)S(1)} %copy-done.5, bf16[1024,1280]{1,0:T(8,128)(2,1)S(1)} %copy-done, f32[1280]{0:T(1024)S(1)} %copy-done.6, f32[1280]{0:T(1024)S(1)} %copy-done.7, f32[1024]{0:T(1024)S(1)} %add_rsqrt_fusion.1, ...), kind=kOutput, calls=%fused_computation.3 | convolution fusion | flops 10082058240 | bytes 20349952 | tf_op jit(solution)/shard_map/dot_general | solution.py:129
  132.7 45.4 %shard_map.136 = bf16[1280,1024]{1,0:T(8,128)(2,1)} custom-call(bf16[3840,1024]{1,0:T(8,128)(2,1)} %add_convert_fusion.q_ref.k_ref.v_ref, bf16[3840,1024]{1,0:T(8,128)(2,1)} %add_convert_fusion.q_ref.k_ref.v_ref, bf16[3840,1024]{1,0:T(8,128)(2,1)} %add_convert_fusion.q_ref.k_ref.v_ref, s32[1024,1]{1,0:T(8,128)} %copy.30.qid_ref, s32[1,1024]{1,0:T(1,128)} %bitcast.39), custom_call_target="tpu_custom_call" | custom-call | flops 5368709120 | bytes 10485760 | tf_op jit(solution)/shard_map/pallas_call | solution.py:63
  178.0 9.0 %slice.21 = bf16[128,3,5120]{2,1,0:T(4,128)(2,1)} slice(bf16[128,16,5120]{2,1,0:T(8,128)(2,1)} %bitcast.32), slice={[0:128], [10:13], [0:5120]} | slice | bytes 7864320 | tf_op jit(solution)/shard_map/slice | solution.py:122
  187.1 9.0 %copy.31 = bf16[128,3,5120]{0,2,1:T(8,128)(2,1)} copy(bf16[128,3,5120]{2,1,0:T(4,128)(2,1)} %slice.21) | data formatting | bytes 7864320 | tf_op jit(solution)/shard_map/slice | solution.py:122
  196.0 2.2 slice.22
  198.2 7.4 %copy.32 = bf16[128,10,1280]{2,1,0:T(8,128)(2,1)} copy(bf16[128,10,1280]{0,2,1:T(8,128)(2,1)S(1)} %slice.22) | data formatting | bytes 6553600 | tf_op jit(solution)/shard_map/slice | solution.py:122
  205.7 7.2 %reshape.126 = bf16[1280,1280]{1,0:T(8,128)(2,1)} reshape(bf16[128,10,1280]{2,1,0:T(8,128)(2,1)} %copy.32) | data formatting | bytes 6553600 | tf_op jit(solution)/shard_map/reshape | solution.py:124
  212.8 0.0 copy-start.3
  212.9 6.5 %convert_reduce_fusion.1 = (f32[1024]{0:T(1024)S(1)}, bf16[1024,1280]{1,0:T(8,128)(2,1)S(1)}) fusion(f32[1280]{0:T(1024)S(1)} %copy-done.8, bf16[1280,1024]{1,0:T(8,128)(2,1)} %shard_map.136, bf16[1280,1280]{1,0:T(8,128)(2,1)} %reshape.126, bf16[1024,1280]{1,0:T(8,128)(2,1)S(1)} %copy-done.1), kind=kOutput, calls=%fused_computation.8 | convolution fusion | flops 3363306496 | bytes 11150336 | tf_op jit(solution)/shard_map/dot_general | solution.py:136
  219.4 0.8 fusion.8
  220.3 1.0 fusion.11
  221.3 2.9 %reshape.127 = bf16[256,5120]{1,0:T(8,128)(2,1)} reshape(bf16[1024,1280]{1,0:T(8,128)(2,1)S(1)} %fusion.11) | data formatting | bytes 5242880 | tf_op jit(solution)/shard_map/reshape | solution.py:145
  224.2 11.6 %fusion.30 = f32[256,2048]{1,0:T(8,128)} fusion(bf16[256,5120]{1,0:T(8,128)(2,1)} %reshape.127, bf16[2048,5120]{1,0:T(8,128)(2,1)} %all-gather.6.cloned.1.call-done), kind=kOutput, calls=%fused_computation.51 | convolution fusion | flops 5368709120 | bytes 25690112 | tf_op jit(solution)/shard_map/dot_general | solution.py:27
  235.9 1.9 copy.33
  237.8 0.2 reshape.130
  238.0 0.2 add_convert_fusion.1
  238.3 0.2 copy.34
  238.5 2.4 scatter_custom_fusion.1
  240.9 1.2 reshape.131
  242.1 0.0 all-to-all-done
  242.2 9.7 %all-to-all-start.1 = ((bf16[128,4,1280]{2,1,0:T(4,128)(2,1)}), bf16[128,4,1280]{2,1,0:T(4,128)(2,1)S(1)}, u32[]{:S(2)}, u32[]{:S(2)}) async-start(bf16[128,4,1280]{2,1,0:T(4,128)(2,1)} %reshape.131), calls=%async_computation.1 | async-start | bytes 2621440 | tf_op jit(solution)/shard_map/all_to_all | solution.py:165
  251.9 0.5 broadcast.115
  252.4 0.8 reduce.3
  253.2 0.1 reshape.120
  253.3 19.9 %all-to-all-done.1 = bf16[128,4,1280]{2,1,0:T(4,128)(2,1)S(1)} async-done(((bf16[128,4,1280]{2,1,0:T(4,128)(2,1)}), bf16[128,4,1280]{2,1,0:T(4,128)(2,1)S(1)}, u32[]{:S(2)}, u32[]{:S(2)}) %all-to-all-start.1) | async-done | bytes 1310752 | tf_op jit(solution)/shard_map/all_to_all | solution.py:165
  273.2 0.3 reshape.153
  273.6 3.5 %scatter_custom_fusion.2 = bf16[256,1280]{1,0:T(8,128)(2,1)} fusion(s32[512]{0:T(512)S(1)} %bitcast.40, bf16[512,1280]{1,0:T(8,128)(2,1)S(1)} %reshape.153, bf16[]{:T(256)} %constant.8.clone.1), kind=kCustom, calls=%fused_computation.30 | custom fusion | bytes 655362 | tf_op jit(solution)/shard_map/scatter | solution.py:183
  (29 shorter events, 0.2 us)
Async XLA Ops:
  6.5 94.1 %copy-start = (bf16[1024,1280]{1,0:T(8,128)(2,1)S(1)}, bf16[1024,1280]{1,0:T(8,128)(2,1)}, u32[]{:S(2)}) copy-start(bf16[1024,1280]{1,0:T(8,128)(2,1)} %param.14) | copy-start | bytes 7864324
  6.5 79.2 %all-gather.8.cloned.1.call-start = ((), (), s32[]{:S(2)}) async-start(), calls=%async_computation.3 | async-start | bytes 10567680 | tf_op jit(solution)/shard_map/all_gather | solution.py:99
  7.3 170.8 %all-gather.6.cloned.1.call-start = ((), (), s32[]{:S(2)}) async-start(), calls=%async_computation.2 | async-start | bytes 21135360 | tf_op jit(solution)/shard_map/all_gather | solution.py:118
  90.7 151.4 %all-to-all-start = ((s32[128,1,4]{2,1,0:T(1,128)}), s32[128,1,4]{2,1,0:T(1,128)S(1)}, u32[]{:S(2)}, u32[]{:S(2)}) async-start(s32[128,1,4]{2,1,0:T(1,128)} %bitcast.4), calls=%async_computation | async-start | bytes 131072 | tf_op jit(solution)/shard_map/all_to_all | solution.py:172
  101.5 13.7 %copy-start.5 = (f32[3840]{0:T(1024)S(1)}, f32[3840]{0:T(1024)}, u32[]{:S(2)}) copy-start(f32[3840]{0:T(1024)} %param.19) | copy-start | bytes 46084
  101.5 13.6 %copy-start.6 = (f32[1280]{0:T(1024)S(1)}, f32[1280]{0:T(1024)}, u32[]{:S(2)}) copy-start(f32[1280]{0:T(1024)} %param.17) | copy-start | bytes 15364
  101.5 13.6 %copy-start.7 = (f32[1280]{0:T(1024)S(1)}, f32[1280]{0:T(1024)}, u32[]{:S(2)}) copy-start(f32[1280]{0:T(1024)} %param.16) | copy-start | bytes 15364
  205.7 7.2 %copy-start.1 = (bf16[1024,1280]{1,0:T(8,128)(2,1)S(1)}, bf16[1024,1280]{1,0:T(8,128)(2,1)}, u32[]{:S(2)}) copy-start(bf16[1024,1280]{1,0:T(8,128)(2,1)} %param.14) | copy-start | bytes 7864324
  205.7 7.2 %copy-start.8 = (f32[1280]{0:T(1024)S(1)}, f32[1280]{0:T(1024)}, u32[]{:S(2)}) copy-start(f32[1280]{0:T(1024)} %param.21) | copy-start | bytes 15364
  212.8 7.4 %copy-start.2 = (f32[1280]{0:T(1024)S(1)}, f32[1280]{0:T(1024)}, u32[]{:S(2)}) copy-start(f32[1280]{0:T(1024)} %param.23) | copy-start | bytes 15364
  212.8 7.4 %copy-start.3 = (f32[1280]{0:T(1024)S(1)}, f32[1280]{0:T(1024)}, u32[]{:S(2)}) copy-start(f32[1280]{0:T(1024)} %param.22) | copy-start | bytes 15364
  235.9 2.1 copy-start.4
  242.2 31.1 %all-to-all-start.1 = ((bf16[128,4,1280]{2,1,0:T(4,128)(2,1)}), bf16[128,4,1280]{2,1,0:T(4,128)(2,1)S(1)}, u32[]{:S(2)}, u32[]{:S(2)}) async-start(bf16[128,4,1280]{2,1,0:T(4,128)(2,1)} %reshape.131), calls=%async_computation.1 | async-start | bytes 2621440 | tf_op jit(solution)/shard_map/all_to_all | solution.py:165
Sparse Core Ops, SparseCore 0:
  10.5 75.2 all-gather.7
  88.7 85.3 all-gather.5

commit v3 on v2

--- a/solution.py
+++ b/solution.py
@@ -101,29 +101,16 @@
     merge_rows = merge_weight.shape[0]
     tile_rows = 16
     wide = 4 * width
-    out_pad_rows = -(-out_rows * width // wide) * (wide // width)
-    out_packed = jnp.concatenate(
-        [out_weight, jnp.zeros((out_pad_rows - out_rows, width), out_weight.dtype)], axis=0
-    ).reshape(-1, wide)
-    packed_rows = out_packed.shape[0]
+    second = jnp.concatenate([merge_weight, out_weight], axis=1)
     second = jnp.concatenate(
-        [
-            merge_weight,
-            out_packed,
-            jnp.zeros((tile_rows - merge_rows - packed_rows, wide), merge_weight.dtype),
-        ],
-        axis=0,
+        [second, jnp.zeros((tile_rows - merge_rows, wide + width), second.dtype)], axis=0
     )
     qkv_full, second = lax.optimization_barrier((qkv_full, second))
     second_parts = lax.all_gather(second, axes, axis=0, tiled=False)
     devices = second_parts.shape[0]
     qkv_full = qkv_full.reshape(devices * qkv_weight.shape[0], width)
-    out_full = (
-        second_parts[:, merge_rows : merge_rows + packed_rows]
-        .reshape(devices, out_pad_rows, width)[:, :out_rows]
-        .reshape(devices * out_rows, width)
-    )
-    merge_full = second_parts.reshape(devices * tile_rows, wide)
+    second_full = second_parts.reshape(devices * tile_rows, wide + width)
+    out_padded = second_full[:, wide:]
 
     normed = layer_norm(patch_states, first_gain, first_shift).astype(jnp.bfloat16)
     joined_t = lax.dot_general(
@@ -133,18 +120,22 @@
 
     attended_t = attention(joined_t, segment_ids, 512)
 
-    projected_att = lax.dot_general(
-        attended_t, out_full, (((0,), (1,)), ((), ())), preferred_element_type=jnp.float32
-    )
-    hidden = (patch_states.astype(jnp.float32) + projected_att + out_bias).astype(
-        jnp.bfloat16
-    )
+    projected_att = lax.optimization_barrier(
+        lax.dot_general(
+            attended_t, out_padded, (((0,), (1,)), ((), ())), preferred_element_type=jnp.float32
+        )
+    )
+    projected_att = projected_att.reshape(tokens, devices, tile_rows)[:, :, :out_rows]
+    hidden = (
+        patch_states.astype(jnp.float32) + projected_att.reshape(tokens, width) + out_bias
+    ).astype(jnp.bfloat16)
     merged = (
         layer_norm(hidden, second_gain, second_shift)
         .astype(jnp.bfloat16)
         .reshape(tokens // 4, 4 * width)
     )
-    projected_padded = lax.optimization_barrier(times_rows(merged, merge_full))
+    merged_wide = jnp.concatenate([merged, jnp.zeros((tokens // 4, width), merged.dtype)], axis=1)
+    projected_padded = lax.optimization_barrier(times_rows(merged_wide, second_full))
     projected = projected_padded.reshape(tokens // 4, devices, tile_rows)[:, :, :merge_rows]
     projected = (projected.reshape(tokens // 4, width) + merge_bias).astype(jnp.bfloat16)
 
@@ -159,28 +150,29 @@
     earlier = jnp.cumsum(matches, axis=0) - matches
     rank = jnp.sum(earlier * matches, axis=1)
     position = dest_device * capacity + rank
-    rows_out = jnp.zeros((count_dev * capacity, width), jnp.bfloat16).at[position].set(projected)
-    slots_out = jnp.full((count_dev * capacity,), row_count, jnp.int32).at[position].set(dest_slot)
-    got_rows, got_slots = (
-        lax.all_to_all(
-            rows_out.reshape(count_dev, capacity, width),
-            axes,
-            split_axis=0,
-            concat_axis=0,
-            tiled=True,
-        ),
-        lax.all_to_all(
-            slots_out.reshape(count_dev, capacity),
-            axes,
-            split_axis=0,
-            concat_axis=0,
-            tiled=True,
-        ),
-    )
-    requests = (
-        jnp.zeros((row_count, width), jnp.bfloat16)
-        .at[got_slots.reshape(-1)]
-        .set(got_rows.reshape(-1, width), mode="drop")
+    lanes = 128
+    slot_block = jnp.broadcast_to(dest_slot.astype(jnp.bfloat16)[:, None], (row_count, lanes))
+    payload = jnp.concatenate([projected, slot_block], axis=1)
+    place = (
+        position[None, :] == jnp.arange(count_dev * capacity, dtype=jnp.int32)[:, None]
+    ).astype(jnp.bfloat16)
+    rows_out = jnp.dot(place, payload, preferred_element_type=jnp.float32)
+    empty = (jnp.sum(place, axis=1, keepdims=True) == 0)
+    slot_lane = jnp.where(empty, float(row_count), rows_out[:, width:])
+    rows_out = jnp.concatenate([rows_out[:, :width], slot_lane], axis=1).astype(jnp.bfloat16)
+    got = lax.all_to_all(
+        rows_out.reshape(count_dev, capacity, width + lanes),
+        axes,
+        split_axis=0,
+        concat_axis=0,
+        tiled=True,
+    ).reshape(count_dev * capacity, width + lanes)
+    got_slots = got[:, width].astype(jnp.int32)
+    pick = (
+        got_slots[None, :] == jnp.arange(row_count, dtype=jnp.int32)[:, None]
+    ).astype(jnp.bfloat16)
+    requests = jnp.dot(pick, got[:, :width], preferred_element_type=jnp.float32).astype(
+        jnp.bfloat16
     )
     return requests
 

time: 285 us -> 282 us (0.989)
  blocking collectives: 0 us -> 29.9 us
  local copies, waits for them, and re-layouts: 67.6 us -> 45.8 us
  starting transfers between devices: 15.8 us -> 0.04 us
  matrix products: 35.7 us -> 42.2 us
  waiting for transfers between devices: 96.5 us -> 92.8 us
    all_to_all x0 -> x1, blocking collectives: none -> 29.9 us  [per_device(): lax.all_to_all(rows_out.reshape(count_dev, capacity, width + lanes), axes...]
    slice x4 -> x1, local copies, waits for them, and re-layouts: 27.6 us -> 0.09 us  [per_device(): rows_out[:, :width]]
    all_to_all x2 -> x0, waiting for transfers between devices: 19.9 us -> none  [the longest x1 19.9 us: per_device(): lax.all_to_all(rows_out.reshape(count_dev, capacity, width), axes, split_...]
    all_to_all x2 -> x0, starting transfers between devices: 15.7 us -> none  [the longest x1 9.71 us: per_device(): lax.all_to_all(rows_out.reshape(count_dev, capacity, width), axes, split_...]
    all_gather x1, waiting for transfers between devices: 0.01 us -> 15.2 us  [per_device(): second_parts = lax.all_gather(second, axes, axis=0, tiled=False)]
    optimization_barrier x1 -> x2, local copies, waits for them, and re-layouts: 1.93 us -> 11.2 us  [the longest x1 9.29 us: per_device(): lax.optimization_barrier(lax.dot_general(attended_t, out_padded, (((0,),...]
    scatter x3 -> x0, local copies, waits for them, and re-layouts: 7.48 us -> none  [the longest x1 3.53 us: per_device(): requests = jnp.zeros((row_count, width), jnp.bfloat16).at[got_slots.resha...]
    dot_general x1 -> x3, matrix products: 6.54 us -> 12.7 us  [the longest x1 10.7 us: per_device(): lax.dot_general(attended_t, out_padded, (((0,), (1,)), ((), ())), preferr...]
  transfers between devices with their start and end apart: 4 -> 2, of which waited for: 2 -> 2; matrix products, arithmetic and copies ran while one was open for 38% -> 13% of each run, Pallas kernels for 16% -> 16%
where the time goes in v3:
time: 282 us; the launch traced here: 281 us
  waiting for transfers between devices  92.8 us (33%)
  local copies, waits for them, and re-layouts  45.8 us (16%)
  Pallas kernels  45.4 us (16%)
  matrix products  42.2 us (15%)
  blocking collectives  29.9 us (11%)
  between operations  13.6 us (5%)
  other arithmetic  10.9 us (4%)
    all_gather x1, waiting for transfers between devices, per_device(): qkv_full = lax.all_gather(qkv_weight, axes, axis=0, tiled=False)  76.8 us
    pallas_call x1, Pallas kernels, attention(): pl.pallas_call(functools.partial(attention_kernel, scale), out_shape=jax....  45.4 us
    all_to_all x1, blocking collectives, per_device(): lax.all_to_all(rows_out.reshape(count_dev, capacity, width + lanes), axes...  29.9 us
    dot_general x1, matrix products, per_device(): lax.dot_general(qkv_full, normed, (((1,), (1,)), ((), ())), preferred_ele...  16 us
    all_gather x1, waiting for transfers between devices, per_device(): second_parts = lax.all_gather(second, axes, axis=0, tiled=False)  15.2 us
    reshape x1, local copies, waits for them, and re-layouts, per_device(): qkv_full = qkv_full.reshape(devices * qkv_weight.shape[0], width)  13.6 us
    dot_general x1, matrix products, times_rows(): lax.dot_general(left, piece, (((1,), (1,)), ((), ())), preferred_element_...  13.5 us
    dot_general x1, matrix products, per_device(): lax.dot_general(attended_t, out_padded, (((0,), (1,)), ((), ())), preferr...  10.7 us
  transfers between devices with their start and end apart: 2, of which 2 were waited for; matrix products, arithmetic and copies ran while one was open for 13% of the time, Pallas kernels for 16%

profile of v3, /device:TPU:1, one launch (start us, length us, event | category | flops | bytes accessed | tf_op | source)
XLA Modules:
  0.0 280.7 jit_solution(11085902912992045280)
XLA Ops:
  6.5 0.0 all-gather.8.cloned.1.call-start
  6.5 0.7 all-gather.8.cloned.1.call-update
  7.3 0.0 all-gather.6.cloned.1.call-start
  7.3 1.7 fusion.35
  9.0 76.8 %all-gather.8.cloned.1.call-done = bf16[128,30,1280]{2,1,0:T(8,128)(2,1)} async-done(((bf16[1,30,1280]{2,1,0:T(8,128)(2,1)}), bf16[128,30,1280]{2,1,0:T(8,128)(2,1)}) %all-gather.8.cloned.1.call-update) | async-done | bytes 9830416 | tf_op jit(solution)/shard_map/all_gather | solution.py:99
  85.8 0.0 all-gather.6.cloned.1.call-update
  85.8 0.0 copy-start.10
  85.8 3.0 %copy.38 = bf16[1024,1280]{0,1:T(8,128)(2,1)S(1)} copy(bf16[1024,1280]{1,0:T(8,128)(2,1)} %param.14) | data formatting | bytes 5242880 | tf_op args[0]
  88.8 0.0 copy-done.6
  88.8 1.0 copy.39.qid_ref
  89.9 0.0 copy-done.1
  89.9 0.1 copy.36
  90.0 0.2 fusion.36
  90.3 0.2 fusion.38
  90.5 0.2 fusion.31
  90.7 0.5 convert_reduce_fusion
  91.1 0.7 fusion.4
  91.9 0.0 copy-start.7
  91.9 0.0 copy-start.8
  91.9 0.0 copy-start.9
  91.9 13.6 %reshape.98 = bf16[3840,1280]{1,0:T(8,128)(2,1)} reshape(bf16[128,30,1280]{2,1,0:T(8,128)(2,1)} %all-gather.8.cloned.1.call-done) | data formatting | bytes 19660800 | tf_op jit(solution)/shard_map/reshape | solution.py:111
  105.6 0.0 copy-done.8
  105.6 16.0 %add_convert_fusion.q_ref.k_ref.v_ref = bf16[3840,1024]{1,0:T(8,128)(2,1)} fusion(bf16[3840,1280]{1,0:T(8,128)(2,1)} %reshape.98, f32[3840]{0:T(1024)S(1)} %copy-done.7, bf16[1024,1280]{0,1:T(8,128)(2,1)S(1)} %copy.38, f32[1280]{0:T(1024)S(1)} %copy-done.8, f32[1280]{0:T(1024)S(1)} %copy-done.9, f32[1024]{0:T(1024)S(1)} %add_rsqrt_fusion.1, ...), kind=kOutput, calls=%fused_computation | convolution fusion | flops 10082058240 | bytes 20349952 | tf_op jit(solution)/shard_map/dot_general | solution.py:116
  121.6 45.4 %shard_map.136 = bf16[1280,1024]{1,0:T(8,128)(2,1)} custom-call(bf16[3840,1024]{1,0:T(8,128)(2,1)} %add_convert_fusion.q_ref.k_ref.v_ref, bf16[3840,1024]{1,0:T(8,128)(2,1)} %add_convert_fusion.q_ref.k_ref.v_ref, bf16[3840,1024]{1,0:T(8,128)(2,1)} %add_convert_fusion.q_ref.k_ref.v_ref, s32[1024,1]{1,0:T(8,128)} %copy.39.qid_ref, s32[1,1024]{1,0:T(1,128)} %bitcast.37), custom_call_target="tpu_custom_call" | custom-call | flops 5368709120 | bytes 10485760 | tf_op jit(solution)/shard_map/pallas_call | solution.py:63
  166.9 15.2 %all-gather.6.cloned.1.call-done = bf16[2048,6400]{1,0:T(8,128)(2,1)} async-done(((bf16[16,6400]{1,0:T(8,128)(2,1)}), bf16[2048,6400]{1,0:T(8,128)(2,1)}) %all-gather.6.cloned.1.call-update) | async-done | bytes 26214416 | tf_op jit(solution)/shard_map/all_gather | solution.py:109
  182.2 10.7 %fusion.14 = f32[1024,2048]{1,0:T(8,128)} fusion(bf16[1280,1024]{1,0:T(8,128)(2,1)} %shard_map.136, bf16[2048,6400]{1,0:T(8,128)(2,1)} %all-gather.6.cloned.1.call-done), kind=kOutput, calls=%fused_computation.20 | convolution fusion | flops 5368709120 | bytes 16252928 | tf_op jit(solution)/shard_map/dot_general | solution.py:124
  192.9 9.3 %copy.40 = f32[1024,2048]{0,1:T(8,128)} copy(f32[1024,2048]{1,0:T(8,128)} %fusion.14) | data formatting | bytes 16777216 | tf_op jit(solution)/shard_map/optimization_barrier | solution.py:123
  202.2 8.0 %reshape.103 = f32[1024,1280]{0,1:T(8,128)} reshape(f32[1024,128,10]{0,2,1:T(8,128)} %bitcast.29) | data formatting | bytes 10485760 | tf_op jit(solution)/shard_map/reshape | solution.py:130
  210.2 3.3 %convert_reduce_fusion.1 = (f32[1024]{0:T(1024)S(1)}, bf16[1024,1280]{0,1:T(8,128)(2,1)S(1)}) fusion(f32[1280]{0:T(1024)S(1)} %copy-done.5, f32[1024,1280]{0,1:T(8,128)} %reshape.103, bf16[1024,1280]{0,1:T(8,128)(2,1)S(1)} %copy.38), kind=kLoop, calls=%fused_computation.5 | loop fusion | flops 7863296 | bytes 10494976 | tf_op jit(solution)/shard_map/reduce_sum | solution.py:21
  213.5 0.7 fusion.8
  214.2 0.0 copy-done.3
  214.2 1.3 fusion.11
  215.5 2.7 copy.41
  218.2 4.0 %reshape.104 = bf16[256,5120]{1,0:T(8,128)(2,1)S(1)} reshape(bf16[1024,1280]{1,0:T(8,128)(2,1)} %copy.41) | data formatting | bytes 5242880 | tf_op jit(solution)/shard_map/reshape | solution.py:135
  222.3 13.5 %fusion.16 = f32[256,2048]{1,0:T(8,128)} fusion(bf16[2048,6400]{1,0:T(8,128)(2,1)} %all-gather.6.cloned.1.call-done, bf16[256,5120]{1,0:T(8,128)(2,1)S(1)} %reshape.104), kind=kOutput, calls=%fused_computation.22 | convolution fusion | flops 6710886400 | bytes 30932992 | tf_op jit(solution)/shard_map/dot_general | solution.py:27
  235.8 1.9 copy.42
  237.7 0.2 reshape.106
  237.9 0.2 add_convert_fusion.1
  238.2 0.6 fusion.24
  238.8 1.1 copy-done
  239.9 0.1 slice.55
  240.0 0.3 concatenate.25
  240.4 1.0 fusion.32
  241.4 0.7 pad_maximum_fusion
  242.1 29.9 %all_to_all.5 = bf16[128,4,1408]{2,1,0:T(4,128)(2,1)S(1)} all-to-all(bf16[128,4,1408]{2,1,0:T(4,128)(2,1)S(1)} %pad_maximum_fusion), channel_id=1, replica_groups=mesh['fsdp'=8,'dp'=16] {'fsdp','dp'}, dimensions={0} | all-to-all | bytes 2883584 | tf_op jit(solution)/shard_map/all_to_all | solution.py:163
  272.0 0.3 reshape.107
  272.4 0.1 convert_reduce_fusion.2
  272.5 1.4 convolution_convert_fusion
  (27 shorter events, 0.2 us)
Async XLA Ops:
  6.5 82.3 %copy-start.6 = (s32[1024]{0:T(1024)S(1)}, s32[1024]{0:T(1024)}, u32[]{:S(2)}) copy-start(s32[1024]{0:T(1024)} %param.15) | copy-start | bytes 12292
  6.5 83.3 %copy-start.1 = (s32[256]{0:T(256)S(1)}, s32[256]{0:T(256)}, u32[]{:S(2)}) copy-start(s32[256]{0:T(256)} %param.26) | copy-start | bytes 3076
  6.5 79.2 %all-gather.8.cloned.1.call-start = ((), (), s32[]{:S(2)}) async-start(), calls=%async_computation.2 | async-start | bytes 10567680 | tf_op jit(solution)/shard_map/all_gather | solution.py:99
  7.3 174.9 %all-gather.6.cloned.1.call-start = ((), (), s32[]{:S(2)}) async-start(), calls=%async_computation.1 | async-start | bytes 26419200 | tf_op jit(solution)/shard_map/all_gather | solution.py:109
  85.8 4.5 %copy-start.10 = (s32[256]{0:T(256)S(1)}, s32[256]{0:T(256)}, u32[]{:S(2)}) copy-start(s32[256]{0:T(256)} %param.27) | copy-start | bytes 3076
  91.9 13.7 %copy-start.7 = (f32[3840]{0:T(1024)S(1)}, f32[3840]{0:T(1024)}, u32[]{:S(2)}) copy-start(f32[3840]{0:T(1024)} %param.19) | copy-start | bytes 46084
  91.9 13.7 %copy-start.8 = (f32[1280]{0:T(1024)S(1)}, f32[1280]{0:T(1024)}, u32[]{:S(2)}) copy-start(f32[1280]{0:T(1024)} %param.17) | copy-start | bytes 15364
  91.9 13.7 %copy-start.9 = (f32[1280]{0:T(1024)S(1)}, f32[1280]{0:T(1024)}, u32[]{:S(2)}) copy-start(f32[1280]{0:T(1024)} %param.16) | copy-start | bytes 15364
  202.2 8.0 %copy-start.5 = (f32[1280]{0:T(1024)S(1)}, f32[1280]{0:T(1024)}, u32[]{:S(2)}) copy-start(f32[1280]{0:T(1024)} %param.21) | copy-start | bytes 15364
  210.1 4.1 %copy-start.2 = (f32[1280]{0:T(1024)S(1)}, f32[1280]{0:T(1024)}, u32[]{:S(2)}) copy-start(f32[1280]{0:T(1024)} %param.23) | copy-start | bytes 15364
  210.1 4.1 %copy-start.3 = (f32[1280]{0:T(1024)S(1)}, f32[1280]{0:T(1024)}, u32[]{:S(2)}) copy-start(f32[1280]{0:T(1024)} %param.22) | copy-start | bytes 15364
  235.8 2.1 copy-start.4
  238.8 1.1 copy-start
Sparse Core Ops, SparseCore 0:
  10.5 75.2 all-gather.7
  88.9 93.2 all-gather.5

commit v4 on v3

--- a/solution.py
+++ b/solution.py
@@ -96,21 +96,20 @@
     width = D
     axes = ("fsdp", "dp")
 
-    qkv_full = lax.all_gather(qkv_weight, axes, axis=0, tiled=False)
+    qkv_parts = lax.all_gather(qkv_weight, axes, axis=0, tiled=False)
     out_rows = out_weight.shape[0]
     merge_rows = merge_weight.shape[0]
-    tile_rows = 16
-    wide = 4 * width
-    second = jnp.concatenate([merge_weight, out_weight], axis=1)
-    second = jnp.concatenate(
-        [second, jnp.zeros((tile_rows - merge_rows, wide + width), second.dtype)], axis=0
+    lanes = 128
+    flat = jnp.concatenate(
+        [out_weight.reshape(-1, lanes), merge_weight.reshape(-1, lanes)], axis=0
     )
-    qkv_full, second = lax.optimization_barrier((qkv_full, second))
-    second_parts = lax.all_gather(second, axes, axis=0, tiled=False)
-    devices = second_parts.shape[0]
-    qkv_full = qkv_full.reshape(devices * qkv_weight.shape[0], width)
-    second_full = second_parts.reshape(devices * tile_rows, wide + width)
-    out_padded = second_full[:, wide:]
+    qkv_parts, flat = lax.optimization_barrier((qkv_parts, flat))
+    rest = lax.all_gather(flat, axes, axis=0, tiled=False)
+    devices = rest.shape[0]
+    qkv_full = qkv_parts.reshape(devices * qkv_weight.shape[0], width)
+    out_cut = out_rows * width // lanes
+    out_full = rest[:, :out_cut].reshape(devices * out_rows, width)
+    merge_full = rest[:, out_cut:].reshape(devices * merge_rows, 4 * width)
 
     normed = layer_norm(patch_states, first_gain, first_shift).astype(jnp.bfloat16)
     joined_t = lax.dot_general(
@@ -120,24 +119,18 @@
 
     attended_t = attention(joined_t, segment_ids, 512)
 
-    projected_att = lax.optimization_barrier(
-        lax.dot_general(
-            attended_t, out_padded, (((0,), (1,)), ((), ())), preferred_element_type=jnp.float32
-        )
+    projected_att = lax.dot_general(
+        attended_t, out_full, (((0,), (1,)), ((), ())), preferred_element_type=jnp.float32
     )
-    projected_att = projected_att.reshape(tokens, devices, tile_rows)[:, :, :out_rows]
-    hidden = (
-        patch_states.astype(jnp.float32) + projected_att.reshape(tokens, width) + out_bias
-    ).astype(jnp.bfloat16)
+    hidden = (patch_states.astype(jnp.float32) + projected_att + out_bias).astype(
+        jnp.bfloat16
+    )
     merged = (
         layer_norm(hidden, second_gain, second_shift)
         .astype(jnp.bfloat16)
         .reshape(tokens // 4, 4 * width)
     )
-    merged_wide = jnp.concatenate([merged, jnp.zeros((tokens // 4, width), merged.dtype)], axis=1)
-    projected_padded = lax.optimization_barrier(times_rows(merged_wide, second_full))
-    projected = projected_padded.reshape(tokens // 4, devices, tile_rows)[:, :, :merge_rows]
-    projected = (projected.reshape(tokens // 4, width) + merge_bias).astype(jnp.bfloat16)
+    projected = (times_rows(merged, merge_full) + merge_bias).astype(jnp.bfloat16)
 
     fsdp_count = lax.axis_size("fsdp")
     dp_count = lax.axis_size("dp")

time: 282 us -> 268 us (0.950)
  waiting for transfers between devices: 92.8 us -> 76.6 us
  local copies, waits for them, and re-layouts: 45.8 us -> 60.5 us
  matrix products: 42.2 us -> 33.3 us
    reshape x3 -> x5, local copies, waits for them, and re-layouts: 21.8 us -> 39.8 us  [the longest x1 19.7 us: per_device(): merge_full = rest[:, out_cut:].reshape(devices * merge_rows, 4 * width)]
    all_gather x2, waiting for transfers between devices: 92 us -> 75.9 us  [the longest x1 75.9 us: per_device(): qkv_parts = lax.all_gather(qkv_weight, axes, axis=0, tiled=False)]
    slice x0 -> x3, local copies, waits for them, and re-layouts: none -> 14.3 us  [the longest x1 12.4 us: per_device(): merge_full = rest[:, out_cut:].reshape(devices * merge_rows, 4 * width)]
    optimization_barrier x2 -> x0, local copies, waits for them, and re-layouts: 11.2 us -> none  [the longest x1 9.29 us: per_device(): lax.optimization_barrier(lax.dot_general(attended_t, out_padded, (((0,),...]
    dot_general x1, matrix products: 13.5 us -> 6.72 us  [times_rows(): lax.dot_general(left, piece, (((1,), (1,)), ((), ())), preferred_element_...]
    unnamed x24 -> x19, local copies, waits for them, and re-layouts: 4.16 us -> 0.05 us
    dot_general x1, matrix products: 10.7 us -> 7.33 us  [per_device(): lax.dot_general(attended_t, out_full, (((0,), (1,)), ((), ())), preferred...]
  transfers between devices with their start and end apart: 2 -> 2, of which waited for: 2 -> 1; matrix products, arithmetic and copies ran while one was open for 13% -> 16% of each run, Pallas kernels for 16% -> 17%
where the time goes in v4:
time: 268 us; the launch traced here: 267 us
  waiting for transfers between devices  76.6 us (29%)
  local copies, waits for them, and re-layouts  60.5 us (23%)
  Pallas kernels  45.3 us (17%)
  matrix products  33.3 us (12%)
  blocking collectives  28.6 us (11%)
  between operations  13.6 us (5%)
  other arithmetic  9.12 us (3%)
    all_gather x1, waiting for transfers between devices, per_device(): qkv_parts = lax.all_gather(qkv_weight, axes, axis=0, tiled=False)  75.9 us
    pallas_call x1, Pallas kernels, attention(): pl.pallas_call(functools.partial(attention_kernel, scale), out_shape=jax....  45.3 us
    all_to_all x1, blocking collectives, per_device(): lax.all_to_all(rows_out.reshape(count_dev, capacity, width + lanes), axes...  28.6 us
    reshape x1, local copies, waits for them, and re-layouts, per_device(): merge_full = rest[:, out_cut:].reshape(devices * merge_rows, 4 * width)  19.7 us
    dot_general x1, matrix products, per_device(): lax.dot_general(qkv_full, normed, (((1,), (1,)), ((), ())), preferred_ele...  17.3 us
    reshape x1, local copies, waits for them, and re-layouts, per_device(): qkv_full = qkv_parts.reshape(devices * qkv_weight.shape[0], width)  13.6 us
    slice x1, local copies, waits for them, and re-layouts, per_device(): merge_full = rest[:, out_cut:].reshape(devices * merge_rows, 4 * width)  12.4 us
    dot_general x1, matrix products, per_device(): lax.dot_general(attended_t, out_full, (((0,), (1,)), ((), ())), preferred...  7.33 us
  transfers between devices with their start and end apart: 2, of which 1 were waited for; matrix products, arithmetic and copies ran while one was open for 16% of the time, Pallas kernels for 17%

profile of v4, /device:TPU:1, one launch (start us, length us, event | category | flops | bytes accessed | tf_op | source)
XLA Modules:
  0.0 267.1 jit_solution(5898816668463937660)
XLA Ops:
  6.5 0.0 all-gather.7.cloned.1.call-start
  6.5 0.7 all-gather.7.cloned.1.call-update
  7.3 0.0 all-gather.9.cloned.1.call-start
  7.3 1.0 reshape.96
  8.3 0.8 reshape.95
  9.2 0.7 pad_maximum_fusion.1
  9.9 75.9 %all-gather.7.cloned.1.call-done = bf16[128,30,1280]{2,1,0:T(8,128)(2,1)} async-done(((bf16[1,30,1280]{2,1,0:T(8,128)(2,1)}), bf16[128,30,1280]{2,1,0:T(8,128)(2,1)}) %all-gather.7.cloned.1.call-update) | async-done | bytes 9830416 | tf_op jit(solution)/shard_map/all_gather | solution.py:99
  85.8 0.0 all-gather.9.cloned.1.call-update
  85.8 1.7 copy.27.qid_ref
  87.5 0.8 copy.25
  88.3 0.2 fusion.30
  88.6 0.7 convert_element_type.67
  89.3 0.9 fusion.32
  90.1 0.7 multiply_add_fusion
  90.8 0.2 fusion.26
  91.0 2.2 convert_reduce_fusion
  93.2 0.0 copy-done
  93.2 0.8 fusion.4
  94.0 0.0 copy-start.4
  94.0 0.0 copy-start.5
  94.0 0.0 copy-start.6
  94.0 13.6 %reshape.97 = bf16[3840,1280]{1,0:T(8,128)(2,1)} reshape(bf16[128,30,1280]{2,1,0:T(8,128)(2,1)} %all-gather.7.cloned.1.call-done) | data formatting | bytes 19660800 | tf_op jit(solution)/shard_map/reshape | solution.py:109
  107.7 0.0 copy-done.4
  107.7 0.0 copy-done.6
  107.7 17.3 %add_convert_fusion.q_ref.k_ref.v_ref = bf16[3840,1024]{1,0:T(8,128)(2,1)} fusion(bf16[3840,1280]{1,0:T(8,128)(2,1)} %reshape.97, f32[3840]{0:T(1024)S(1)} %copy-done.4, bf16[1024,1280]{1,0:T(8,128)(2,1)S(1)} %copy-done, f32[1280]{0:T(1024)S(1)} %copy-done.5, f32[1280]{0:T(1024)S(1)} %copy-done.6, f32[1024]{0:T(1024)S(1)} %add_rsqrt_fusion.1, ...), kind=kOutput, calls=%fused_computation | convolution fusion | flops 10082058240 | bytes 20349952 | tf_op jit(solution)/shard_map/dot_general | solution.py:115
  125.0 45.3 %shard_map.136 = bf16[1280,1024]{1,0:T(8,128)(2,1)} custom-call(bf16[3840,1024]{1,0:T(8,128)(2,1)} %add_convert_fusion.q_ref.k_ref.v_ref, bf16[3840,1024]{1,0:T(8,128)(2,1)} %add_convert_fusion.q_ref.k_ref.v_ref, bf16[3840,1024]{1,0:T(8,128)(2,1)} %add_convert_fusion.q_ref.k_ref.v_ref, s32[1024,1]{1,0:T(8,128)} %copy.27.qid_ref, s32[1,1024]{1,0:T(1,128)} %bitcast.32), custom_call_target="tpu_custom_call" | custom-call | flops 5368709120 | bytes 10485760 | tf_op jit(solution)/shard_map/pallas_call | solution.py:63
  170.3 2.0 slice-done
  172.3 4.6 %reshape.100 = bf16[1280,1280]{1,0:T(8,128)(2,1)} reshape(bf16[128,100,128]{2,1,0:T(8,128)(2,1)S(1)} %slice-done) | data formatting | bytes 6553600 | tf_op jit(solution)/shard_map/reshape | solution.py:111
  176.9 0.0 copy-done.7
  176.9 7.3 %convert_reduce_fusion.1 = (f32[1024]{0:T(1024)S(1)}, bf16[1024,1280]{1,0:T(8,128)(2,1)S(1)}) fusion(f32[1280]{0:T(1024)S(1)} %copy-done.7, bf16[1280,1024]{1,0:T(8,128)(2,1)} %shard_map.136, bf16[1280,1280]{1,0:T(8,128)(2,1)} %reshape.100, bf16[1024,1280]{1,0:T(8,128)(2,1)} %param.14), kind=kOutput, calls=%fused_computation.5 | convolution fusion | flops 3363306496 | bytes 11150336 | tf_op jit(solution)/shard_map/dot_general | solution.py:122
  184.3 0.8 fusion.8
  185.1 0.0 copy-done.2
  185.1 0.0 copy-done.3
  185.1 1.0 fusion.11
  186.2 2.9 %reshape.101 = bf16[256,5120]{1,0:T(8,128)(2,1)} reshape(bf16[1024,1280]{1,0:T(8,128)(2,1)S(1)} %fusion.11) | data formatting | bytes 5242880 | tf_op jit(solution)/shard_map/reshape | solution.py:131
  189.1 12.4 %slice.35 = bf16[128,400,128]{2,1,0:T(8,128)(2,1)} slice(bf16[128,500,128]{2,1,0:T(8,128)(2,1)} %all-gather.9.cloned.1.call-done), slice={[0:128], [100:500], [0:128]} | slice | bytes 26214400 | tf_op jit(solution)/shard_map/slice | solution.py:112
  201.5 19.7 %reshape.102 = bf16[1280,5120]{1,0:T(8,128)(2,1)} reshape(bf16[128,400,128]{2,1,0:T(8,128)(2,1)} %slice.35) | data formatting | bytes 26214400 | tf_op jit(solution)/shard_map/reshape | solution.py:112
  221.1 6.7 %fusion.19 = bf16[256,1280]{1,0:T(8,128)(2,1)S(1)} fusion(bf16[256,5120]{1,0:T(8,128)(2,1)S(1)} %copy-done.1, bf16[1280,5120]{1,0:T(8,128)(2,1)} %reshape.102, f32[1280]{0:T(1024)S(1)} %copy-done.8), kind=kOutput, calls=%fused_computation.26 | convolution fusion | flops 3356098560 | bytes 16389120 | tf_op jit(solution)/shard_map/dot_general | solution.py:27
  227.9 0.1 broadcast_in_dim.10
  228.0 0.6 fusion.21
  228.6 0.1 slice.48
  228.7 0.1 fusion.27
  228.8 0.3 concatenate.17
  229.1 0.7 pad_maximum_fusion
  229.8 28.6 %all_to_all.5 = bf16[128,4,1408]{2,1,0:T(4,128)(2,1)S(1)} all-to-all(bf16[128,4,1408]{2,1,0:T(4,128)(2,1)S(1)} %pad_maximum_fusion), channel_id=1, replica_groups=mesh['fsdp'=8,'dp'=16] {'fsdp','dp'}, dimensions={0} | all-to-all | bytes 2883584 | tf_op jit(solution)/shard_map/all_to_all | solution.py:156
  258.4 0.3 reshape.103
  258.8 0.1 convert_reduce_fusion.2
  258.9 1.3 convolution_convert_fusion
  (22 shorter events, 0.1 us)
Async XLA Ops:
  6.5 86.6 %copy-start = (bf16[1024,1280]{1,0:T(8,128)(2,1)S(1)}, bf16[1024,1280]{1,0:T(8,128)(2,1)}, u32[]{:S(2)}) copy-start(bf16[1024,1280]{1,0:T(8,128)(2,1)} %param.14) | copy-start | bytes 7864324
  6.5 79.2 %all-gather.7.cloned.1.call-start = ((), (), s32[]{:S(2)}) async-start(), calls=%async_computation.1 | async-start | bytes 10567680 | tf_op jit(solution)/shard_map/all_gather | solution.py:99
  7.3 163.1 %all-gather.9.cloned.1.call-start = ((), (), s32[]{:S(2)}) async-start(), calls=%async_computation.2 | async-start | bytes 16644096 | tf_op jit(solution)/shard_map/all_gather | solution.py:107
  94.0 13.7 %copy-start.4 = (f32[3840]{0:T(1024)S(1)}, f32[3840]{0:T(1024)}, u32[]{:S(2)}) copy-start(f32[3840]{0:T(1024)} %param.19) | copy-start | bytes 46084
  94.0 13.7 %copy-start.5 = (f32[1280]{0:T(1024)S(1)}, f32[1280]{0:T(1024)}, u32[]{:S(2)}) copy-start(f32[1280]{0:T(1024)} %param.17) | copy-start | bytes 15364
  94.0 13.6 %copy-start.6 = (f32[1280]{0:T(1024)S(1)}, f32[1280]{0:T(1024)}, u32[]{:S(2)}) copy-start(f32[1280]{0:T(1024)} %param.16) | copy-start | bytes 15364
  170.3 2.0 slice-start
  172.3 4.6 %copy-start.7 = (f32[1280]{0:T(1024)S(1)}, f32[1280]{0:T(1024)}, u32[]{:S(2)}) copy-start(f32[1280]{0:T(1024)} %param.21) | copy-start | bytes 15364
  176.9 8.2 %copy-start.2 = (f32[1280]{0:T(1024)S(1)}, f32[1280]{0:T(1024)}, u32[]{:S(2)}) copy-start(f32[1280]{0:T(1024)} %param.23) | copy-start | bytes 15364
  176.9 8.2 %copy-start.3 = (f32[1280]{0:T(1024)S(1)}, f32[1280]{0:T(1024)}, u32[]{:S(2)}) copy-start(f32[1280]{0:T(1024)} %param.22) | copy-start | bytes 15364
  201.5 19.7 %copy-start.1 = (bf16[256,5120]{1,0:T(8,128)(2,1)S(1)}, bf16[256,5120]{1,0:T(8,128)(2,1)}, u32[]{:S(2)}) copy-start(bf16[256,5120]{1,0:T(8,128)(2,1)} %reshape.101) | copy-start | bytes 7864324
  201.5 19.7 %copy-start.8 = (f32[1280]{0:T(1024)S(1)}, f32[1280]{0:T(1024)}, u32[]{:S(2)}) copy-start(f32[1280]{0:T(1024)} %param.25) | copy-start | bytes 15364
Sparse Core Ops, SparseCore 0:
  10.5 75.2 all-gather.6
  88.7 77.6 all-gather.8

commit v5 on v4

--- a/solution.py
+++ b/solution.py
@@ -117,7 +117,7 @@
     )
     joined_t = (joined_t + qkv_bias[:, None]).astype(jnp.bfloat16)
 
-    attended_t = attention(joined_t, segment_ids, 512)
+    attended_t = attention(joined_t, segment_ids, 1024)
 
     projected_att = lax.dot_general(
         attended_t, out_full, (((0,), (1,)), ((), ())), preferred_element_type=jnp.float32

time: 268 us -> 266 us (level)
  Pallas kernels: 45.3 us -> 38.4 us
  waiting for transfers between devices: 76.6 us -> 79.7 us
    pallas_call x1, Pallas kernels: 45.3 us -> 38.4 us  [attention(): pl.pallas_call(functools.partial(attention_kernel, scale), out_shape=jax....]
    all_gather x1, waiting for transfers between devices: 0.01 us -> 3.1 us  [per_device(): rest = lax.all_gather(flat, axes, axis=0, tiled=False)]
  transfers between devices with their start and end apart: 2 -> 2, of which waited for: 1 -> 2; matrix products, arithmetic and copies ran while one was open for 16% -> 16% of each run, Pallas kernels for 17% -> 15%
where the time goes in v5:
time: 266 us; the launch traced here: 265 us
  waiting for transfers between devices  79.7 us (30%)
  local copies, waits for them, and re-layouts  60.5 us (23%)
  Pallas kernels  38.4 us (14%)
  matrix products  33.3 us (13%)
  blocking collectives  29.9 us (11%)
  between operations  13.6 us (5%)
  other arithmetic  9.12 us (3%)
    all_gather x1, waiting for transfers between devices, per_device(): qkv_parts = lax.all_gather(qkv_weight, axes, axis=0, tiled=False)  75.9 us
    pallas_call x1, Pallas kernels, attention(): pl.pallas_call(functools.partial(attention_kernel, scale), out_shape=jax....  38.4 us
    all_to_all x1, blocking collectives, per_device(): lax.all_to_all(rows_out.reshape(count_dev, capacity, width + lanes), axes...  29.9 us
    reshape x1, local copies, waits for them, and re-layouts, per_device(): merge_full = rest[:, out_cut:].reshape(devices * merge_rows, 4 * width)  19.7 us
    dot_general x1, matrix products, per_device(): lax.dot_general(qkv_full, normed, (((1,), (1,)), ((), ())), preferred_ele...  17.3 us
    reshape x1, local copies, waits for them, and re-layouts, per_device(): qkv_full = qkv_parts.reshape(devices * qkv_weight.shape[0], width)  13.6 us
    slice x1, local copies, waits for them, and re-layouts, per_device(): merge_full = rest[:, out_cut:].reshape(devices * merge_rows, 4 * width)  12.4 us
    dot_general x1, matrix products, per_device(): lax.dot_general(attended_t, out_full, (((0,), (1,)), ((), ())), preferred...  7.32 us
  transfers between devices with their start and end apart: 2, of which 2 were waited for; matrix products, arithmetic and copies ran while one was open for 16% of the time, Pallas kernels for 15%

profile of v5, /device:TPU:1, one launch (start us, length us, event | category | flops | bytes accessed | tf_op | source)
XLA Modules:
  0.0 264.6 jit_solution(7641833776280478940)
XLA Ops:
  6.5 0.0 all-gather.7.cloned.1.call-start
  6.5 0.7 all-gather.7.cloned.1.call-update
  7.3 0.0 all-gather.9.cloned.1.call-start
  7.3 1.0 reshape.96
  8.3 0.8 reshape.95
  9.2 0.7 pad_maximum_fusion.1
  9.9 75.9 %all-gather.7.cloned.1.call-done = bf16[128,30,1280]{2,1,0:T(8,128)(2,1)} async-done(((bf16[1,30,1280]{2,1,0:T(8,128)(2,1)}), bf16[128,30,1280]{2,1,0:T(8,128)(2,1)}) %all-gather.7.cloned.1.call-update) | async-done | bytes 9830416 | tf_op jit(solution)/shard_map/all_gather | solution.py:99
  85.8 0.0 all-gather.9.cloned.1.call-update
  85.8 1.7 copy.27.qid_ref
  87.5 0.8 copy.25
  88.3 0.2 fusion.30
  88.6 0.7 convert_element_type.67
  89.3 0.9 fusion.32
  90.1 0.7 multiply_add_fusion
  90.8 0.2 fusion.26
  91.0 2.2 convert_reduce_fusion
  93.2 0.0 copy-done
  93.2 0.8 fusion.4
  94.0 0.0 copy-start.4
  94.0 0.0 copy-start.5
  94.0 0.0 copy-start.6
  94.0 13.6 %reshape.97 = bf16[3840,1280]{1,0:T(8,128)(2,1)} reshape(bf16[128,30,1280]{2,1,0:T(8,128)(2,1)} %all-gather.7.cloned.1.call-done) | data formatting | bytes 19660800 | tf_op jit(solution)/shard_map/reshape | solution.py:109
  107.7 0.0 copy-done.4
  107.7 0.0 copy-done.5
  107.7 0.0 copy-done.6
  107.7 17.3 %add_convert_fusion.q_ref.k_ref.v_ref = bf16[3840,1024]{1,0:T(8,128)(2,1)} fusion(bf16[3840,1280]{1,0:T(8,128)(2,1)} %reshape.97, f32[3840]{0:T(1024)S(1)} %copy-done.4, bf16[1024,1280]{1,0:T(8,128)(2,1)S(1)} %copy-done, f32[1280]{0:T(1024)S(1)} %copy-done.5, f32[1280]{0:T(1024)S(1)} %copy-done.6, f32[1024]{0:T(1024)S(1)} %add_rsqrt_fusion.1, ...), kind=kOutput, calls=%fused_computation | convolution fusion | flops 10082058240 | bytes 20349952 | tf_op jit(solution)/shard_map/dot_general | solution.py:115
  125.0 38.4 %shard_map.136 = bf16[1280,1024]{1,0:T(8,128)(2,1)} custom-call(bf16[3840,1024]{1,0:T(8,128)(2,1)} %add_convert_fusion.q_ref.k_ref.v_ref, bf16[3840,1024]{1,0:T(8,128)(2,1)} %add_convert_fusion.q_ref.k_ref.v_ref, bf16[3840,1024]{1,0:T(8,128)(2,1)} %add_convert_fusion.q_ref.k_ref.v_ref, s32[1024,1]{1,0:T(8,128)} %copy.27.qid_ref, s32[1,1024]{1,0:T(1,128)} %bitcast.32), custom_call_target="tpu_custom_call" | custom-call | flops 5368709120 | bytes 10485760 | tf_op jit(solution)/shard_map/pallas_call | solution.py:63
  163.4 3.1 %all-gather.9.cloned.1.call-done = bf16[128,500,128]{2,1,0:T(8,128)(2,1)} async-done(((bf16[1,500,128]{2,1,0:T(8,128)(2,1)}), bf16[128,500,128]{2,1,0:T(8,128)(2,1)}) %all-gather.9.cloned.1.call-update) | async-done | bytes 16384016 | tf_op jit(solution)/shard_map/all_gather | solution.py:107
  166.5 2.0 slice-done
  168.5 4.6 %reshape.100 = bf16[1280,1280]{1,0:T(8,128)(2,1)} reshape(bf16[128,100,128]{2,1,0:T(8,128)(2,1)S(1)} %slice-done) | data formatting | bytes 6553600 | tf_op jit(solution)/shard_map/reshape | solution.py:111
  173.1 7.3 %convert_reduce_fusion.1 = (f32[1024]{0:T(1024)S(1)}, bf16[1024,1280]{1,0:T(8,128)(2,1)S(1)}) fusion(f32[1280]{0:T(1024)S(1)} %copy-done.7, bf16[1280,1024]{1,0:T(8,128)(2,1)} %shard_map.136, bf16[1280,1280]{1,0:T(8,128)(2,1)} %reshape.100, bf16[1024,1280]{1,0:T(8,128)(2,1)} %param.14), kind=kOutput, calls=%fused_computation.5 | convolution fusion | flops 3363306496 | bytes 11150336 | tf_op jit(solution)/shard_map/dot_general | solution.py:122
  180.4 0.8 fusion.8
  181.3 1.0 fusion.11
  182.3 2.9 %reshape.101 = bf16[256,5120]{1,0:T(8,128)(2,1)} reshape(bf16[1024,1280]{1,0:T(8,128)(2,1)S(1)} %fusion.11) | data formatting | bytes 5242880 | tf_op jit(solution)/shard_map/reshape | solution.py:131
  185.3 12.4 %slice.35 = bf16[128,400,128]{2,1,0:T(8,128)(2,1)} slice(bf16[128,500,128]{2,1,0:T(8,128)(2,1)} %all-gather.9.cloned.1.call-done), slice={[0:128], [100:500], [0:128]} | slice | bytes 26214400 | tf_op jit(solution)/shard_map/slice | solution.py:112
  197.6 19.7 %reshape.102 = bf16[1280,5120]{1,0:T(8,128)(2,1)} reshape(bf16[128,400,128]{2,1,0:T(8,128)(2,1)} %slice.35) | data formatting | bytes 26214400 | tf_op jit(solution)/shard_map/reshape | solution.py:112
  217.3 0.0 copy-done.1
  217.3 6.7 %fusion.19 = bf16[256,1280]{1,0:T(8,128)(2,1)S(1)} fusion(bf16[256,5120]{1,0:T(8,128)(2,1)S(1)} %copy-done.1, bf16[1280,5120]{1,0:T(8,128)(2,1)} %reshape.102, f32[1280]{0:T(1024)S(1)} %copy-done.8), kind=kOutput, calls=%fused_computation.26 | convolution fusion | flops 3356098560 | bytes 16389120 | tf_op jit(solution)/shard_map/dot_general | solution.py:27
  224.0 0.1 broadcast_in_dim.10
  224.1 0.6 fusion.21
  224.7 0.1 slice.48
  224.8 0.1 fusion.27
  225.0 0.3 concatenate.17
  225.3 0.7 pad_maximum_fusion
  226.0 29.9 %all_to_all.5 = bf16[128,4,1408]{2,1,0:T(4,128)(2,1)S(1)} all-to-all(bf16[128,4,1408]{2,1,0:T(4,128)(2,1)S(1)} %pad_maximum_fusion), channel_id=1, replica_groups=mesh['fsdp'=8,'dp'=16] {'fsdp','dp'}, dimensions={0} | all-to-all | bytes 2883584 | tf_op jit(solution)/shard_map/all_to_all | solution.py:156
  255.9 0.3 reshape.103
  256.3 0.1 convert_reduce_fusion.2
  256.4 1.4 convolution_convert_fusion
  (22 shorter events, 0.1 us)
Async XLA Ops:
  6.5 86.6 %copy-start = (bf16[1024,1280]{1,0:T(8,128)(2,1)S(1)}, bf16[1024,1280]{1,0:T(8,128)(2,1)}, u32[]{:S(2)}) copy-start(bf16[1024,1280]{1,0:T(8,128)(2,1)} %param.14) | copy-start | bytes 7864324
  6.5 79.2 %all-gather.7.cloned.1.call-start = ((), (), s32[]{:S(2)}) async-start(), calls=%async_computation.1 | async-start | bytes 10567680 | tf_op jit(solution)/shard_map/all_gather | solution.py:99
  7.3 159.2 %all-gather.9.cloned.1.call-start = ((), (), s32[]{:S(2)}) async-start(), calls=%async_computation.2 | async-start | bytes 16644096 | tf_op jit(solution)/shard_map/all_gather | solution.py:107
  94.0 13.7 %copy-start.4 = (f32[3840]{0:T(1024)S(1)}, f32[3840]{0:T(1024)}, u32[]{:S(2)}) copy-start(f32[3840]{0:T(1024)} %param.19) | copy-start | bytes 46084
  94.0 13.7 %copy-start.5 = (f32[1280]{0:T(1024)S(1)}, f32[1280]{0:T(1024)}, u32[]{:S(2)}) copy-start(f32[1280]{0:T(1024)} %param.17) | copy-start | bytes 15364
  94.0 13.6 %copy-start.6 = (f32[1280]{0:T(1024)S(1)}, f32[1280]{0:T(1024)}, u32[]{:S(2)}) copy-start(f32[1280]{0:T(1024)} %param.16) | copy-start | bytes 15364
  166.5 2.0 slice-start
  168.4 4.6 %copy-start.7 = (f32[1280]{0:T(1024)S(1)}, f32[1280]{0:T(1024)}, u32[]{:S(2)}) copy-start(f32[1280]{0:T(1024)} %param.21) | copy-start | bytes 15364
  173.1 8.2 %copy-start.2 = (f32[1280]{0:T(1024)S(1)}, f32[1280]{0:T(1024)}, u32[]{:S(2)}) copy-start(f32[1280]{0:T(1024)} %param.23) | copy-start | bytes 15364
  173.1 8.2 %copy-start.3 = (f32[1280]{0:T(1024)S(1)}, f32[1280]{0:T(1024)}, u32[]{:S(2)}) copy-start(f32[1280]{0:T(1024)} %param.22) | copy-start | bytes 15364
  197.6 19.7 %copy-start.1 = (bf16[256,5120]{1,0:T(8,128)(2,1)S(1)}, bf16[256,5120]{1,0:T(8,128)(2,1)}, u32[]{:S(2)}) copy-start(bf16[256,5120]{1,0:T(8,128)(2,1)} %reshape.101) | copy-start | bytes 7864324
  197.6 19.7 %copy-start.8 = (f32[1280]{0:T(1024)S(1)}, f32[1280]{0:T(1024)}, u32[]{:S(2)}) copy-start(f32[1280]{0:T(1024)} %param.25) | copy-start | bytes 15364
Sparse Core Ops, SparseCore 0:
  10.5 75.2 all-gather.6
  88.7 77.6 all-gather.8

commit v6 on v5

--- a/solution.py
+++ b/solution.py
@@ -96,20 +96,26 @@
     width = D
     axes = ("fsdp", "dp")
 
-    qkv_parts = lax.all_gather(qkv_weight, axes, axis=0, tiled=False)
+    qkv_rows = qkv_weight.shape[0]
     out_rows = out_weight.shape[0]
     merge_rows = merge_weight.shape[0]
-    lanes = 128
-    flat = jnp.concatenate(
-        [out_weight.reshape(-1, lanes), merge_weight.reshape(-1, lanes)], axis=0
-    )
-    qkv_parts, flat = lax.optimization_barrier((qkv_parts, flat))
-    rest = lax.all_gather(flat, axes, axis=0, tiled=False)
-    devices = rest.shape[0]
-    qkv_full = qkv_parts.reshape(devices * qkv_weight.shape[0], width)
-    out_cut = out_rows * width // lanes
-    out_full = rest[:, :out_cut].reshape(devices * out_rows, width)
-    merge_full = rest[:, out_cut:].reshape(devices * merge_rows, 4 * width)
+    tile_rows = 16
+    wide = 4 * width
+    first = jnp.concatenate([qkv_weight, out_weight], axis=0)
+    first_rows = first.shape[0]
+    first_parts = lax.all_gather(first, axes, axis=0, tiled=True)
+    merge_padded = jnp.concatenate(
+        [merge_weight, jnp.zeros((tile_rows - merge_rows, wide), merge_weight.dtype)], axis=0
+    )
+    first_parts, merge_padded = lax.optimization_barrier((first_parts, merge_padded))
+    merge_parts = lax.all_gather(merge_padded, axes, axis=0, tiled=True)
+    devices = first_parts.shape[0] // first_rows
+    device_base = jnp.arange(devices, dtype=jnp.int32)[:, None] * first_rows
+    qkv_index = (device_base + jnp.arange(qkv_rows, dtype=jnp.int32)[None, :]).reshape(-1)
+    out_index = (device_base + qkv_rows + jnp.arange(out_rows, dtype=jnp.int32)[None, :]).reshape(-1)
+    qkv_full = jnp.take(first_parts, qkv_index, axis=0, unique_indices=True, indices_are_sorted=True)
+    out_full = jnp.take(first_parts, out_index, axis=0, unique_indices=True, indices_are_sorted=True)
+    merge_full = merge_parts
 
     normed = layer_norm(patch_states, first_gain, first_shift).astype(jnp.bfloat16)
     joined_t = lax.dot_general(
@@ -130,7 +136,9 @@
         .astype(jnp.bfloat16)
         .reshape(tokens // 4, 4 * width)
     )
-    projected = (times_rows(merged, merge_full) + merge_bias).astype(jnp.bfloat16)
+    projected_padded = lax.optimization_barrier(times_rows(merged, merge_full))
+    projected = projected_padded.reshape(tokens // 4, devices, tile_rows)[:, :, :merge_rows]
+    projected = (projected.reshape(tokens // 4, width) + merge_bias).astype(jnp.bfloat16)
 
     fsdp_count = lax.axis_size("fsdp")
     dp_count = lax.axis_size("dp")

time: 266 us -> 267 us (level)
  local copies, waits for them, and re-layouts: 60.5 us -> 56.3 us
  matrix products: 33.3 us -> 37.4 us
    gather x0 -> x2, local copies, waits for them, and re-layouts: none -> 41.3 us  [the longest x1 27 us: per_device(): jnp.take(first_parts, qkv_index, axis=0, unique_indices=True, indices_are...]
    reshape x5 -> x1, local copies, waits for them, and re-layouts: 39.8 us -> 1.25 us  [per_device(): projected.reshape(tokens // 4, width) + merge_bias]
    slice x3 -> x0, local copies, waits for them, and re-layouts: 14.3 us -> none  [the longest x1 12.4 us: per_device(): merge_full = rest[:, out_cut:].reshape(devices * merge_rows, 4 * width)]
    dot_general x1, matrix products: 6.72 us -> 11.6 us  [times_rows(): lax.dot_general(left, piece, (((1,), (1,)), ((), ())), preferred_element_...]
  transfers between devices with their start and end apart: 2 -> 2, of which waited for: 2 -> 1; matrix products, arithmetic and copies ran while one was open for 16% -> 30% of each run, Pallas kernels for 15% -> 15%
where the time goes in v6:
time: 267 us
  waiting for transfers between devices  78.7 us (29%)
  local copies, waits for them, and re-layouts  56.3 us (21%)
  Pallas kernels  39 us (15%)
  matrix products  37.4 us (14%)
  blocking collectives  30 us (11%)
  between operations  13.7 us (5%)
  other arithmetic  11.5 us (4%)
    all_gather x1, waiting for transfers between devices, per_device(): first_parts = lax.all_gather(first, axes, axis=0, tiled=True)  78.6 us
    pallas_call x1, Pallas kernels, attention(): pl.pallas_call(functools.partial(attention_kernel, scale), out_shape=jax....  39 us
    all_to_all x1, blocking collectives, per_device(): lax.all_to_all(rows_out.reshape(count_dev, capacity, width + lanes), axes...  30 us
    gather x1, local copies, waits for them, and re-layouts, per_device(): jnp.take(first_parts, qkv_index, axis=0, unique_indices=True, indices_are...  27 us
    dot_general x1, matrix products, per_device(): lax.dot_general(qkv_full, normed, (((1,), (1,)), ((), ())), preferred_ele...  17.1 us
    gather x1, local copies, waits for them, and re-layouts, per_device(): jnp.take(first_parts, out_index, axis=0, unique_indices=True, indices_are...  14.3 us
    dot_general x1, matrix products, times_rows(): lax.dot_general(left, piece, (((1,), (1,)), ((), ())), preferred_element_...  11.6 us
    dot_general x1, matrix products, per_device(): lax.dot_general(attended_t, out_full, (((0,), (1,)), ((), ())), preferred...  6.76 us
  transfers between devices with their start and end apart: 2, of which 1 were waited for; matrix products, arithmetic and copies ran while one was open for 30% of the time, Pallas kernels for 15%

profile of v6, /device:TPU:1, one launch (start us, length us, event | category | flops | bytes accessed | tf_op | source)
XLA Modules:
  0.0 266.6 jit_solution(4624884022439234322)
XLA Ops:
  6.5 0.0 all-gather.3.cloned.1.call-start
  6.5 1.7 pad_maximum_fusion.1
  8.3 0.0 all-gather.3.cloned.1.call-update
  8.3 0.0 all-gather.5.cloned.1.call-start
  8.3 1.6 concatenate.19
  9.9 78.6 %all-gather.3.cloned.1.call-done = bf16[5120,1280]{1,0:T(8,128)(2,1)} async-done(((bf16[40,1280]{1,0:T(8,128)(2,1)}), bf16[5120,1280]{1,0:T(8,128)(2,1)}) %all-gather.3.cloned.1.call-update) | async-done | bytes 13107216 | tf_op jit(solution)/shard_map/all_gather | solution.py:106
  88.6 0.0 all-gather.5.cloned.1.call-update
  88.6 0.1 iota_add_fusion.1
  88.7 0.1 add.196
  88.8 0.1 add.193
  89.0 0.1 iota_add_fusion
  89.1 0.1 add.212
  89.2 0.1 add.209
  89.4 1.7 copy.26.qid_ref
  91.1 0.8 copy.24
  91.9 0.2 fusion.38
  92.2 0.7 convert_element_type.67
  93.0 0.9 fusion.40
  93.8 0.7 multiply_add_fusion
  94.5 0.2 fusion.34
  94.7 0.0 copy-done
  94.7 0.4 convert_reduce_fusion
  95.1 0.8 fusion.9
  96.0 27.0 %gather_fusion = bf16[3840,1280]{1,0:T(8,128)(2,1)} fusion(bf16[5120,1280]{1,0:T(8,128)(2,1)} %all-gather.3.cloned.1.call-done, s32[4096]{0:T(1024)S(1)} %pad_clamp_fusion), kind=kCustom, calls=%fused_computation | custom fusion | bytes 19676160 | tf_op jit(solution)/shard_map/jit(_take)/gather | solution.py:116
  123.0 14.3 %gather_fusion.1 = bf16[1280,1280]{1,0:T(8,128)(2,1)} fusion(bf16[5120,1280]{1,0:T(8,128)(2,1)} %all-gather.3.cloned.1.call-done, s32[2048]{0:T(1024)S(1)} %pad_clamp_fusion.1), kind=kCustom, calls=%fused_computation.1 | custom fusion | bytes 6558720 | tf_op jit(solution)/shard_map/jit(_take)/gather | solution.py:117
  137.3 0.0 copy-done.4
  137.3 0.0 copy-done.5
  137.3 17.1 %add_convert_fusion.q_ref.k_ref.v_ref = bf16[3840,1024]{1,0:T(8,128)(2,1)} fusion(f32[3840]{0:T(1024)S(1)} %copy-done.4, bf16[3840,1280]{1,0:T(8,128)(2,1)} %gather_fusion, pred[3840]{0:T(1024)(128)(4,1)S(1)} %compare_and_fusion, bf16[1024,1280]{1,0:T(8,128)(2,1)S(1)} %copy-done, f32[1280]{0:T(1024)S(1)} %copy-done.5, f32[1280]{0:T(1024)S(1)} %copy-done.6, ...), kind=kOutput, calls=%fused_computation.2 | convolution fusion | flops 10086973440 | bytes 20353792 | tf_op jit(solution)/shard_map/dot_general | solution.py:121
  154.4 39.0 %shard_map.136 = bf16[1280,1024]{1,0:T(8,128)(2,1)} custom-call(bf16[3840,1024]{1,0:T(8,128)(2,1)} %add_convert_fusion.q_ref.k_ref.v_ref, bf16[3840,1024]{1,0:T(8,128)(2,1)} %add_convert_fusion.q_ref.k_ref.v_ref, bf16[3840,1024]{1,0:T(8,128)(2,1)} %add_convert_fusion.q_ref.k_ref.v_ref, s32[1024,1]{1,0:T(8,128)} %copy.26.qid_ref, s32[1,1024]{1,0:T(1,128)} %bitcast.31), custom_call_target="tpu_custom_call" | custom-call | flops 5368709120 | bytes 10485760 | tf_op jit(solution)/shard_map/pallas_call | solution.py:63
  193.3 0.0 copy-start.2
  193.3 6.8 %convert_reduce_fusion.1 = (f32[1024]{0:T(1024)S(1)}, bf16[1024,1280]{1,0:T(8,128)(2,1)S(1)}) fusion(f32[1280]{0:T(1024)S(1)} %copy-done.7, bf16[1280,1024]{1,0:T(8,128)(2,1)} %shard_map.136, bf16[1280,1280]{1,0:T(8,128)(2,1)} %gather_fusion.1, pred[1280]{0:T(1024)(128)(4,1)S(1)} %compare_and_fusion.1, bf16[1024,1280]{1,0:T(8,128)(2,1)S(1)} %copy-done), kind=kOutput, calls=%fused_computation.10 | convolution fusion | flops 3364944896 | bytes 11151616 | tf_op jit(solution)/shard_map/dot_general | solution.py:128
  200.1 0.8 fusion.13
  201.0 1.0 fusion.16
  202.0 2.9 %reshape.174 = bf16[256,5120]{1,0:T(8,128)(2,1)} reshape(bf16[1024,1280]{1,0:T(8,128)(2,1)S(1)} %fusion.16) | data formatting | bytes 5242880 | tf_op jit(solution)/shard_map/reshape | solution.py:137
  204.9 11.6 %fusion.48 = f32[256,2048]{1,0:T(8,128)} fusion(bf16[256,5120]{1,0:T(8,128)(2,1)} %reshape.174, bf16[2048,5120]{1,0:T(8,128)(2,1)} %all-gather.5.cloned.1.call-done), kind=kOutput, calls=%fused_computation.85 | convolution fusion | flops 5368709120 | bytes 25690112 | tf_op jit(solution)/shard_map/dot_general | solution.py:27
  216.6 2.2 copy.27
  218.8 1.2 reshape.176
  220.0 0.0 copy-done.3
  220.0 1.5 add_convert_fusion.1
  221.6 0.6 fusion.29
  222.2 0.1 slice.47
  222.3 0.1 fusion.35
  222.5 1.2 concatenate.21
  223.7 2.0 pad_maximum_fusion
  225.7 30.0 %all_to_all.5 = bf16[128,4,1408]{2,1,0:T(4,128)(2,1)} all-to-all(bf16[128,4,1408]{2,1,0:T(4,128)(2,1)S(1)} %pad_maximum_fusion), channel_id=1, replica_groups=mesh['fsdp'=8,'dp'=16] {'fsdp','dp'}, dimensions={0} | all-to-all | bytes 2883584 | tf_op jit(solution)/shard_map/all_to_all | solution.py:164
  255.7 2.6 reshape.177
  258.3 0.1 convert_reduce_fusion.2
  258.4 1.4 convolution_convert_fusion
  (32 shorter events, 0.3 us)
Async XLA Ops:
  6.5 88.1 %copy-start = (bf16[1024,1280]{1,0:T(8,128)(2,1)S(1)}, bf16[1024,1280]{1,0:T(8,128)(2,1)}, u32[]{:S(2)}) copy-start(bf16[1024,1280]{1,0:T(8,128)(2,1)} %param.14) | copy-start | bytes 7864324
  6.5 82.0 %all-gather.3.cloned.1.call-start = ((), (), s32[]{:S(2)}) async-start(), calls=%async_computation.1 | async-start | bytes 13209600 | tf_op jit(solution)/shard_map/all_gather | solution.py:106
  8.3 196.7 %all-gather.5.cloned.1.call-start = ((), (), s32[]{:S(2)}) async-start(), calls=%async_computation.2 | async-start | bytes 21135360 | tf_op jit(solution)/shard_map/all_gather | solution.py:111
  123.0 14.3 %copy-start.4 = (f32[3840]{0:T(1024)S(1)}, f32[3840]{0:T(1024)}, u32[]{:S(2)}) copy-start(f32[3840]{0:T(1024)} %param.19) | copy-start | bytes 46084
  123.0 14.3 %copy-start.5 = (f32[1280]{0:T(1024)S(1)}, f32[1280]{0:T(1024)}, u32[]{:S(2)}) copy-start(f32[1280]{0:T(1024)} %param.17) | copy-start | bytes 15364
  123.0 14.3 %copy-start.6 = (f32[1280]{0:T(1024)S(1)}, f32[1280]{0:T(1024)}, u32[]{:S(2)}) copy-start(f32[1280]{0:T(1024)} %param.16) | copy-start | bytes 15364
  154.4 39.0 %copy-start.7 = (f32[1280]{0:T(1024)S(1)}, f32[1280]{0:T(1024)}, u32[]{:S(2)}) copy-start(f32[1280]{0:T(1024)} %param.21) | copy-start | bytes 15364
  193.3 7.6 %copy-start.1 = (f32[1280]{0:T(1024)S(1)}, f32[1280]{0:T(1024)}, u32[]{:S(2)}) copy-start(f32[1280]{0:T(1024)} %param.23) | copy-start | bytes 15364
  193.3 7.6 %copy-start.2 = (f32[1280]{0:T(1024)S(1)}, f32[1280]{0:T(1024)}, u32[]{:S(2)}) copy-start(f32[1280]{0:T(1024)} %param.22) | copy-start | bytes 15364
  216.6 3.5 %copy-start.3 = (f32[1280]{0:T(1024)S(1)}, f32[1280]{0:T(1024)}, u32[]{:S(2)}) copy-start(f32[1280]{0:T(1024)} %param.25) | copy-start | bytes 15364
Sparse Core Ops, SparseCore 0:
  10.3 78.1 all-gather.2
  91.5 86.7 all-gather.4

commit v7 on v6

--- a/solution.py
+++ b/solution.py
@@ -110,11 +110,23 @@
     first_parts, merge_padded = lax.optimization_barrier((first_parts, merge_padded))
     merge_parts = lax.all_gather(merge_padded, axes, axis=0, tiled=True)
     devices = first_parts.shape[0] // first_rows
-    device_base = jnp.arange(devices, dtype=jnp.int32)[:, None] * first_rows
-    qkv_index = (device_base + jnp.arange(qkv_rows, dtype=jnp.int32)[None, :]).reshape(-1)
-    out_index = (device_base + qkv_rows + jnp.arange(out_rows, dtype=jnp.int32)[None, :]).reshape(-1)
-    qkv_full = jnp.take(first_parts, qkv_index, axis=0, unique_indices=True, indices_are_sorted=True)
-    out_full = jnp.take(first_parts, out_index, axis=0, unique_indices=True, indices_are_sorted=True)
+    group = 8
+    blocks = first_parts.reshape(devices // group, group * first_rows, width)
+    source = lax.broadcasted_iota(jnp.int32, (1, group * first_rows), 1)
+
+    def selector(rows, offset):
+        target = lax.broadcasted_iota(jnp.int32, (group * rows, 1), 0)
+        wanted = (target // rows) * first_rows + offset + target % rows
+        return (wanted == source).astype(first_parts.dtype)
+
+    def pick(rows, offset):
+        picked = jnp.einsum(
+            "ij,bjk->bik", selector(rows, offset), blocks, preferred_element_type=jnp.float32
+        )
+        return picked.astype(first_parts.dtype).reshape(devices * rows, width)
+
+    qkv_full = pick(qkv_rows, 0)
+    out_full = pick(out_rows, qkv_rows)
     merge_full = merge_parts
 
     normed = layer_norm(patch_states, first_gain, first_shift).astype(jnp.bfloat16)

time: 267 us -> 233 us (0.87)
  local copies, waits for them, and re-layouts: 56.3 us -> 9.98 us
  matrix products: 37.4 us -> 50.6 us
    gather x2 -> x0, local copies, waits for them, and re-layouts: 41.3 us -> none  [the longest x1 27 us: per_device(): jnp.take(first_parts, qkv_index, axis=0, unique_indices=True, indices_are...]
    dot_general x0 -> x2, matrix products: none -> 19.1 us  [pick(): jnp.einsum('ij,bjk->bik', selector(rows, offset), blocks, preferred_eleme...]
    dot_general x1, matrix products: 17.1 us -> 13.5 us  [per_device(): lax.dot_general(qkv_full, normed, (((1,), (1,)), ((), ())), preferred_ele...]
  transfers between devices with their start and end apart: 2 -> 2, of which waited for: 1 -> 2; matrix products, arithmetic and copies ran while one was open for 30% -> 22% of each run, Pallas kernels for 15% -> 17%
where the time goes in v7:
time: 233 us
  waiting for transfers between devices  79.5 us (34%)
  matrix products  50.6 us (22%)
  Pallas kernels  38.6 us (17%)
  blocking collectives  29.9 us (13%)
  between operations  13.7 us (6%)
  other arithmetic  10.4 us (4%)
  local copies, waits for them, and re-layouts  9.98 us (4%)
    all_gather x1, waiting for transfers between devices, per_device(): first_parts = lax.all_gather(first, axes, axis=0, tiled=True)  78.6 us
    pallas_call x1, Pallas kernels, attention(): pl.pallas_call(functools.partial(attention_kernel, scale), out_shape=jax....  38.6 us
    all_to_all x1, blocking collectives, per_device(): lax.all_to_all(rows_out.reshape(count_dev, capacity, width + lanes), axes...  29.9 us
    dot_general x2, matrix products, pick(): jnp.einsum('ij,bjk->bik', selector(rows, offset), blocks, preferred_eleme...  19.1 us
    dot_general x1, matrix products, per_device(): lax.dot_general(qkv_full, normed, (((1,), (1,)), ((), ())), preferred_ele...  13.5 us
    dot_general x1, matrix products, times_rows(): lax.dot_general(left, piece, (((1,), (1,)), ((), ())), preferred_element_...  11.6 us
  transfers between devices with their start and end apart: 2, of which 2 were waited for; matrix products, arithmetic and copies ran while one was open for 22% of the time, Pallas kernels for 17%

profile of v7, /device:TPU:1, one launch (start us, length us, event | category | flops | bytes accessed | tf_op | source)
XLA Modules:
  0.0 232.8 jit_solution(6161518563963650995)
XLA Ops:
  6.5 0.0 all-gather.3.cloned.1.call-start
  6.5 1.7 pad_maximum_fusion.1
  8.3 0.0 all-gather.3.cloned.1.call-update
  8.3 0.0 all-gather.5.cloned.1.call-start
  8.3 1.6 concatenate.19
  9.9 78.6 %all-gather.3.cloned.1.call-done = bf16[5120,1280]{1,0:T(8,128)(2,1)} async-done(((bf16[40,1280]{1,0:T(8,128)(2,1)}), bf16[5120,1280]{1,0:T(8,128)(2,1)}) %all-gather.3.cloned.1.call-update) | async-done | bytes 13107216 | tf_op jit(solution)/shard_map/all_gather | solution.py:106
  88.6 0.0 all-gather.5.cloned.1.call-update
  88.6 1.7 copy.26.qid_ref
  90.3 0.8 copy.24
  91.1 0.2 fusion.32
  91.4 0.7 convert_element_type.85
  92.1 0.9 fusion.34
  93.0 0.7 multiply_add_fusion
  93.7 0.2 fusion.27
  93.8 2.2 convert_reduce_fusion
  96.0 0.0 copy-done
  96.0 0.8 fusion.4
  96.8 0.0 copy-start.4
  96.8 0.0 copy-start.5
  96.9 0.0 copy-start.6
  96.9 10.7 %convolution_convert_fusion = bf16[16,1280,240]{1,2,0:T(8,128)(2,1)S(1)} fusion(bf16[16,320,1280]{2,1,0:T(8,128)(2,1)} %bitcast.41, s32[240]{0:T(256)S(1)} %fusion.42), kind=kOutput, calls=%fused_computation.1 | convolution fusion | flops 3150720000 | bytes 22938560 | tf_op jit(solution)/shard_map/ij,bjk->bik/dot_general | solution.py:123
  107.6 13.5 %add_convert_fusion.q_ref.k_ref.v_ref = bf16[3840,1024]{1,0:T(8,128)(2,1)} fusion(bf16[3840,1280]{1,0:T(8,128)(2,1)S(1)} %bitcast.43, f32[3840]{0:T(1024)S(1)} %copy-done.4, bf16[1024,1280]{1,0:T(8,128)(2,1)S(1)} %copy-done, f32[1280]{0:T(1024)S(1)} %copy-done.5, f32[1280]{0:T(1024)S(1)} %copy-done.6, f32[1024]{0:T(1024)S(1)} %add_rsqrt_fusion.1, ...), kind=kOutput, calls=%fused_computation | convolution fusion | flops 10082058240 | bytes 20349952 | tf_op jit(solution)/shard_map/dot_general | solution.py:133
  121.2 38.6 %shard_map.136 = bf16[1280,1024]{1,0:T(8,128)(2,1)} custom-call(bf16[3840,1024]{1,0:T(8,128)(2,1)} %add_convert_fusion.q_ref.k_ref.v_ref, bf16[3840,1024]{1,0:T(8,128)(2,1)} %add_convert_fusion.q_ref.k_ref.v_ref, bf16[3840,1024]{1,0:T(8,128)(2,1)} %add_convert_fusion.q_ref.k_ref.v_ref, s32[1024,1]{1,0:T(8,128)} %copy.26.qid_ref, s32[1,1024]{1,0:T(1,128)} %bitcast.52), custom_call_target="tpu_custom_call" | custom-call | flops 5368709120 | bytes 10485760 | tf_op jit(solution)/shard_map/pallas_call | solution.py:63
  159.7 8.4 %convolution_convert_fusion.1 = bf16[16,1280,80]{1,2,0:T(8,128)(2,1)S(1)} fusion(bf16[16,320,1280]{2,1,0:T(8,128)(2,1)} %bitcast.42, s32[80]{0:T(128)S(1)} %fusion.44), kind=kOutput, calls=%fused_computation.21 | convolution fusion | flops 1050240000 | bytes 16384320 | tf_op jit(solution)/shard_map/ij,bjk->bik/dot_general | solution.py:123
  168.1 0.0 copy-done.7
  168.1 0.0 copy-done.8
  168.1 0.0 copy-start.1
  168.2 0.0 copy-start.2
  168.2 4.4 %convert_reduce_fusion.1 = (f32[1024]{0:T(1024)S(1)}, bf16[1024,1280]{1,0:T(8,128)(2,1)S(1)}) fusion(f32[1280]{0:T(1024)S(1)} %copy-done.7, bf16[1280,1024]{1,0:T(8,128)(2,1)S(1)} %copy-done.8, bf16[1280,1280]{1,0:T(8,128)(2,1)S(1)} %bitcast.45, bf16[1024,1280]{1,0:T(8,128)(2,1)S(1)} %copy-done), kind=kOutput, calls=%fused_computation.6 | convolution fusion | flops 3363306496 | bytes 11150336 | tf_op jit(solution)/shard_map/dot_general | solution.py:140
  172.6 0.8 fusion.8
  173.4 0.0 copy-done.1
  173.4 0.0 copy-done.2
  173.4 1.0 fusion.11
  174.5 2.9 %reshape.178 = bf16[256,5120]{1,0:T(8,128)(2,1)} reshape(bf16[1024,1280]{1,0:T(8,128)(2,1)S(1)} %fusion.11) | data formatting | bytes 5242880 | tf_op jit(solution)/shard_map/reshape | solution.py:149
  177.4 0.8 all-gather.5.cloned.1.call-done
  178.2 11.6 %fusion.48 = f32[256,2048]{1,0:T(8,128)} fusion(bf16[256,5120]{1,0:T(8,128)(2,1)} %reshape.178, bf16[2048,5120]{1,0:T(8,128)(2,1)} %all-gather.5.cloned.1.call-done), kind=kOutput, calls=%fused_computation.85 | convolution fusion | flops 5368709120 | bytes 25690112 | tf_op jit(solution)/shard_map/dot_general | solution.py:27
  189.9 1.9 copy.27
  191.8 0.2 reshape.180
  192.0 0.2 add_convert_fusion.1
  192.3 0.6 fusion.20
  192.9 0.1 slice.43
  193.0 0.1 fusion.28
  193.1 0.3 concatenate.21
  193.5 0.7 pad_maximum_fusion
  194.2 29.9 %all_to_all.5 = bf16[128,4,1408]{2,1,0:T(4,128)(2,1)S(1)} all-to-all(bf16[128,4,1408]{2,1,0:T(4,128)(2,1)S(1)} %pad_maximum_fusion), channel_id=1, replica_groups=mesh['fsdp'=8,'dp'=16] {'fsdp','dp'}, dimensions={0} | all-to-all | bytes 2883584 | tf_op jit(solution)/shard_map/all_to_all | solution.py:176
  224.1 0.3 reshape.181
  224.4 0.1 convert_reduce_fusion.2
  224.6 1.4 convolution_convert_fusion.2
  (22 shorter events, 0.2 us)
Async XLA Ops:
  6.5 89.4 %copy-start = (bf16[1024,1280]{1,0:T(8,128)(2,1)S(1)}, bf16[1024,1280]{1,0:T(8,128)(2,1)}, u32[]{:S(2)}) copy-start(bf16[1024,1280]{1,0:T(8,128)(2,1)} %param.14) | copy-start | bytes 7864324
  6.5 82.0 %all-gather.3.cloned.1.call-start = ((), (), s32[]{:S(2)}) async-start(), calls=%async_computation.1 | async-start | bytes 13209600 | tf_op jit(solution)/shard_map/all_gather | solution.py:106
  8.3 169.9 %all-gather.5.cloned.1.call-start = ((), (), s32[]{:S(2)}) async-start(), calls=%async_computation.2 | async-start | bytes 21135360 | tf_op jit(solution)/shard_map/all_gather | solution.py:111
  96.8 10.8 %copy-start.4 = (f32[3840]{0:T(1024)S(1)}, f32[3840]{0:T(1024)}, u32[]{:S(2)}) copy-start(f32[3840]{0:T(1024)} %param.19) | copy-start | bytes 46084
  96.8 10.8 %copy-start.5 = (f32[1280]{0:T(1024)S(1)}, f32[1280]{0:T(1024)}, u32[]{:S(2)}) copy-start(f32[1280]{0:T(1024)} %param.17) | copy-start | bytes 15364
  96.9 10.8 %copy-start.6 = (f32[1280]{0:T(1024)S(1)}, f32[1280]{0:T(1024)}, u32[]{:S(2)}) copy-start(f32[1280]{0:T(1024)} %param.16) | copy-start | bytes 15364
  159.7 8.4 %copy-start.7 = (f32[1280]{0:T(1024)S(1)}, f32[1280]{0:T(1024)}, u32[]{:S(2)}) copy-start(f32[1280]{0:T(1024)} %param.21) | copy-start | bytes 15364
  159.7 8.4 %copy-start.8 = (bf16[1280,1024]{1,0:T(8,128)(2,1)S(1)}, bf16[1280,1024]{1,0:T(8,128)(2,1)}, u32[]{:S(2)}) copy-start(bf16[1280,1024]{1,0:T(8,128)(2,1)} %shard_map.136) | copy-start | bytes 7864324
  168.1 5.3 %copy-start.1 = (f32[1280]{0:T(1024)S(1)}, f32[1280]{0:T(1024)}, u32[]{:S(2)}) copy-start(f32[1280]{0:T(1024)} %param.23) | copy-start | bytes 15364
  168.2 5.3 %copy-start.2 = (f32[1280]{0:T(1024)S(1)}, f32[1280]{0:T(1024)}, u32[]{:S(2)}) copy-start(f32[1280]{0:T(1024)} %param.22) | copy-start | bytes 15364
  189.9 2.1 copy-start.3
Sparse Core Ops, SparseCore 0:
  10.3 78.1 all-gather.2
  91.5 86.6 all-gather.4

commit v8 on v7

--- a/solution.py
+++ b/solution.py
@@ -173,13 +173,10 @@
     empty = (jnp.sum(place, axis=1, keepdims=True) == 0)
     slot_lane = jnp.where(empty, float(row_count), rows_out[:, width:])
     rows_out = jnp.concatenate([rows_out[:, :width], slot_lane], axis=1).astype(jnp.bfloat16)
-    got = lax.all_to_all(
-        rows_out.reshape(count_dev, capacity, width + lanes),
-        axes,
-        split_axis=0,
-        concat_axis=0,
-        tiled=True,
-    ).reshape(count_dev * capacity, width + lanes)
+    staged = rows_out.reshape(fsdp_count, dp_count, capacity, width + lanes)
+    staged = lax.all_to_all(staged, "dp", split_axis=1, concat_axis=1, tiled=True)
+    staged = lax.all_to_all(staged, "fsdp", split_axis=0, concat_axis=0, tiled=True)
+    got = staged.reshape(count_dev * capacity, width + lanes)
     got_slots = got[:, width].astype(jnp.int32)
     pick = (
         got_slots[None, :] == jnp.arange(row_count, dtype=jnp.int32)[:, None]

time: 233 us -> 255 us (1.094)
  blocking collectives: 29.9 us -> 50.6 us
    all_to_all x1 -> x2, blocking collectives: 29.9 us -> 50.6 us  [the longest x1 26.1 us: per_device(): lax.all_to_all(staged, 'dp', split_axis=1, concat_axis=1, tiled=True)]
  transfers between devices with their start and end apart: 2 -> 2, of which waited for: 2 -> 2; matrix products, arithmetic and copies ran while one was open for 22% -> 20% of each run, Pallas kernels for 17% -> 15%
where the time goes in v8:
time: 255 us; the launch traced here: 254 us
  waiting for transfers between devices  79.5 us (31%)
  matrix products  50.6 us (20%)
  blocking collectives  50.6 us (20%)
  Pallas kernels  38.6 us (15%)
  between operations  13.7 us (5%)
  local copies, waits for them, and re-layouts  11 us (4%)
  other arithmetic  10.5 us (4%)
    all_gather x1, waiting for transfers between devices, per_device(): first_parts = lax.all_gather(first, axes, axis=0, tiled=True)  78.6 us
    pallas_call x1, Pallas kernels, attention(): pl.pallas_call(functools.partial(attention_kernel, scale), out_shape=jax....  38.6 us
    all_to_all x1, blocking collectives, per_device(): lax.all_to_all(staged, 'dp', split_axis=1, concat_axis=1, tiled=True)  26.1 us
    all_to_all x1, blocking collectives, per_device(): lax.all_to_all(staged, 'fsdp', split_axis=0, concat_axis=0, tiled=True)  24.4 us
    dot_general x2, matrix products, pick(): jnp.einsum('ij,bjk->bik', selector(rows, offset), blocks, preferred_eleme...  19.1 us
    dot_general x1, matrix products, per_device(): lax.dot_general(qkv_full, normed, (((1,), (1,)), ((), ())), preferred_ele...  13.5 us
    dot_general x1, matrix products, times_rows(): lax.dot_general(left, piece, (((1,), (1,)), ((), ())), preferred_element_...  11.6 us
  transfers between devices with their start and end apart: 2, of which 2 were waited for; matrix products, arithmetic and copies ran while one was open for 20% of the time, Pallas kernels for 15%

profile of v8, /device:TPU:1, one launch (start us, length us, event | category | flops | bytes accessed | tf_op | source)
XLA Modules:
  0.0 254.5 jit_solution(46538396096138168)
XLA Ops:
  6.5 0.0 all-gather.3.cloned.1.call-start
  6.5 1.7 pad_maximum_fusion.1
  8.3 0.0 all-gather.3.cloned.1.call-update
  8.3 0.0 all-gather.5.cloned.1.call-start
  8.3 1.6 concatenate.19
  9.9 78.6 %all-gather.3.cloned.1.call-done = bf16[5120,1280]{1,0:T(8,128)(2,1)} async-done(((bf16[40,1280]{1,0:T(8,128)(2,1)}), bf16[5120,1280]{1,0:T(8,128)(2,1)}) %all-gather.3.cloned.1.call-update) | async-done | bytes 13107216 | tf_op jit(solution)/shard_map/all_gather | solution.py:106
  88.6 0.0 all-gather.5.cloned.1.call-update
  88.6 1.7 copy.40.qid_ref
  90.3 0.8 copy.38
  91.1 0.2 fusion.32
  91.4 0.7 convert_element_type.85
  92.1 0.9 fusion.34
  93.0 0.7 multiply_add_fusion
  93.7 0.2 fusion.27
  93.8 2.2 convert_reduce_fusion
  96.0 0.8 fusion.4
  96.8 0.0 copy-start.4
  96.8 0.0 copy-start.5
  96.9 0.0 copy-start.6
  96.9 10.7 %convolution_convert_fusion = bf16[16,1280,240]{1,2,0:T(8,128)(2,1)S(1)} fusion(bf16[16,320,1280]{2,1,0:T(8,128)(2,1)} %bitcast.41, s32[240]{0:T(256)S(1)} %fusion.42), kind=kOutput, calls=%fused_computation.1 | convolution fusion | flops 3150720000 | bytes 22938560 | tf_op jit(solution)/shard_map/ij,bjk->bik/dot_general | solution.py:123
  107.6 0.0 copy-done.4
  107.6 0.0 copy-done.5
  107.6 13.5 %add_convert_fusion.q_ref.k_ref.v_ref = bf16[3840,1024]{1,0:T(8,128)(2,1)} fusion(bf16[3840,1280]{1,0:T(8,128)(2,1)S(1)} %bitcast.43, f32[3840]{0:T(1024)S(1)} %copy-done.4, bf16[1024,1280]{1,0:T(8,128)(2,1)S(1)} %copy-done, f32[1280]{0:T(1024)S(1)} %copy-done.5, f32[1280]{0:T(1024)S(1)} %copy-done.6, f32[1024]{0:T(1024)S(1)} %add_rsqrt_fusion.1, ...), kind=kOutput, calls=%fused_computation | convolution fusion | flops 10082058240 | bytes 20349952 | tf_op jit(solution)/shard_map/dot_general | solution.py:133
  121.2 38.6 %shard_map.136 = bf16[1280,1024]{1,0:T(8,128)(2,1)} custom-call(bf16[3840,1024]{1,0:T(8,128)(2,1)} %add_convert_fusion.q_ref.k_ref.v_ref, bf16[3840,1024]{1,0:T(8,128)(2,1)} %add_convert_fusion.q_ref.k_ref.v_ref, bf16[3840,1024]{1,0:T(8,128)(2,1)} %add_convert_fusion.q_ref.k_ref.v_ref, s32[1024,1]{1,0:T(8,128)} %copy.40.qid_ref, s32[1,1024]{1,0:T(1,128)} %bitcast.52), custom_call_target="tpu_custom_call" | custom-call | flops 5368709120 | bytes 10485760 | tf_op jit(solution)/shard_map/pallas_call | solution.py:63
  159.7 8.4 %convolution_convert_fusion.1 = bf16[16,1280,80]{1,2,0:T(8,128)(2,1)S(1)} fusion(bf16[16,320,1280]{2,1,0:T(8,128)(2,1)} %bitcast.42, s32[80]{0:T(128)S(1)} %fusion.44), kind=kOutput, calls=%fused_computation.21 | convolution fusion | flops 1050240000 | bytes 16384320 | tf_op jit(solution)/shard_map/ij,bjk->bik/dot_general | solution.py:123
  168.1 0.0 copy-start.1
  168.2 0.0 copy-start.2
  168.2 4.4 %convert_reduce_fusion.1 = (f32[1024]{0:T(1024)S(1)}, bf16[1024,1280]{1,0:T(8,128)(2,1)S(1)}) fusion(f32[1280]{0:T(1024)S(1)} %copy-done.7, bf16[1280,1024]{1,0:T(8,128)(2,1)S(1)} %copy-done.8, bf16[1280,1280]{1,0:T(8,128)(2,1)S(1)} %bitcast.45, bf16[1024,1280]{1,0:T(8,128)(2,1)S(1)} %copy-done), kind=kOutput, calls=%fused_computation.6 | convolution fusion | flops 3363306496 | bytes 11150336 | tf_op jit(solution)/shard_map/dot_general | solution.py:140
  172.6 0.8 fusion.8
  173.4 1.0 fusion.11
  174.5 2.9 %reshape.178 = bf16[256,5120]{1,0:T(8,128)(2,1)} reshape(bf16[1024,1280]{1,0:T(8,128)(2,1)S(1)} %fusion.11) | data formatting | bytes 5242880 | tf_op jit(solution)/shard_map/reshape | solution.py:149
  177.4 0.8 all-gather.5.cloned.1.call-done
  178.2 11.6 %fusion.48 = f32[256,2048]{1,0:T(8,128)} fusion(bf16[256,5120]{1,0:T(8,128)(2,1)} %reshape.178, bf16[2048,5120]{1,0:T(8,128)(2,1)} %all-gather.5.cloned.1.call-done), kind=kOutput, calls=%fused_computation.85 | convolution fusion | flops 5368709120 | bytes 25690112 | tf_op jit(solution)/shard_map/dot_general | solution.py:27
  189.9 1.9 copy.41
  191.8 0.2 reshape.180
  192.0 0.2 add_convert_fusion.1
  192.3 0.6 fusion.20
  192.9 0.1 slice.43
  193.0 0.1 fusion.28
  193.1 0.3 concatenate.21
  193.5 0.7 pad_maximum_fusion
  194.2 0.5 copy.45
  194.7 26.1 %all_to_all.10 = bf16[8,16,4,1408]{3,2,0,1:T(4,128)(2,1)S(1)} all-to-all(bf16[8,16,4,1408]{3,2,0,1:T(4,128)(2,1)S(1)} %copy.45), channel_id=1, replica_groups=mesh['fsdp'=8,'dp'=16] {'dp'}, dimensions={1} | all-to-all | bytes 2883584 | tf_op jit(solution)/shard_map/all_to_all | solution.py:177
  220.9 0.5 copy.44
  221.4 24.4 %all_to_all.11 = bf16[8,16,4,1408]{3,2,1,0:T(4,128)(2,1)S(1)} all-to-all(bf16[8,16,4,1408]{3,2,1,0:T(4,128)(2,1)S(1)} %copy.44), channel_id=1, replica_groups=mesh['fsdp'=8,'dp'=16] {'fsdp'}, dimensions={0} | all-to-all | bytes 2883584 | tf_op jit(solution)/shard_map/all_to_all | solution.py:178
  245.8 0.3 reshape.181
  246.2 0.1 convert_reduce_fusion.2
  246.3 1.3 convolution_convert_fusion.2
  (25 shorter events, 0.2 us)
Async XLA Ops:
  6.5 89.4 %copy-start = (bf16[1024,1280]{1,0:T(8,128)(2,1)S(1)}, bf16[1024,1280]{1,0:T(8,128)(2,1)}, u32[]{:S(2)}) copy-start(bf16[1024,1280]{1,0:T(8,128)(2,1)} %param.14) | copy-start | bytes 7864324
  6.5 82.0 %all-gather.3.cloned.1.call-start = ((), (), s32[]{:S(2)}) async-start(), calls=%async_computation.2 | async-start | bytes 13209600 | tf_op jit(solution)/shard_map/all_gather | solution.py:106
  8.3 169.9 %all-gather.5.cloned.1.call-start = ((), (), s32[]{:S(2)}) async-start(), calls=%async_computation.3 | async-start | bytes 21135360 | tf_op jit(solution)/shard_map/all_gather | solution.py:111
  96.8 10.8 %copy-start.4 = (f32[3840]{0:T(1024)S(1)}, f32[3840]{0:T(1024)}, u32[]{:S(2)}) copy-start(f32[3840]{0:T(1024)} %param.19) | copy-start | bytes 46084
  96.8 10.8 %copy-start.5 = (f32[1280]{0:T(1024)S(1)}, f32[1280]{0:T(1024)}, u32[]{:S(2)}) copy-start(f32[1280]{0:T(1024)} %param.17) | copy-start | bytes 15364
  96.9 10.8 %copy-start.6 = (f32[1280]{0:T(1024)S(1)}, f32[1280]{0:T(1024)}, u32[]{:S(2)}) copy-start(f32[1280]{0:T(1024)} %param.16) | copy-start | bytes 15364
  159.7 8.4 %copy-start.7 = (f32[1280]{0:T(1024)S(1)}, f32[1280]{0:T(1024)}, u32[]{:S(2)}) copy-start(f32[1280]{0:T(1024)} %param.21) | copy-start | bytes 15364
  159.7 8.4 %copy-start.8 = (bf16[1280,1024]{1,0:T(8,128)(2,1)S(1)}, bf16[1280,1024]{1,0:T(8,128)(2,1)}, u32[]{:S(2)}) copy-start(bf16[1280,1024]{1,0:T(8,128)(2,1)} %shard_map.136) | copy-start | bytes 7864324
  168.1 5.3 %copy-start.1 = (f32[1280]{0:T(1024)S(1)}, f32[1280]{0:T(1024)}, u32[]{:S(2)}) copy-start(f32[1280]{0:T(1024)} %param.23) | copy-start | bytes 15364
  168.2 5.3 %copy-start.2 = (f32[1280]{0:T(1024)S(1)}, f32[1280]{0:T(1024)}, u32[]{:S(2)}) copy-start(f32[1280]{0:T(1024)} %param.22) | copy-start | bytes 15364
  189.9 2.1 copy-start.3
Sparse Core Ops, SparseCore 0:
  10.3 78.1 all-gather.2
  91.5 86.6 all-gather.4

commit v9 on v7

--- a/solution.py
+++ b/solution.py
@@ -107,7 +107,6 @@
     merge_padded = jnp.concatenate(
         [merge_weight, jnp.zeros((tile_rows - merge_rows, wide), merge_weight.dtype)], axis=0
     )
-    first_parts, merge_padded = lax.optimization_barrier((first_parts, merge_padded))
     merge_parts = lax.all_gather(merge_padded, axes, axis=0, tiled=True)
     devices = first_parts.shape[0] // first_rows
     group = 8

time: 233 us -> 233 us (level)
    all_gather x1, waiting for transfers between devices: 0.83 us -> 9.22 us  [per_device(): merge_parts = lax.all_gather(merge_padded, axes, axis=0, tiled=True)]
    all_gather x1, waiting for transfers between devices: 78.6 us -> 70.4 us  [per_device(): first_parts = lax.all_gather(first, axes, axis=0, tiled=True)]
  transfers between devices with their start and end apart: 2 -> 2, of which waited for: 2 -> 2; matrix products, arithmetic and copies ran while one was open for 22% -> 22% of each run, Pallas kernels for 17% -> 16%
where the time goes in v9:
time: 233 us
  waiting for transfers between devices  79.6 us (34%)
  matrix products  50.8 us (22%)
  Pallas kernels  38.4 us (16%)
  blocking collectives  29.9 us (13%)
  between operations  13.7 us (6%)
  other arithmetic  10.4 us (4%)
  local copies, waits for them, and re-layouts  9.98 us (4%)
    all_gather x1, waiting for transfers between devices, per_device(): first_parts = lax.all_gather(first, axes, axis=0, tiled=True)  70.4 us
    pallas_call x1, Pallas kernels, attention(): pl.pallas_call(functools.partial(attention_kernel, scale), out_shape=jax....  38.4 us
    all_to_all x1, blocking collectives, per_device(): lax.all_to_all(rows_out.reshape(count_dev, capacity, width + lanes), axes...  29.9 us
    dot_general x2, matrix products, pick(): jnp.einsum('ij,bjk->bik', selector(rows, offset), blocks, preferred_eleme...  19.2 us
    dot_general x1, matrix products, per_device(): lax.dot_general(qkv_full, normed, (((1,), (1,)), ((), ())), preferred_ele...  13.5 us
    dot_general x1, matrix products, times_rows(): lax.dot_general(left, piece, (((1,), (1,)), ((), ())), preferred_element_...  11.6 us
    all_gather x1, waiting for transfers between devices, per_device(): merge_parts = lax.all_gather(merge_padded, axes, axis=0, tiled=True)  9.22 us
  transfers between devices with their start and end apart: 2, of which 2 were waited for; matrix products, arithmetic and copies ran while one was open for 22% of the time, Pallas kernels for 16%

profile of v9, /device:TPU:1, one launch (start us, length us, event | category | flops | bytes accessed | tf_op | source)
XLA Modules:
  0.0 232.8 jit_solution(1475597498422621237)
XLA Ops:
  6.5 0.0 all-gather.3.cloned.1.call-start
  6.5 1.7 pad_maximum_fusion.1
  8.2 0.0 all-gather.3.cloned.1.call-update
  8.3 0.0 all-gather.5.cloned.1.call-start
  8.3 1.6 concatenate.19
  9.9 0.0 all-gather.5.cloned.1.call-update
  9.9 1.7 copy.26.qid_ref
  11.6 0.8 copy.24
  12.4 0.2 fusion.32
  12.7 0.7 convert_element_type.85
  13.4 0.9 fusion.34
  14.3 0.7 multiply_add_fusion
  15.0 0.2 fusion.27
  15.2 2.2 convert_reduce_fusion
  17.3 0.0 copy-done
  17.3 0.8 fusion.4
  18.2 70.4 %all-gather.3.cloned.1.call-done = bf16[5120,1280]{1,0:T(8,128)(2,1)} async-done(((bf16[40,1280]{1,0:T(8,128)(2,1)}), bf16[5120,1280]{1,0:T(8,128)(2,1)}) %all-gather.3.cloned.1.call-update) | async-done | bytes 13107216 | tf_op jit(solution)/shard_map/all_gather | solution.py:106
  88.6 10.7 %convolution_convert_fusion = bf16[16,1280,240]{1,2,0:T(8,128)(2,1)S(1)} fusion(bf16[16,320,1280]{2,1,0:T(8,128)(2,1)} %bitcast.41, s32[240]{0:T(256)S(1)} %fusion.42), kind=kOutput, calls=%fused_computation.1 | convolution fusion | flops 3150720000 | bytes 22938560 | tf_op jit(solution)/shard_map/ij,bjk->bik/dot_general | solution.py:122
  99.3 0.0 copy-done.4
  99.3 0.0 copy-done.5
  99.3 0.0 copy-done.6
  99.3 13.5 %add_convert_fusion.q_ref.k_ref.v_ref = bf16[3840,1024]{1,0:T(8,128)(2,1)} fusion(bf16[3840,1280]{1,0:T(8,128)(2,1)S(1)} %bitcast.43, f32[3840]{0:T(1024)S(1)} %copy-done.4, bf16[1024,1280]{1,0:T(8,128)(2,1)S(1)} %copy-done, f32[1280]{0:T(1024)S(1)} %copy-done.5, f32[1280]{0:T(1024)S(1)} %copy-done.6, f32[1024]{0:T(1024)S(1)} %add_rsqrt_fusion.1, ...), kind=kOutput, calls=%fused_computation | convolution fusion | flops 10082058240 | bytes 20349952 | tf_op jit(solution)/shard_map/dot_general | solution.py:132
  112.8 38.4 %shard_map.136 = bf16[1280,1024]{1,0:T(8,128)(2,1)} custom-call(bf16[3840,1024]{1,0:T(8,128)(2,1)} %add_convert_fusion.q_ref.k_ref.v_ref, bf16[3840,1024]{1,0:T(8,128)(2,1)} %add_convert_fusion.q_ref.k_ref.v_ref, bf16[3840,1024]{1,0:T(8,128)(2,1)} %add_convert_fusion.q_ref.k_ref.v_ref, s32[1024,1]{1,0:T(8,128)} %copy.26.qid_ref, s32[1,1024]{1,0:T(1,128)} %bitcast.52), custom_call_target="tpu_custom_call" | custom-call | flops 5368709120 | bytes 10485760 | tf_op jit(solution)/shard_map/pallas_call | solution.py:63
  151.2 8.5 %convolution_convert_fusion.1 = bf16[16,1280,80]{1,2,0:T(8,128)(2,1)S(1)} fusion(bf16[16,320,1280]{2,1,0:T(8,128)(2,1)} %bitcast.42, s32[80]{0:T(128)S(1)} %fusion.44), kind=kOutput, calls=%fused_computation.21 | convolution fusion | flops 1050240000 | bytes 16384320 | tf_op jit(solution)/shard_map/ij,bjk->bik/dot_general | solution.py:122
  159.7 0.0 copy-done.7
  159.8 0.0 copy-done.8
  159.8 0.0 copy-start.1
  159.8 0.0 copy-start.2
  159.8 4.4 %convert_reduce_fusion.1 = (f32[1024]{0:T(1024)S(1)}, bf16[1024,1280]{1,0:T(8,128)(2,1)S(1)}) fusion(f32[1280]{0:T(1024)S(1)} %copy-done.7, bf16[1280,1024]{1,0:T(8,128)(2,1)S(1)} %copy-done.8, bf16[1280,1280]{1,0:T(8,128)(2,1)S(1)} %bitcast.45, bf16[1024,1280]{1,0:T(8,128)(2,1)S(1)} %copy-done), kind=kOutput, calls=%fused_computation.6 | convolution fusion | flops 3363306496 | bytes 11150336 | tf_op jit(solution)/shard_map/dot_general | solution.py:139
  164.2 0.8 fusion.8
  165.0 0.0 copy-done.1
  165.1 0.0 copy-done.2
  165.1 1.0 fusion.11
  166.1 2.9 %reshape.178 = bf16[256,5120]{1,0:T(8,128)(2,1)} reshape(bf16[1024,1280]{1,0:T(8,128)(2,1)S(1)} %fusion.11) | data formatting | bytes 5242880 | tf_op jit(solution)/shard_map/reshape | solution.py:148
  169.0 9.2 %all-gather.5.cloned.1.call-done = bf16[2048,5120]{1,0:T(8,128)(2,1)} async-done(((bf16[16,5120]{1,0:T(8,128)(2,1)}), bf16[2048,5120]{1,0:T(8,128)(2,1)}) %all-gather.5.cloned.1.call-update) | async-done | bytes 20971536 | tf_op jit(solution)/shard_map/all_gather | solution.py:110
  178.2 11.6 %fusion.48 = f32[256,2048]{1,0:T(8,128)} fusion(bf16[256,5120]{1,0:T(8,128)(2,1)} %reshape.178, bf16[2048,5120]{1,0:T(8,128)(2,1)} %all-gather.5.cloned.1.call-done), kind=kOutput, calls=%fused_computation.85 | convolution fusion | flops 5368709120 | bytes 25690112 | tf_op jit(solution)/shard_map/dot_general | solution.py:27
  189.9 1.9 copy.27
  191.8 0.2 reshape.180
  192.0 0.2 add_convert_fusion.1
  192.3 0.6 fusion.20
  192.9 0.1 slice.43
  193.0 0.1 fusion.28
  193.1 0.3 concatenate.21
  193.5 0.7 pad_maximum_fusion
  194.2 29.9 %all_to_all.5 = bf16[128,4,1408]{2,1,0:T(4,128)(2,1)S(1)} all-to-all(bf16[128,4,1408]{2,1,0:T(4,128)(2,1)S(1)} %pad_maximum_fusion), channel_id=1, replica_groups=mesh['fsdp'=8,'dp'=16] {'fsdp','dp'}, dimensions={0} | all-to-all | bytes 2883584 | tf_op jit(solution)/shard_map/all_to_all | solution.py:175
  224.1 0.3 reshape.181
  224.4 0.1 convert_reduce_fusion.2
  224.6 1.4 convolution_convert_fusion.2
  (22 shorter events, 0.2 us)
Async XLA Ops:
  6.5 10.8 %copy-start = (bf16[1024,1280]{1,0:T(8,128)(2,1)S(1)}, bf16[1024,1280]{1,0:T(8,128)(2,1)}, u32[]{:S(2)}) copy-start(bf16[1024,1280]{1,0:T(8,128)(2,1)} %param.14) | copy-start | bytes 7864324
  6.5 82.0 %all-gather.3.cloned.1.call-start = ((), (), s32[]{:S(2)}) async-start(), calls=%async_computation.1 | async-start | bytes 13209600 | tf_op jit(solution)/shard_map/all_gather | solution.py:106
  8.3 170.0 %all-gather.5.cloned.1.call-start = ((), (), s32[]{:S(2)}) async-start(), calls=%async_computation.2 | async-start | bytes 21135360 | tf_op jit(solution)/shard_map/all_gather | solution.py:110
  88.6 10.7 %copy-start.4 = (f32[3840]{0:T(1024)S(1)}, f32[3840]{0:T(1024)}, u32[]{:S(2)}) copy-start(f32[3840]{0:T(1024)} %param.19) | copy-start | bytes 46084
  88.6 10.7 %copy-start.5 = (f32[1280]{0:T(1024)S(1)}, f32[1280]{0:T(1024)}, u32[]{:S(2)}) copy-start(f32[1280]{0:T(1024)} %param.17) | copy-start | bytes 15364
  88.6 10.7 %copy-start.6 = (f32[1280]{0:T(1024)S(1)}, f32[1280]{0:T(1024)}, u32[]{:S(2)}) copy-start(f32[1280]{0:T(1024)} %param.16) | copy-start | bytes 15364
  151.2 8.6 %copy-start.7 = (f32[1280]{0:T(1024)S(1)}, f32[1280]{0:T(1024)}, u32[]{:S(2)}) copy-start(f32[1280]{0:T(1024)} %param.21) | copy-start | bytes 15364
  151.2 8.6 %copy-start.8 = (bf16[1280,1024]{1,0:T(8,128)(2,1)S(1)}, bf16[1280,1024]{1,0:T(8,128)(2,1)}, u32[]{:S(2)}) copy-start(bf16[1280,1024]{1,0:T(8,128)(2,1)} %shard_map.136) | copy-start | bytes 7864324
  159.8 5.3 %copy-start.1 = (f32[1280]{0:T(1024)S(1)}, f32[1280]{0:T(1024)}, u32[]{:S(2)}) copy-start(f32[1280]{0:T(1024)} %param.23) | copy-start | bytes 15364
  159.8 5.3 %copy-start.2 = (f32[1280]{0:T(1024)S(1)}, f32[1280]{0:T(1024)}, u32[]{:S(2)}) copy-start(f32[1280]{0:T(1024)} %param.22) | copy-start | bytes 15364
  189.9 2.1 copy-start.3
Sparse Core Ops, SparseCore 0:
  10.3 78.1 all-gather.2
  91.5 86.6 all-gather.4

commit v10 on v9

--- a/solution.py
+++ b/solution.py
@@ -162,30 +162,24 @@
     earlier = jnp.cumsum(matches, axis=0) - matches
     rank = jnp.sum(earlier * matches, axis=1)
     position = dest_device * capacity + rank
-    lanes = 128
-    slot_block = jnp.broadcast_to(dest_slot.astype(jnp.bfloat16)[:, None], (row_count, lanes))
-    payload = jnp.concatenate([projected, slot_block], axis=1)
     place = (
         position[None, :] == jnp.arange(count_dev * capacity, dtype=jnp.int32)[:, None]
     ).astype(jnp.bfloat16)
-    rows_out = jnp.dot(place, payload, preferred_element_type=jnp.float32)
-    empty = (jnp.sum(place, axis=1, keepdims=True) == 0)
-    slot_lane = jnp.where(empty, float(row_count), rows_out[:, width:])
-    rows_out = jnp.concatenate([rows_out[:, :width], slot_lane], axis=1).astype(jnp.bfloat16)
+    empty = jnp.sum(place, axis=1) == 0
+    slot_sent = jnp.where(
+        empty, row_count, jnp.sum(place.astype(jnp.int32) * dest_slot[None, :], axis=1)
+    )
+    got_slots = lax.all_to_all(
+        slot_sent.reshape(count_dev, capacity), axes, split_axis=0, concat_axis=0, tiled=True
+    ).reshape(-1)
+    rows_out = jnp.dot(place, projected, preferred_element_type=jnp.float32).astype(jnp.bfloat16)
     got = lax.all_to_all(
-        rows_out.reshape(count_dev, capacity, width + lanes),
-        axes,
-        split_axis=0,
-        concat_axis=0,
-        tiled=True,
-    ).reshape(count_dev * capacity, width + lanes)
-    got_slots = got[:, width].astype(jnp.int32)
+        rows_out.reshape(count_dev, capacity, width), axes, split_axis=0, concat_axis=0, tiled=True
+    ).reshape(count_dev * capacity, width)
     pick = (
         got_slots[None, :] == jnp.arange(row_count, dtype=jnp.int32)[:, None]
     ).astype(jnp.bfloat16)
-    requests = jnp.dot(pick, got[:, :width], preferred_element_type=jnp.float32).astype(
-        jnp.bfloat16
-    )
+    requests = jnp.dot(pick, got, preferred_element_type=jnp.float32).astype(jnp.bfloat16)
     return requests
 
 

time: 233 us -> 232 us (level)
  blocking collectives: 29.9 us -> 0 us
  starting transfers between devices: 0.04 us -> 18.8 us
  waiting for transfers between devices: 79.6 us -> 87.3 us
    all_to_all x1 -> x0, blocking collectives: 29.9 us -> none  [per_device(): lax.all_to_all(rows_out.reshape(count_dev, capacity, width + lanes), axes...]
    all_to_all x0 -> x2, waiting for transfers between devices: none -> 19.9 us  [the longest x1 19.9 us: per_device(): lax.all_to_all(rows_out.reshape(count_dev, capacity, width), axes, split_...]
    all_to_all x0 -> x2, starting transfers between devices: none -> 18.8 us  [the longest x1 11.5 us: per_device(): lax.all_to_all(slot_sent.reshape(count_dev, capacity), axes, split_axis=0...]
    all_gather x1, waiting for transfers between devices: 70.4 us -> 58 us  [per_device(): first_parts = lax.all_gather(first, axes, axis=0, tiled=True)]
  transfers between devices with their start and end apart: 2 -> 4, of which waited for: 2 -> 3; matrix products, arithmetic and copies ran while one was open for 22% -> 30% of each run, Pallas kernels for 16% -> 17%
where the time goes in v10:
time: 232 us; the launch traced here: 231 us
  waiting for transfers between devices  87.3 us (38%)
  matrix products  50.6 us (22%)
  Pallas kernels  38.4 us (17%)
  starting transfers between devices  18.8 us (8%)
  between operations  13.6 us (6%)
  local copies, waits for them, and re-layouts  12.1 us (5%)
  other arithmetic  10.2 us (4%)
    all_gather x1, waiting for transfers between devices, per_device(): first_parts = lax.all_gather(first, axes, axis=0, tiled=True)  58 us
    pallas_call x1, Pallas kernels, attention(): pl.pallas_call(functools.partial(attention_kernel, scale), out_shape=jax....  38.4 us
    all_to_all x1, waiting for transfers between devices, per_device(): lax.all_to_all(rows_out.reshape(count_dev, capacity, width), axes, split_...  19.9 us
    dot_general x2, matrix products, pick(): jnp.einsum('ij,bjk->bik', selector(rows, offset), blocks, preferred_eleme...  19.2 us
    dot_general x1, matrix products, per_device(): lax.dot_general(qkv_full, normed, (((1,), (1,)), ((), ())), preferred_ele...  13.5 us
    dot_general x1, matrix products, times_rows(): lax.dot_general(left, piece, (((1,), (1,)), ((), ())), preferred_element_...  11.6 us
    all_to_all x1, starting transfers between devices, per_device(): lax.all_to_all(slot_sent.reshape(count_dev, capacity), axes, split_axis=0...  11.5 us
    all_gather x1, waiting for transfers between devices, per_device(): merge_parts = lax.all_gather(merge_padded, axes, axis=0, tiled=True)  9.38 us
  transfers between devices with their start and end apart: 4, of which 3 were waited for; matrix products, arithmetic and copies ran while one was open for 30% of the time, Pallas kernels for 17%

profile of v10, /device:TPU:1, one launch (start us, length us, event | category | flops | bytes accessed | tf_op | source)
XLA Modules:
  0.0 231.1 jit_solution(3986210016806654054)
XLA Ops:
  6.5 0.0 all-gather.3.cloned.1.call-start
  6.5 1.7 pad_maximum_fusion
  8.2 0.0 all-gather.3.cloned.1.call-update
  8.3 0.0 all-gather.5.cloned.1.call-start
  8.3 1.6 concatenate.7
  9.9 0.0 all-gather.5.cloned.1.call-update
  9.9 0.8 copy.24
  10.7 0.2 fusion.27
  11.0 0.9 fusion.29
  11.9 0.7 multiply_add_fusion
  12.6 0.2 fusion.21
  12.7 0.9 multiply_reduce_fusion
  13.6 0.7 select_n.59
  14.3 11.5 %all-to-all-start = ((s32[128,1,4]{2,1,0:T(1,128)}), s32[128,1,4]{2,1,0:T(1,128)S(1)}, u32[]{:S(2)}, u32[]{:S(2)}) async-start(s32[128,1,4]{2,1,0:T(1,128)} %bitcast.4), calls=%async_computation | async-start | bytes 131072 | tf_op jit(solution)/shard_map/all_to_all | solution.py:172
  25.8 1.7 copy.27.qid_ref
  27.6 2.2 convert_reduce_fusion
  29.8 0.0 copy-done
  29.8 0.8 fusion.4
  30.6 58.0 %all-gather.3.cloned.1.call-done = bf16[5120,1280]{1,0:T(8,128)(2,1)} async-done(((bf16[40,1280]{1,0:T(8,128)(2,1)}), bf16[5120,1280]{1,0:T(8,128)(2,1)}) %all-gather.3.cloned.1.call-update) | async-done | bytes 13107216 | tf_op jit(solution)/shard_map/all_gather | solution.py:106
  88.6 10.7 %convolution_convert_fusion = bf16[16,1280,240]{1,2,0:T(8,128)(2,1)S(1)} fusion(bf16[16,320,1280]{2,1,0:T(8,128)(2,1)} %bitcast.42, s32[240]{0:T(256)S(1)} %fusion.37), kind=kOutput, calls=%fused_computation.1 | convolution fusion | flops 3150720000 | bytes 22938560 | tf_op jit(solution)/shard_map/ij,bjk->bik/dot_general | solution.py:122
  99.3 0.0 copy-done.4
  99.3 0.0 copy-done.5
  99.3 0.0 copy-done.6
  99.3 13.5 %add_convert_fusion.q_ref.k_ref.v_ref = bf16[3840,1024]{1,0:T(8,128)(2,1)} fusion(bf16[3840,1280]{1,0:T(8,128)(2,1)S(1)} %bitcast.44, f32[3840]{0:T(1024)S(1)} %copy-done.4, bf16[1024,1280]{1,0:T(8,128)(2,1)S(1)} %copy-done, f32[1280]{0:T(1024)S(1)} %copy-done.5, f32[1280]{0:T(1024)S(1)} %copy-done.6, f32[1024]{0:T(1024)S(1)} %add_rsqrt_fusion.1, ...), kind=kOutput, calls=%fused_computation | convolution fusion | flops 10082058240 | bytes 20349952 | tf_op jit(solution)/shard_map/dot_general | solution.py:132
  112.8 38.4 %shard_map.136 = bf16[1280,1024]{1,0:T(8,128)(2,1)} custom-call(bf16[3840,1024]{1,0:T(8,128)(2,1)} %add_convert_fusion.q_ref.k_ref.v_ref, bf16[3840,1024]{1,0:T(8,128)(2,1)} %add_convert_fusion.q_ref.k_ref.v_ref, bf16[3840,1024]{1,0:T(8,128)(2,1)} %add_convert_fusion.q_ref.k_ref.v_ref, s32[1024,1]{1,0:T(8,128)} %copy.27.qid_ref, s32[1,1024]{1,0:T(1,128)} %bitcast.52), custom_call_target="tpu_custom_call" | custom-call | flops 5368709120 | bytes 10485760 | tf_op jit(solution)/shard_map/pallas_call | solution.py:63
  151.2 8.6 %convolution_convert_fusion.1 = bf16[16,1280,80]{1,2,0:T(8,128)(2,1)S(1)} fusion(bf16[16,320,1280]{2,1,0:T(8,128)(2,1)} %bitcast.43, s32[80]{0:T(128)S(1)} %fusion.39), kind=kOutput, calls=%fused_computation.21 | convolution fusion | flops 1050240000 | bytes 16384320 | tf_op jit(solution)/shard_map/ij,bjk->bik/dot_general | solution.py:122
  159.8 0.0 copy-start.1
  159.8 0.0 copy-start.2
  159.8 4.2 %convert_reduce_fusion.1 = (f32[1024]{0:T(1024)S(1)}, bf16[1024,1280]{1,0:T(8,128)(2,1)S(1)}) fusion(f32[1280]{0:T(1024)S(1)} %copy-done.7, bf16[1280,1024]{1,0:T(8,128)(2,1)S(1)} %copy-done.8, bf16[1280,1280]{1,0:T(8,128)(2,1)S(1)} %bitcast.46, bf16[1024,1280]{1,0:T(8,128)(2,1)S(1)} %copy-done), kind=kOutput, calls=%fused_computation.6 | convolution fusion | flops 3363306496 | bytes 11150336 | tf_op jit(solution)/shard_map/dot_general | solution.py:139
  164.0 0.8 fusion.8
  164.9 0.0 copy-done.1
  164.9 0.0 copy-done.2
  164.9 1.0 fusion.11
  165.9 2.9 %reshape.194 = bf16[256,5120]{1,0:T(8,128)(2,1)} reshape(bf16[1024,1280]{1,0:T(8,128)(2,1)S(1)} %fusion.11) | data formatting | bytes 5242880 | tf_op jit(solution)/shard_map/reshape | solution.py:148
  168.9 9.4 %all-gather.5.cloned.1.call-done = bf16[2048,5120]{1,0:T(8,128)(2,1)} async-done(((bf16[16,5120]{1,0:T(8,128)(2,1)}), bf16[2048,5120]{1,0:T(8,128)(2,1)}) %all-gather.5.cloned.1.call-update) | async-done | bytes 20971536 | tf_op jit(solution)/shard_map/all_gather | solution.py:110
  178.2 11.6 %fusion.42 = f32[256,2048]{1,0:T(8,128)} fusion(bf16[256,5120]{1,0:T(8,128)(2,1)} %reshape.194, bf16[2048,5120]{1,0:T(8,128)(2,1)} %all-gather.5.cloned.1.call-done), kind=kOutput, calls=%fused_computation.77 | convolution fusion | flops 5368709120 | bytes 25690112 | tf_op jit(solution)/shard_map/dot_general | solution.py:27
  189.9 1.9 copy.28
  191.8 0.2 reshape.196
  192.0 0.6 convolution_convert_fusion.2
  192.7 1.2 reshape.197
  193.9 0.0 all-to-all-done
  193.9 7.3 %all-to-all-start.1 = ((bf16[128,4,1280]{2,1,0:T(4,128)(2,1)}), bf16[128,4,1280]{2,1,0:T(4,128)(2,1)S(1)}, u32[]{:S(2)}, u32[]{:S(2)}) async-start(bf16[128,4,1280]{2,1,0:T(4,128)(2,1)} %reshape.197), calls=%async_computation.1 | async-start | bytes 2621440 | tf_op jit(solution)/shard_map/all_to_all | solution.py:176
  201.2 0.5 broadcast.200
  201.7 0.8 reduce.4
  202.5 0.1 eq.108
  202.6 19.9 %all-to-all-done.1 = bf16[128,4,1280]{2,1,0:T(4,128)(2,1)S(1)} async-done(((bf16[128,4,1280]{2,1,0:T(4,128)(2,1)}), bf16[128,4,1280]{2,1,0:T(4,128)(2,1)S(1)}, u32[]{:S(2)}, u32[]{:S(2)}) %all-to-all-start.1) | async-done | bytes 1310752 | tf_op jit(solution)/shard_map/all_to_all | solution.py:176
  222.6 0.3 reshape.198
  222.9 1.3 convolution_convert_fusion.3
  (23 shorter events, 0.1 us)
Async XLA Ops:
  6.5 23.2 %copy-start = (bf16[1024,1280]{1,0:T(8,128)(2,1)S(1)}, bf16[1024,1280]{1,0:T(8,128)(2,1)}, u32[]{:S(2)}) copy-start(bf16[1024,1280]{1,0:T(8,128)(2,1)} %param.14) | copy-start | bytes 7864324
  6.5 82.0 %all-gather.3.cloned.1.call-start = ((), (), s32[]{:S(2)}) async-start(), calls=%async_computation.2 | async-start | bytes 13209600 | tf_op jit(solution)/shard_map/all_gather | solution.py:106
  8.3 170.0 %all-gather.5.cloned.1.call-start = ((), (), s32[]{:S(2)}) async-start(), calls=%async_computation.3 | async-start | bytes 21135360 | tf_op jit(solution)/shard_map/all_gather | solution.py:110
  14.3 179.6 %all-to-all-start = ((s32[128,1,4]{2,1,0:T(1,128)}), s32[128,1,4]{2,1,0:T(1,128)S(1)}, u32[]{:S(2)}, u32[]{:S(2)}) async-start(s32[128,1,4]{2,1,0:T(1,128)} %bitcast.4), calls=%async_computation | async-start | bytes 131072 | tf_op jit(solution)/shard_map/all_to_all | solution.py:172
  88.6 10.7 %copy-start.4 = (f32[3840]{0:T(1024)S(1)}, f32[3840]{0:T(1024)}, u32[]{:S(2)}) copy-start(f32[3840]{0:T(1024)} %param.19) | copy-start | bytes 46084
  88.6 10.7 %copy-start.5 = (f32[1280]{0:T(1024)S(1)}, f32[1280]{0:T(1024)}, u32[]{:S(2)}) copy-start(f32[1280]{0:T(1024)} %param.17) | copy-start | bytes 15364
  88.6 10.7 %copy-start.6 = (f32[1280]{0:T(1024)S(1)}, f32[1280]{0:T(1024)}, u32[]{:S(2)}) copy-start(f32[1280]{0:T(1024)} %param.16) | copy-start | bytes 15364
  151.2 8.6 %copy-start.7 = (f32[1280]{0:T(1024)S(1)}, f32[1280]{0:T(1024)}, u32[]{:S(2)}) copy-start(f32[1280]{0:T(1024)} %param.21) | copy-start | bytes 15364
  151.2 8.6 %copy-start.8 = (bf16[1280,1024]{1,0:T(8,128)(2,1)S(1)}, bf16[1280,1024]{1,0:T(8,128)(2,1)}, u32[]{:S(2)}) copy-start(bf16[1280,1024]{1,0:T(8,128)(2,1)} %shard_map.136) | copy-start | bytes 7864324
  159.8 5.1 %copy-start.1 = (f32[1280]{0:T(1024)S(1)}, f32[1280]{0:T(1024)}, u32[]{:S(2)}) copy-start(f32[1280]{0:T(1024)} %param.23) | copy-start | bytes 15364
  159.8 5.1 %copy-start.2 = (f32[1280]{0:T(1024)S(1)}, f32[1280]{0:T(1024)}, u32[]{:S(2)}) copy-start(f32[1280]{0:T(1024)} %param.22) | copy-start | bytes 15364
  189.9 2.1 copy-start.3
  193.9 28.7 %all-to-all-start.1 = ((bf16[128,4,1280]{2,1,0:T(4,128)(2,1)}), bf16[128,4,1280]{2,1,0:T(4,128)(2,1)S(1)}, u32[]{:S(2)}, u32[]{:S(2)}) async-start(bf16[128,4,1280]{2,1,0:T(4,128)(2,1)} %reshape.197), calls=%async_computation.1 | async-start | bytes 2621440 | tf_op jit(solution)/shard_map/all_to_all | solution.py:176
Sparse Core Ops, SparseCore 0:
  10.3 78.1 all-gather.2
  91.5 86.6 all-gather.4

commit v11 on v10

--- a/solution.py
+++ b/solution.py
@@ -99,15 +99,16 @@
     qkv_rows = qkv_weight.shape[0]
     out_rows = out_weight.shape[0]
     merge_rows = merge_weight.shape[0]
-    tile_rows = 16
-    wide = 4 * width
-    first = jnp.concatenate([qkv_weight, out_weight], axis=0)
+    merge_head = (merge_rows // 8) * 8
+    merge_tail = merge_rows - merge_head
+    pieces = 4
+    tail_rows = merge_tail * pieces
+    first = jnp.concatenate(
+        [qkv_weight, out_weight, merge_weight[merge_head:].reshape(tail_rows, width)], axis=0
+    )
     first_rows = first.shape[0]
     first_parts = lax.all_gather(first, axes, axis=0, tiled=True)
-    merge_padded = jnp.concatenate(
-        [merge_weight, jnp.zeros((tile_rows - merge_rows, wide), merge_weight.dtype)], axis=0
-    )
-    merge_parts = lax.all_gather(merge_padded, axes, axis=0, tiled=True)
+    merge_full = lax.all_gather(merge_weight[:merge_head], axes, axis=0, tiled=True)
     devices = first_parts.shape[0] // first_rows
     group = 8
     blocks = first_parts.reshape(devices // group, group * first_rows, width)
@@ -126,7 +127,19 @@
 
     qkv_full = pick(qkv_rows, 0)
     out_full = pick(out_rows, qkv_rows)
-    merge_full = merge_parts
+    piece = lax.broadcasted_iota(jnp.int32, (pieces, group * merge_tail, 1), 0)
+    local = lax.broadcasted_iota(jnp.int32, (pieces, group * merge_tail, 1), 1)
+    wanted = (
+        (local // merge_tail) * first_rows
+        + qkv_rows
+        + out_rows
+        + pieces * (local % merge_tail)
+        + piece
+    )
+    tail_select = (wanted == source[None]).astype(first_parts.dtype)
+    tail_full = jnp.einsum(
+        "jis,bsk->jbik", tail_select, blocks, preferred_element_type=jnp.float32
+    ).astype(first_parts.dtype).reshape(pieces, devices * merge_tail, width)
 
     normed = layer_norm(patch_states, first_gain, first_shift).astype(jnp.bfloat16)
     joined_t = lax.dot_general(
@@ -147,9 +160,18 @@
         .astype(jnp.bfloat16)
         .reshape(tokens // 4, 4 * width)
     )
-    projected_padded = lax.optimization_barrier(times_rows(merged, merge_full))
-    projected = projected_padded.reshape(tokens // 4, devices, tile_rows)[:, :, :merge_rows]
-    projected = (projected.reshape(tokens // 4, width) + merge_bias).astype(jnp.bfloat16)
+    head_part = lax.optimization_barrier(times_rows(merged, merge_full))
+    head_part = head_part.reshape(tokens // 4, devices, merge_head)
+    tail_part = lax.optimization_barrier(
+        jnp.einsum(
+            "mjc,joc->mo",
+            merged.reshape(tokens // 4, pieces, width),
+            tail_full,
+            preferred_element_type=jnp.float32,
+        )
+    ).reshape(tokens // 4, devices, merge_tail)
+    projected = jnp.concatenate([head_part, tail_part], axis=2).reshape(tokens // 4, width)
+    projected = (projected + merge_bias).astype(jnp.bfloat16)
 
     fsdp_count = lax.axis_size("fsdp")
     dp_count = lax.axis_size("dp")

time: 232 us -> 237 us (1.022)
  waiting for transfers between devices: 87.3 us -> 80.7 us
  matrix products: 50.6 us -> 56.9 us
  local copies, waits for them, and re-layouts: 12.1 us -> 16.9 us
    all_gather x1, waiting for transfers between devices: 9.38 us -> 0.02 us  [per_device(): lax.all_gather(merge_weight[:merge_head], axes, axis=0, tiled=True)]
    dot_general x0 -> x2, matrix products: none -> 9.08 us  [the longest x1 8.21 us: per_device(): jnp.einsum('jis,bsk->jbik', tail_select, blocks, preferred_element_type=j...]
    dot_general x1, matrix products: 11.6 us -> 7.87 us  [times_rows(): lax.dot_general(left, piece, (((1,), (1,)), ((), ())), preferred_element_...]
    all_gather x1, waiting for transfers between devices: 58 us -> 60.7 us  [per_device(): first_parts = lax.all_gather(first, axes, axis=0, tiled=True)]
    slice x0 -> x2, local copies, waits for them, and re-layouts: none -> 2.58 us  [the longest x1 1.53 us: per_device(): merge_weight[:merge_head]]
  transfers between devices with their start and end apart: 4 -> 4, of which waited for: 3 -> 2; matrix products, arithmetic and copies ran while one was open for 30% -> 33% of each run, Pallas kernels for 17% -> 16%
where the time goes in v11:
time: 237 us; the launch traced here: 236 us
  waiting for transfers between devices  80.7 us (34%)
  matrix products  56.9 us (24%)
  Pallas kernels  38.4 us (16%)
  starting transfers between devices  19 us (8%)
  local copies, waits for them, and re-layouts  16.9 us (7%)
  between operations  13.8 us (6%)
  other arithmetic  10.3 us (4%)
    all_gather x1, waiting for transfers between devices, per_device(): first_parts = lax.all_gather(first, axes, axis=0, tiled=True)  60.7 us
    pallas_call x1, Pallas kernels, attention(): pl.pallas_call(functools.partial(attention_kernel, scale), out_shape=jax....  38.4 us
    dot_general x2, matrix products, pick(): jnp.einsum('ij,bjk->bik', selector(rows, offset), blocks, preferred_eleme...  20.5 us
    all_to_all x1, waiting for transfers between devices, per_device(): lax.all_to_all(rows_out.reshape(count_dev, capacity, width), axes, split_...  19.9 us
    dot_general x1, matrix products, per_device(): lax.dot_general(qkv_full, normed, (((1,), (1,)), ((), ())), preferred_ele...  13.3 us
    all_to_all x1, starting transfers between devices, per_device(): lax.all_to_all(slot_sent.reshape(count_dev, capacity), axes, split_axis=0...  11.5 us
    dot_general x1, matrix products, per_device(): jnp.einsum('jis,bsk->jbik', tail_select, blocks, preferred_element_type=j...  8.21 us
    dot_general x1, matrix products, times_rows(): lax.dot_general(left, piece, (((1,), (1,)), ((), ())), preferred_element_...  7.87 us
  transfers between devices with their start and end apart: 4, of which 2 were waited for; matrix products, arithmetic and copies ran while one was open for 33% of the time, Pallas kernels for 16%

profile of v11, /device:TPU:1, one launch (start us, length us, event | category | flops | bytes accessed | tf_op | source)
XLA Modules:
  0.0 236.0 jit_solution(7091486672481228641)
XLA Ops:
  6.5 1.0 slice.14
  7.6 1.6 pad_maximum_fusion.1
  9.2 0.0 all-gather.3.cloned.1.call-update
  9.2 0.0 all-gather.5.cloned.1.call-start
  9.3 1.5 slice.15
  10.8 0.0 all-gather.5.cloned.1.call-update
  10.8 0.8 copy.31
  11.6 0.2 fusion.33
  11.9 0.9 fusion.35
  12.8 0.7 multiply_add_fusion
  13.5 0.2 fusion.29
  13.6 0.9 multiply_reduce_fusion
  14.5 0.7 select_n.80
  15.2 11.5 %all-to-all-start = ((s32[128,1,4]{2,1,0:T(1,128)}), s32[128,1,4]{2,1,0:T(1,128)S(1)}, u32[]{:S(2)}, u32[]{:S(2)}) async-start(s32[128,1,4]{2,1,0:T(1,128)} %bitcast.4), calls=%async_computation | async-start | bytes 131072 | tf_op jit(solution)/shard_map/all_to_all | solution.py:194
  26.7 1.7 copy.34.qid_ref
  28.5 2.2 convert_reduce_fusion
  30.7 0.8 fusion.4
  31.6 60.7 %all-gather.3.cloned.1.call-done = bf16[6144,1280]{1,0:T(8,128)(2,1)} async-done(((bf16[48,1280]{1,0:T(8,128)(2,1)}), bf16[6144,1280]{1,0:T(8,128)(2,1)}) %all-gather.3.cloned.1.call-update) | async-done | bytes 15728656 | tf_op jit(solution)/shard_map/all_gather | solution.py:110
  92.2 11.2 %convolution_convert_fusion = bf16[16,1280,240]{1,2,0:T(8,128)(2,1)S(1)} fusion(bf16[16,384,1280]{2,1,0:T(8,128)(2,1)} %bitcast.57, s32[240]{0:T(256)S(1)} %fusion.46), kind=kOutput, calls=%fused_computation.1 | convolution fusion | flops 3779880960 | bytes 25560000 | tf_op jit(solution)/shard_map/ij,bjk->bik/dot_general | solution.py:123
  103.5 13.3 %add_convert_fusion.q_ref.k_ref.v_ref = bf16[3840,1024]{1,0:T(8,128)(2,1)} fusion(bf16[3840,1280]{1,0:T(8,128)(2,1)S(1)} %bitcast.60, f32[3840]{0:T(1024)S(1)} %copy-done.6, bf16[1024,1280]{1,0:T(8,128)(2,1)S(1)} %copy-done, f32[1280]{0:T(1024)S(1)} %copy-done.7, f32[1280]{0:T(1024)S(1)} %copy-done.8, f32[1024]{0:T(1024)S(1)} %add_rsqrt_fusion.1, ...), kind=kOutput, calls=%fused_computation | convolution fusion | flops 10082058240 | bytes 20349952 | tf_op jit(solution)/shard_map/dot_general | solution.py:145
  116.9 38.4 %shard_map.136 = bf16[1280,1024]{1,0:T(8,128)(2,1)} custom-call(bf16[3840,1024]{1,0:T(8,128)(2,1)} %add_convert_fusion.q_ref.k_ref.v_ref, bf16[3840,1024]{1,0:T(8,128)(2,1)} %add_convert_fusion.q_ref.k_ref.v_ref, bf16[3840,1024]{1,0:T(8,128)(2,1)} %add_convert_fusion.q_ref.k_ref.v_ref, s32[1024,1]{1,0:T(8,128)} %copy.34.qid_ref, s32[1,1024]{1,0:T(1,128)} %bitcast.69), custom_call_target="tpu_custom_call" | custom-call | flops 5368709120 | bytes 10485760 | tf_op jit(solution)/shard_map/pallas_call | solution.py:63
  155.3 9.3 %convolution_convert_fusion.1 = bf16[16,1280,80]{1,2,0:T(8,128)(2,1)S(1)} fusion(bf16[16,384,1280]{2,1,0:T(8,128)(2,1)} %bitcast.58, s32[80]{0:T(128)S(1)} %fusion.48), kind=kOutput, calls=%fused_computation.21 | convolution fusion | flops 1259960320 | bytes 19005760 | tf_op jit(solution)/shard_map/ij,bjk->bik/dot_general | solution.py:123
  164.6 0.0 copy-start.3
  164.6 4.1 %convert_reduce_fusion.1 = (f32[1024]{0:T(1024)S(1)}, bf16[1024,1280]{1,0:T(8,128)(2,1)S(1)}) fusion(f32[1280]{0:T(1024)S(1)} %copy-done.9, bf16[1280,1024]{1,0:T(8,128)(2,1)S(1)} %copy-done.10, bf16[1280,1280]{1,0:T(8,128)(2,1)S(1)} %bitcast.61, bf16[1024,1280]{1,0:T(8,128)(2,1)S(1)} %copy-done), kind=kOutput, calls=%fused_computation.6 | convolution fusion | flops 3363306496 | bytes 11150336 | tf_op jit(solution)/shard_map/dot_general | solution.py:152
  168.7 0.8 fusion.8
  169.6 1.0 fusion.11
  170.6 2.3 reshape_reshape.3
  172.9 2.9 %reshape.286 = bf16[256,5120]{1,0:T(8,128)(2,1)} reshape(bf16[1024,1280]{1,0:T(8,128)(2,1)S(1)} %fusion.11) | data formatting | bytes 5242880 | tf_op jit(solution)/shard_map/reshape | solution.py:161
  175.8 8.2 %fusion.14 = bf16[4,16,16,1280]{3,2,0,1:T(8,128)(2,1)S(1)} fusion(bf16[16,384,1280,1]{2,1,3,0:T(8,128)(2,1)} %bitcast.59, s32[4,16]{1,0:T(4,128)S(1)} %iota_add_fusion), kind=kOutput, calls=%fused_computation.23 | convolution fusion | flops 1007968256 | bytes 18350336 | tf_op jit(solution)/shard_map/jis,bsk->jbik/dot_general | solution.py:140
  184.0 0.2 copy.36
  184.2 1.5 copy-done.2
  185.7 0.9 fusion.22
  186.6 0.1 copy.38
  186.7 0.1 reshape.289
  186.9 0.0 all-gather.5.cloned.1.call-done
  186.9 7.9 %fusion.51 = f32[256,1024]{1,0:T(8,128)} fusion(bf16[256,5120]{1,0:T(8,128)(2,1)S(1)} %copy-done.1, bf16[1024,5120]{1,0:T(8,128)(2,1)} %all-gather.5.cloned.1.call-done), kind=kOutput, calls=%fused_computation.94 | convolution fusion | flops 2684354560 | bytes 14155776 | tf_op jit(solution)/shard_map/dot_general | solution.py:27
  194.8 1.6 copy.35
  196.4 0.2 pad_maximum_fusion
  196.6 0.2 reshape.290
  196.8 0.6 convolution_convert_fusion.3
  197.4 1.2 reshape.291
  198.6 7.5 %all-to-all-start.1 = ((bf16[128,4,1280]{2,1,0:T(4,128)(2,1)}), bf16[128,4,1280]{2,1,0:T(4,128)(2,1)S(1)}, u32[]{:S(2)}, u32[]{:S(2)}) async-start(bf16[128,4,1280]{2,1,0:T(4,128)(2,1)} %reshape.291), calls=%async_computation.1 | async-start | bytes 2621440 | tf_op jit(solution)/shard_map/all_to_all | solution.py:198
  206.1 0.5 broadcast.308
  206.6 0.8 reduce.4
  207.4 0.1 eq.123
  207.5 19.9 %all-to-all-done.1 = bf16[128,4,1280]{2,1,0:T(4,128)(2,1)S(1)} async-done(((bf16[128,4,1280]{2,1,0:T(4,128)(2,1)}), bf16[128,4,1280]{2,1,0:T(4,128)(2,1)S(1)}, u32[]{:S(2)}, u32[]{:S(2)}) %all-to-all-start.1) | async-done | bytes 1310752 | tf_op jit(solution)/shard_map/all_to_all | solution.py:198
  227.5 0.3 reshape.292
  227.8 1.4 convolution_convert_fusion.4
  (40 shorter events, 0.2 us)
Async XLA Ops:
  6.5 24.2 %copy-start = (bf16[1024,1280]{1,0:T(8,128)(2,1)S(1)}, bf16[1024,1280]{1,0:T(8,128)(2,1)}, u32[]{:S(2)}) copy-start(bf16[1024,1280]{1,0:T(8,128)(2,1)} %param.14) | copy-start | bytes 7864324
  6.5 85.7 %all-gather.3.cloned.1.call-start = ((), (), s32[]{:S(2)}) async-start(), calls=%async_computation.2 | async-start | bytes 15851520 | tf_op jit(solution)/shard_map/all_gather | solution.py:110
  9.2 177.7 %all-gather.5.cloned.1.call-start = ((), (), s32[]{:S(2)}) async-start(), calls=%async_computation.3 | async-start | bytes 10567680 | tf_op jit(solution)/shard_map/all_gather | solution.py:111
  15.2 183.4 %all-to-all-start = ((s32[128,1,4]{2,1,0:T(1,128)}), s32[128,1,4]{2,1,0:T(1,128)S(1)}, u32[]{:S(2)}, u32[]{:S(2)}) async-start(s32[128,1,4]{2,1,0:T(1,128)} %bitcast.4), calls=%async_computation | async-start | bytes 131072 | tf_op jit(solution)/shard_map/all_to_all | solution.py:194
  92.2 11.3 %copy-start.6 = (f32[3840]{0:T(1024)S(1)}, f32[3840]{0:T(1024)}, u32[]{:S(2)}) copy-start(f32[3840]{0:T(1024)} %param.19) | copy-start | bytes 46084
  92.2 11.3 %copy-start.7 = (f32[1280]{0:T(1024)S(1)}, f32[1280]{0:T(1024)}, u32[]{:S(2)}) copy-start(f32[1280]{0:T(1024)} %param.17) | copy-start | bytes 15364
  92.2 11.3 %copy-start.8 = (f32[1280]{0:T(1024)S(1)}, f32[1280]{0:T(1024)}, u32[]{:S(2)}) copy-start(f32[1280]{0:T(1024)} %param.16) | copy-start | bytes 15364
  155.3 9.3 %copy-start.9 = (f32[1280]{0:T(1024)S(1)}, f32[1280]{0:T(1024)}, u32[]{:S(2)}) copy-start(f32[1280]{0:T(1024)} %param.21) | copy-start | bytes 15364
  155.3 9.3 %copy-start.10 = (bf16[1280,1024]{1,0:T(8,128)(2,1)S(1)}, bf16[1280,1024]{1,0:T(8,128)(2,1)}, u32[]{:S(2)}) copy-start(bf16[1280,1024]{1,0:T(8,128)(2,1)} %shard_map.136) | copy-start | bytes 7864324
  164.6 5.0 %copy-start.3 = (f32[1280]{0:T(1024)S(1)}, f32[1280]{0:T(1024)}, u32[]{:S(2)}) copy-start(f32[1280]{0:T(1024)} %param.23) | copy-start | bytes 15364
  164.6 5.0 %copy-start.4 = (f32[1280]{0:T(1024)S(1)}, f32[1280]{0:T(1024)}, u32[]{:S(2)}) copy-start(f32[1280]{0:T(1024)} %param.22) | copy-start | bytes 15364
  184.0 1.7 copy-start.2
  184.0 2.9 %copy-start.1 = (bf16[256,5120]{1,0:T(8,128)(2,1)S(1)}, bf16[256,5120]{1,0:T(8,128)(2,1)}, u32[]{:S(2)}) copy-start(bf16[256,5120]{1,0:T(8,128)(2,1)} %reshape.286) | copy-start | bytes 7864324
  194.8 2.0 copy-start.5
  198.6 28.8 %all-to-all-start.1 = ((bf16[128,4,1280]{2,1,0:T(4,128)(2,1)}), bf16[128,4,1280]{2,1,0:T(4,128)(2,1)S(1)}, u32[]{:S(2)}, u32[]{:S(2)}) async-start(bf16[128,4,1280]{2,1,0:T(4,128)(2,1)} %reshape.291), calls=%async_computation.1 | async-start | bytes 2621440 | tf_op jit(solution)/shard_map/all_to_all | solution.py:198
Sparse Core Ops, SparseCore 0:
  10.2 81.9 all-gather.2
  95.4 71.0 all-gather.4

commit v12 on v10

--- a/solution.py
+++ b/solution.py
@@ -148,8 +148,18 @@
         .reshape(tokens // 4, 4 * width)
     )
     projected_padded = lax.optimization_barrier(times_rows(merged, merge_full))
-    projected = projected_padded.reshape(tokens // 4, devices, tile_rows)[:, :, :merge_rows]
-    projected = (projected.reshape(tokens // 4, width) + merge_bias).astype(jnp.bfloat16)
+    bias_padded = jnp.pad(
+        merge_bias.reshape(devices, merge_rows), ((0, 0), (0, tile_rows - merge_rows))
+    ).reshape(-1)
+    projected_padded = (projected_padded + bias_padded).astype(jnp.bfloat16)
+    column = lax.broadcasted_iota(jnp.int32, (1, width), 1)
+    padded_column = lax.broadcasted_iota(jnp.int32, (devices * tile_rows, 1), 0)
+    keep = (
+        padded_column == (column // merge_rows) * tile_rows + column % merge_rows
+    ).astype(jnp.bfloat16)
+    projected = jnp.dot(projected_padded, keep, preferred_element_type=jnp.float32).astype(
+        jnp.bfloat16
+    )
 
     fsdp_count = lax.axis_size("fsdp")
     dp_count = lax.axis_size("dp")

time: 232 us -> 233 us (level)
  matrix products: 50.6 us -> 54.3 us
    dot_general x1, matrix products: 0.61 us -> 4.37 us  [per_device(): jnp.dot(place, projected, preferred_element_type=jnp.float32)]
  transfers between devices with their start and end apart: 4 -> 4, of which waited for: 3 -> 3; matrix products, arithmetic and copies ran while one was open for 30% -> 31% of each run, Pallas kernels for 17% -> 17%
where the time goes in v12:
time: 233 us; the launch traced here: 232 us
  waiting for transfers between devices  86.1 us (37%)
  matrix products  54.3 us (23%)
  Pallas kernels  38.4 us (16%)
  starting transfers between devices  18.8 us (8%)
  between operations  13.6 us (6%)
  local copies, waits for them, and re-layouts  10.9 us (5%)
  other arithmetic  10.3 us (4%)
    all_gather x1, waiting for transfers between devices, per_device(): first_parts = lax.all_gather(first, axes, axis=0, tiled=True)  57 us
    pallas_call x1, Pallas kernels, attention(): pl.pallas_call(functools.partial(attention_kernel, scale), out_shape=jax....  38.4 us
    all_to_all x1, waiting for transfers between devices, per_device(): lax.all_to_all(rows_out.reshape(count_dev, capacity, width), axes, split_...  19.9 us
    dot_general x2, matrix products, pick(): jnp.einsum('ij,bjk->bik', selector(rows, offset), blocks, preferred_eleme...  19.2 us
    dot_general x1, matrix products, per_device(): lax.dot_general(qkv_full, normed, (((1,), (1,)), ((), ())), preferred_ele...  13.5 us
    dot_general x1, matrix products, times_rows(): lax.dot_general(left, piece, (((1,), (1,)), ((), ())), preferred_element_...  11.6 us
    all_to_all x1, starting transfers between devices, per_device(): lax.all_to_all(slot_sent.reshape(count_dev, capacity), axes, split_axis=0...  11.5 us
    all_gather x1, waiting for transfers between devices, per_device(): merge_parts = lax.all_gather(merge_padded, axes, axis=0, tiled=True)  9.14 us
  transfers between devices with their start and end apart: 4, of which 3 were waited for; matrix products, arithmetic and copies ran while one was open for 31% of the time, Pallas kernels for 17%

profile of v12, /device:TPU:1, one launch (start us, length us, event | category | flops | bytes accessed | tf_op | source)
XLA Modules:
  0.0 232.4 jit_solution(10496855227081456544)
XLA Ops:
  6.5 0.0 all-gather.3.cloned.1.call-start
  6.5 1.7 pad_maximum_fusion
  8.2 0.0 all-gather.3.cloned.1.call-update
  8.3 0.0 all-gather.5.cloned.1.call-start
  8.3 1.6 concatenate.7
  9.9 0.0 all-gather.5.cloned.1.call-update
  9.9 0.8 copy.22
  10.7 0.2 fusion.31
  11.0 0.9 fusion.33
  11.9 0.7 multiply_add_fusion
  12.6 0.2 fusion.25
  12.7 0.9 multiply_reduce_fusion
  13.6 0.7 select_n.80
  14.3 11.5 %all-to-all-start = ((s32[128,1,4]{2,1,0:T(1,128)}), s32[128,1,4]{2,1,0:T(1,128)S(1)}, u32[]{:S(2)}, u32[]{:S(2)}) async-start(s32[128,1,4]{2,1,0:T(1,128)} %bitcast.4), calls=%async_computation | async-start | bytes 131072 | tf_op jit(solution)/shard_map/all_to_all | solution.py:182
  25.8 1.7 copy.25.qid_ref
  27.6 0.8 reshape.230
  28.4 0.1 add.172
  28.5 2.2 convert_reduce_fusion
  30.7 0.0 copy-done
  30.7 0.8 fusion.5
  31.6 57.0 %all-gather.3.cloned.1.call-done = bf16[5120,1280]{1,0:T(8,128)(2,1)} async-done(((bf16[40,1280]{1,0:T(8,128)(2,1)}), bf16[5120,1280]{1,0:T(8,128)(2,1)}) %all-gather.3.cloned.1.call-update) | async-done | bytes 13107216 | tf_op jit(solution)/shard_map/all_gather | solution.py:106
  88.6 10.7 %convolution_convert_fusion = bf16[16,1280,240]{1,2,0:T(8,128)(2,1)S(1)} fusion(bf16[16,320,1280]{2,1,0:T(8,128)(2,1)} %bitcast.38, s32[240]{0:T(256)S(1)} %fusion.50), kind=kOutput, calls=%fused_computation.1 | convolution fusion | flops 3150720000 | bytes 22938560 | tf_op jit(solution)/shard_map/ij,bjk->bik/dot_general | solution.py:122
  99.3 0.0 copy-done.3
  99.3 13.5 %add_convert_fusion.q_ref.k_ref.v_ref = bf16[3840,1024]{1,0:T(8,128)(2,1)} fusion(bf16[3840,1280]{1,0:T(8,128)(2,1)S(1)} %bitcast.40, f32[3840]{0:T(1024)S(1)} %copy-done.3, bf16[1024,1280]{1,0:T(8,128)(2,1)S(1)} %copy-done, f32[1280]{0:T(1024)S(1)} %copy-done.4, f32[1280]{0:T(1024)S(1)} %copy-done.5, f32[1024]{0:T(1024)S(1)} %add_rsqrt_fusion.1, ...), kind=kOutput, calls=%fused_computation | convolution fusion | flops 10082058240 | bytes 20349952 | tf_op jit(solution)/shard_map/dot_general | solution.py:132
  112.8 38.4 %shard_map.136 = bf16[1280,1024]{1,0:T(8,128)(2,1)} custom-call(bf16[3840,1024]{1,0:T(8,128)(2,1)} %add_convert_fusion.q_ref.k_ref.v_ref, bf16[3840,1024]{1,0:T(8,128)(2,1)} %add_convert_fusion.q_ref.k_ref.v_ref, bf16[3840,1024]{1,0:T(8,128)(2,1)} %add_convert_fusion.q_ref.k_ref.v_ref, s32[1024,1]{1,0:T(8,128)} %copy.25.qid_ref, s32[1,1024]{1,0:T(1,128)} %bitcast.47), custom_call_target="tpu_custom_call" | custom-call | flops 5368709120 | bytes 10485760 | tf_op jit(solution)/shard_map/pallas_call | solution.py:63
  151.2 8.6 %convolution_convert_fusion.1 = bf16[16,1280,80]{1,2,0:T(8,128)(2,1)S(1)} fusion(bf16[16,320,1280]{2,1,0:T(8,128)(2,1)} %bitcast.39, s32[80]{0:T(128)S(1)} %fusion.52), kind=kOutput, calls=%fused_computation.24 | convolution fusion | flops 1050240000 | bytes 16384320 | tf_op jit(solution)/shard_map/ij,bjk->bik/dot_general | solution.py:122
  159.7 0.0 copy-done.6
  159.8 0.0 copy-done.7
  159.8 0.0 copy-start.1
  159.8 0.0 copy-start.2
  159.8 4.2 %convert_reduce_fusion.1 = (f32[1024]{0:T(1024)S(1)}, bf16[1024,1280]{1,0:T(8,128)(2,1)S(1)}) fusion(f32[1280]{0:T(1024)S(1)} %copy-done.6, bf16[1280,1024]{1,0:T(8,128)(2,1)S(1)} %copy-done.7, bf16[1280,1280]{1,0:T(8,128)(2,1)S(1)} %bitcast.41, bf16[1024,1280]{1,0:T(8,128)(2,1)S(1)} %copy-done), kind=kOutput, calls=%fused_computation.8 | convolution fusion | flops 3363306496 | bytes 11150336 | tf_op jit(solution)/shard_map/dot_general | solution.py:139
  164.0 0.8 fusion.9
  164.9 0.0 copy-done.1
  164.9 0.0 copy-done.2
  164.9 1.0 fusion.12
  165.9 2.9 %reshape.229 = bf16[256,5120]{1,0:T(8,128)(2,1)} reshape(bf16[1024,1280]{1,0:T(8,128)(2,1)S(1)} %fusion.12) | data formatting | bytes 5242880 | tf_op jit(solution)/shard_map/reshape | solution.py:148
  168.8 9.1 %all-gather.5.cloned.1.call-done = bf16[2048,5120]{1,0:T(8,128)(2,1)} async-done(((bf16[16,5120]{1,0:T(8,128)(2,1)}), bf16[2048,5120]{1,0:T(8,128)(2,1)}) %all-gather.5.cloned.1.call-update) | async-done | bytes 20971536 | tf_op jit(solution)/shard_map/all_gather | solution.py:110
  178.0 11.6 %fusion.55 = f32[256,2048]{1,0:T(8,128)} fusion(bf16[256,5120]{1,0:T(8,128)(2,1)} %reshape.229, bf16[2048,5120]{1,0:T(8,128)(2,1)} %all-gather.5.cloned.1.call-done), kind=kOutput, calls=%fused_computation.94 | convolution fusion | flops 5368709120 | bytes 25690112 | tf_op jit(solution)/shard_map/dot_general | solution.py:27
  189.6 4.4 %convolution_convert_fusion.2 = bf16[512,1280]{1,0:T(8,128)(2,1)S(1)} fusion(s32[1280]{0:T(1024)S(1)} %fusion.46, f32[256,2048]{1,0:T(8,128)} %fusion.55, f32[2048]{0:T(1024)S(1)} %add.172, s32[256]{0:T(256)S(1)} %multiply_add_fusion), kind=kOutput, calls=%fused_computation.25 | convolution fusion | flops 1682505728 | bytes 3422208 | tf_op jit(solution)/shard_map/dot_general | solution.py:185
  194.0 1.2 reshape.231
  195.2 0.0 all-to-all-done
  195.2 7.3 %all-to-all-start.1 = ((bf16[128,4,1280]{2,1,0:T(4,128)(2,1)}), bf16[128,4,1280]{2,1,0:T(4,128)(2,1)S(1)}, u32[]{:S(2)}, u32[]{:S(2)}) async-start(bf16[128,4,1280]{2,1,0:T(4,128)(2,1)} %reshape.231), calls=%async_computation.1 | async-start | bytes 2621440 | tf_op jit(solution)/shard_map/all_to_all | solution.py:186
  202.5 0.5 broadcast.248
  203.1 0.8 reduce.4
  203.9 0.1 eq.123
  204.0 19.9 %all-to-all-done.1 = bf16[128,4,1280]{2,1,0:T(4,128)(2,1)S(1)} async-done(((bf16[128,4,1280]{2,1,0:T(4,128)(2,1)}), bf16[128,4,1280]{2,1,0:T(4,128)(2,1)S(1)}, u32[]{:S(2)}, u32[]{:S(2)}) %all-to-all-start.1) | async-done | bytes 1310752 | tf_op jit(solution)/shard_map/all_to_all | solution.py:186
  223.9 0.3 reshape.232
  224.2 1.4 convolution_convert_fusion.3
  (23 shorter events, 0.2 us)
Async XLA Ops:
  6.5 24.2 %copy-start = (bf16[1024,1280]{1,0:T(8,128)(2,1)S(1)}, bf16[1024,1280]{1,0:T(8,128)(2,1)}, u32[]{:S(2)}) copy-start(bf16[1024,1280]{1,0:T(8,128)(2,1)} %param.14) | copy-start | bytes 7864324
  6.5 82.0 %all-gather.3.cloned.1.call-start = ((), (), s32[]{:S(2)}) async-start(), calls=%async_computation.2 | async-start | bytes 13209600 | tf_op jit(solution)/shard_map/all_gather | solution.py:106
  8.3 169.7 %all-gather.5.cloned.1.call-start = ((), (), s32[]{:S(2)}) async-start(), calls=%async_computation.3 | async-start | bytes 21135360 | tf_op jit(solution)/shard_map/all_gather | solution.py:110
  14.3 180.9 %all-to-all-start = ((s32[128,1,4]{2,1,0:T(1,128)}), s32[128,1,4]{2,1,0:T(1,128)S(1)}, u32[]{:S(2)}, u32[]{:S(2)}) async-start(s32[128,1,4]{2,1,0:T(1,128)} %bitcast.4), calls=%async_computation | async-start | bytes 131072 | tf_op jit(solution)/shard_map/all_to_all | solution.py:182
  88.6 10.7 %copy-start.3 = (f32[3840]{0:T(1024)S(1)}, f32[3840]{0:T(1024)}, u32[]{:S(2)}) copy-start(f32[3840]{0:T(1024)} %param.19) | copy-start | bytes 46084
  88.6 10.7 %copy-start.4 = (f32[1280]{0:T(1024)S(1)}, f32[1280]{0:T(1024)}, u32[]{:S(2)}) copy-start(f32[1280]{0:T(1024)} %param.17) | copy-start | bytes 15364
  88.6 10.7 %copy-start.5 = (f32[1280]{0:T(1024)S(1)}, f32[1280]{0:T(1024)}, u32[]{:S(2)}) copy-start(f32[1280]{0:T(1024)} %param.16) | copy-start | bytes 15364
  151.2 8.6 %copy-start.6 = (f32[1280]{0:T(1024)S(1)}, f32[1280]{0:T(1024)}, u32[]{:S(2)}) copy-start(f32[1280]{0:T(1024)} %param.21) | copy-start | bytes 15364
  151.2 8.6 %copy-start.7 = (bf16[1280,1024]{1,0:T(8,128)(2,1)S(1)}, bf16[1280,1024]{1,0:T(8,128)(2,1)}, u32[]{:S(2)}) copy-start(bf16[1280,1024]{1,0:T(8,128)(2,1)} %shard_map.136) | copy-start | bytes 7864324
  159.8 5.1 %copy-start.1 = (f32[1280]{0:T(1024)S(1)}, f32[1280]{0:T(1024)}, u32[]{:S(2)}) copy-start(f32[1280]{0:T(1024)} %param.23) | copy-start | bytes 15364
  159.8 5.1 %copy-start.2 = (f32[1280]{0:T(1024)S(1)}, f32[1280]{0:T(1024)}, u32[]{:S(2)}) copy-start(f32[1280]{0:T(1024)} %param.22) | copy-start | bytes 15364
  195.2 28.7 %all-to-all-start.1 = ((bf16[128,4,1280]{2,1,0:T(4,128)(2,1)}), bf16[128,4,1280]{2,1,0:T(4,128)(2,1)S(1)}, u32[]{:S(2)}, u32[]{:S(2)}) async-start(bf16[128,4,1280]{2,1,0:T(4,128)(2,1)} %reshape.231), calls=%async_computation.1 | async-start | bytes 2621440 | tf_op jit(solution)/shard_map/all_to_all | solution.py:186
Sparse Core Ops, SparseCore 0:
  10.3 78.1 all-gather.2
  91.5 86.3 all-gather.4

commit v13 on v10

--- a/solution.py
+++ b/solution.py
@@ -147,10 +147,6 @@
         .astype(jnp.bfloat16)
         .reshape(tokens // 4, 4 * width)
     )
-    projected_padded = lax.optimization_barrier(times_rows(merged, merge_full))
-    projected = projected_padded.reshape(tokens // 4, devices, tile_rows)[:, :, :merge_rows]
-    projected = (projected.reshape(tokens // 4, width) + merge_bias).astype(jnp.bfloat16)
-
     fsdp_count = lax.axis_size("fsdp")
     dp_count = lax.axis_size("dp")
     count_dev = fsdp_count * dp_count
@@ -172,10 +168,31 @@
     got_slots = lax.all_to_all(
         slot_sent.reshape(count_dev, capacity), axes, split_axis=0, concat_axis=0, tiled=True
     ).reshape(-1)
-    rows_out = jnp.dot(place, projected, preferred_element_type=jnp.float32).astype(jnp.bfloat16)
-    got = lax.all_to_all(
-        rows_out.reshape(count_dev, capacity, width), axes, split_axis=0, concat_axis=0, tiled=True
-    ).reshape(count_dev * capacity, width)
+    halves = 2
+    half_rows = devices * tile_rows // halves
+    half_width = width // halves
+    results = []
+    for half in range(halves):
+        padded = lax.optimization_barrier(
+            times_rows(merged, merge_full[half * half_rows : (half + 1) * half_rows])
+        )
+        projected = padded.reshape(tokens // 4, devices // halves, tile_rows)[:, :, :merge_rows]
+        projected = (
+            projected.reshape(tokens // 4, half_width)
+            + merge_bias[half * half_width : (half + 1) * half_width]
+        ).astype(jnp.bfloat16)
+        rows_out = jnp.dot(place, projected, preferred_element_type=jnp.float32).astype(
+            jnp.bfloat16
+        )
+        got = lax.all_to_all(
+            rows_out.reshape(count_dev, capacity, half_width),
+            axes,
+            split_axis=0,
+            concat_axis=0,
+            tiled=True,
+        ).reshape(count_dev * capacity, half_width)
+        results.append(got)
+    got = jnp.concatenate(results, axis=1)
     pick = (
         got_slots[None, :] == jnp.arange(row_count, dtype=jnp.int32)[:, None]
     ).astype(jnp.bfloat16)

time: 232 us -> 240 us (1.034)
  starting transfers between devices: 18.8 us -> 25 us
  matrix products: 50.6 us -> 54.4 us
  waiting for transfers between devices: 87.3 us -> 84.6 us
    all_to_all x1 -> x2, starting transfers between devices: 7.3 us -> 13.4 us  [per_device(): lax.all_to_all(rows_out.reshape(count_dev, capacity, half_width), axes, s...]
    dot_general x1 -> x2, matrix products: 11.6 us -> 15.1 us  [times_rows(): lax.dot_general(left, piece, (((1,), (1,)), ((), ())), preferred_element_...]
    all_to_all x1 -> x2, waiting for transfers between devices: 19.9 us -> 17.3 us  [per_device(): lax.all_to_all(rows_out.reshape(count_dev, capacity, half_width), axes, s...]
  transfers between devices with their start and end apart: 4 -> 5, of which waited for: 3 -> 4; matrix products, arithmetic and copies ran while one was open for 30% -> 31% of each run, Pallas kernels for 17% -> 16%
where the time goes in v13:
time: 240 us; the launch traced here: 239 us
  waiting for transfers between devices  84.6 us (35%)
  matrix products  54.4 us (23%)
  Pallas kernels  38.4 us (16%)
  starting transfers between devices  25 us (10%)
  between operations  13.7 us (6%)
  local copies, waits for them, and re-layouts  12.9 us (5%)
  other arithmetic  10.3 us (4%)
    all_gather x1, waiting for transfers between devices, per_device(): first_parts = lax.all_gather(first, axes, axis=0, tiled=True)  57.9 us
    pallas_call x1, Pallas kernels, attention(): pl.pallas_call(functools.partial(attention_kernel, scale), out_shape=jax....  38.4 us
    dot_general x2, matrix products, pick(): jnp.einsum('ij,bjk->bik', selector(rows, offset), blocks, preferred_eleme...  19.2 us
    all_to_all x2, waiting for transfers between devices, per_device(): lax.all_to_all(rows_out.reshape(count_dev, capacity, half_width), axes, s...  17.3 us
    dot_general x2, matrix products, times_rows(): lax.dot_general(left, piece, (((1,), (1,)), ((), ())), preferred_element_...  15.1 us
    dot_general x1, matrix products, per_device(): lax.dot_general(qkv_full, normed, (((1,), (1,)), ((), ())), preferred_ele...  13.5 us
    all_to_all x2, starting transfers between devices, per_device(): lax.all_to_all(rows_out.reshape(count_dev, capacity, half_width), axes, s...  13.4 us
    all_to_all x1, starting transfers between devices, per_device(): lax.all_to_all(slot_sent.reshape(count_dev, capacity), axes, split_axis=0...  11.5 us
  transfers between devices with their start and end apart: 5, of which 4 were waited for; matrix products, arithmetic and copies ran while one was open for 31% of the time, Pallas kernels for 16%

profile of v13, /device:TPU:1, one launch (start us, length us, event | category | flops | bytes accessed | tf_op | source)
XLA Modules:
  0.0 239.3 jit_solution(1989294874222703157)
XLA Ops:
  6.5 1.7 pad_maximum_fusion
  8.3 0.0 all-gather.3.cloned.1.call-update
  8.3 0.0 all-gather.5.cloned.1.call-start
  8.3 1.6 concatenate.10
  9.9 0.0 all-gather.5.cloned.1.call-update
  9.9 0.8 copy.26
  10.7 0.2 fusion.36
  11.0 0.9 fusion.38
  11.9 0.7 multiply_add_fusion
  12.6 0.2 fusion.27
  12.7 0.9 multiply_reduce_fusion
  13.6 0.7 select_n.59
  14.3 11.5 %all-to-all-start = ((s32[128,1,4]{2,1,0:T(1,128)}), s32[128,1,4]{2,1,0:T(1,128)S(1)}, u32[]{:S(2)}, u32[]{:S(2)}) async-start(s32[128,1,4]{2,1,0:T(1,128)} %bitcast.4), calls=%async_computation | async-start | bytes 131072 | tf_op jit(solution)/shard_map/all_to_all | solution.py:168
  25.8 1.7 copy.29.qid_ref
  27.6 2.2 convert_reduce_fusion
  29.8 0.8 fusion.8
  30.6 57.9 %all-gather.3.cloned.1.call-done = bf16[5120,1280]{1,0:T(8,128)(2,1)} async-done(((bf16[40,1280]{1,0:T(8,128)(2,1)}), bf16[5120,1280]{1,0:T(8,128)(2,1)}) %all-gather.3.cloned.1.call-update) | async-done | bytes 13107216 | tf_op jit(solution)/shard_map/all_gather | solution.py:106
  88.6 10.7 %convolution_convert_fusion = bf16[16,1280,240]{1,2,0:T(8,128)(2,1)S(1)} fusion(bf16[16,320,1280]{2,1,0:T(8,128)(2,1)} %bitcast.45, s32[240]{0:T(256)S(1)} %fusion.46), kind=kOutput, calls=%fused_computation.1 | convolution fusion | flops 3150720000 | bytes 22938560 | tf_op jit(solution)/shard_map/ij,bjk->bik/dot_general | solution.py:122
  99.3 13.5 %add_convert_fusion.q_ref.k_ref.v_ref = bf16[3840,1024]{1,0:T(8,128)(2,1)} fusion(bf16[3840,1280]{1,0:T(8,128)(2,1)S(1)} %bitcast.47, f32[3840]{0:T(1024)S(1)} %copy-done.4, bf16[1024,1280]{1,0:T(8,128)(2,1)S(1)} %copy-done, f32[1280]{0:T(1024)S(1)} %copy-done.5, f32[1280]{0:T(1024)S(1)} %copy-done.6, f32[1024]{0:T(1024)S(1)} %add_rsqrt_fusion.1, ...), kind=kOutput, calls=%fused_computation | convolution fusion | flops 10082058240 | bytes 20349952 | tf_op jit(solution)/shard_map/dot_general | solution.py:132
  112.8 38.4 %shard_map.136 = bf16[1280,1024]{1,0:T(8,128)(2,1)} custom-call(bf16[3840,1024]{1,0:T(8,128)(2,1)} %add_convert_fusion.q_ref.k_ref.v_ref, bf16[3840,1024]{1,0:T(8,128)(2,1)} %add_convert_fusion.q_ref.k_ref.v_ref, bf16[3840,1024]{1,0:T(8,128)(2,1)} %add_convert_fusion.q_ref.k_ref.v_ref, s32[1024,1]{1,0:T(8,128)} %copy.29.qid_ref, s32[1,1024]{1,0:T(1,128)} %bitcast.56), custom_call_target="tpu_custom_call" | custom-call | flops 5368709120 | bytes 10485760 | tf_op jit(solution)/shard_map/pallas_call | solution.py:63
  151.2 8.6 %convolution_convert_fusion.1 = bf16[16,1280,80]{1,2,0:T(8,128)(2,1)S(1)} fusion(bf16[16,320,1280]{2,1,0:T(8,128)(2,1)} %bitcast.46, s32[80]{0:T(128)S(1)} %fusion.48), kind=kOutput, calls=%fused_computation.25 | convolution fusion | flops 1050240000 | bytes 16384320 | tf_op jit(solution)/shard_map/ij,bjk->bik/dot_general | solution.py:122
  159.8 0.0 copy-start.1
  159.8 0.0 copy-start.2
  159.8 4.2 %convert_reduce_fusion.1 = (f32[1024]{0:T(1024)S(1)}, bf16[1024,1280]{1,0:T(8,128)(2,1)S(1)}) fusion(f32[1280]{0:T(1024)S(1)} %copy-done.7, bf16[1280,1024]{1,0:T(8,128)(2,1)S(1)} %copy-done.8, bf16[1280,1280]{1,0:T(8,128)(2,1)S(1)} %bitcast.48, bf16[1024,1280]{1,0:T(8,128)(2,1)S(1)} %copy-done), kind=kOutput, calls=%fused_computation.10 | convolution fusion | flops 3363306496 | bytes 11150336 | tf_op jit(solution)/shard_map/dot_general | solution.py:139
  164.0 0.8 fusion.12
  164.9 1.0 fusion.15
  165.9 2.9 %reshape.207 = bf16[256,5120]{1,0:T(8,128)(2,1)} reshape(bf16[1024,1280]{1,0:T(8,128)(2,1)S(1)} %fusion.15) | data formatting | bytes 5242880 | tf_op jit(solution)/shard_map/reshape | solution.py:148
  168.8 9.4 %all-gather.5.cloned.1.call-done = bf16[2048,5120]{1,0:T(8,128)(2,1)} async-done(((bf16[16,5120]{1,0:T(8,128)(2,1)}), bf16[2048,5120]{1,0:T(8,128)(2,1)}) %all-gather.5.cloned.1.call-update) | async-done | bytes 20971536 | tf_op jit(solution)/shard_map/all_gather | solution.py:110
  178.2 6.5 %fusion.2 = f32[256,1024]{1,0:T(8,128)S(1)} fusion(bf16[256,5120]{1,0:T(8,128)(2,1)} %reshape.207, bf16[2048,5120]{1,0:T(8,128)(2,1)} %all-gather.5.cloned.1.call-done), kind=kOutput, calls=%fused_computation.4 | convolution fusion | flops 2684354560 | bytes 14155776 | tf_op jit(solution)/shard_map/dot_general | solution.py:27
  184.7 0.3 copy.30
  185.0 0.1 reshape.209
  185.1 0.5 convolution_convert_fusion.4
  185.6 1.0 reshape.210
  186.7 7.3 %all-to-all-start.1 = ((bf16[128,4,640]{2,1,0:T(4,128)(2,1)}), bf16[128,4,640]{2,1,0:T(4,128)(2,1)S(1)}, u32[]{:S(2)}, u32[]{:S(2)}) async-start(bf16[128,4,640]{2,1,0:T(4,128)(2,1)} %reshape.210), calls=%async_computation.1 | async-start | bytes 1310720 | tf_op jit(solution)/shard_map/all_to_all | solution.py:187
  194.0 8.6 %fusion = f32[256,1024]{1,0:T(8,128)} fusion(bf16[256,5120]{1,0:T(8,128)(2,1)} %reshape.207, bf16[2048,5120]{1,0:T(8,128)(2,1)} %all-gather.5.cloned.1.call-done), kind=kOutput, calls=%fused_computation.2 | convolution fusion | flops 2684354560 | bytes 14155776 | tf_op jit(solution)/shard_map/dot_general | solution.py:27
  202.6 1.6 copy.31
  204.2 0.1 reshape.213
  204.3 0.5 convolution_convert_fusion.3
  204.8 1.0 reshape.214
  205.8 3.6 %all-to-all-done.1 = bf16[128,4,640]{2,1,0:T(4,128)(2,1)S(1)} async-done(((bf16[128,4,640]{2,1,0:T(4,128)(2,1)}), bf16[128,4,640]{2,1,0:T(4,128)(2,1)S(1)}, u32[]{:S(2)}, u32[]{:S(2)}) %all-to-all-start.1) | async-done | bytes 655392 | tf_op jit(solution)/shard_map/all_to_all | solution.py:187
  209.4 6.2 %all-to-all-start.2 = ((bf16[128,4,640]{2,1,0:T(4,128)(2,1)}), bf16[128,4,640]{2,1,0:T(4,128)(2,1)S(1)}, u32[]{:S(2)}, u32[]{:S(2)}) async-start(bf16[128,4,640]{2,1,0:T(4,128)(2,1)} %reshape.214), calls=%async_computation.2 | async-start | bytes 1310720 | tf_op jit(solution)/shard_map/all_to_all | solution.py:187
  215.5 0.6 broadcast.201
  216.1 0.8 reduce.4
  217.0 0.1 eq.108
  217.1 0.2 reshape.211
  217.2 13.7 %all-to-all-done.2 = bf16[128,4,640]{2,1,0:T(4,128)(2,1)S(1)} async-done(((bf16[128,4,640]{2,1,0:T(4,128)(2,1)}), bf16[128,4,640]{2,1,0:T(4,128)(2,1)S(1)}, u32[]{:S(2)}, u32[]{:S(2)}) %all-to-all-start.2) | async-done | bytes 655392 | tf_op jit(solution)/shard_map/all_to_all | solution.py:187
  230.9 0.1 reshape.215
  231.1 1.3 convolution_convert_fusion.2
  (32 shorter events, 0.2 us)
Async XLA Ops:
  6.5 23.2 %copy-start = (bf16[1024,1280]{1,0:T(8,128)(2,1)S(1)}, bf16[1024,1280]{1,0:T(8,128)(2,1)}, u32[]{:S(2)}) copy-start(bf16[1024,1280]{1,0:T(8,128)(2,1)} %param.14) | copy-start | bytes 7864324
  6.5 24.1 %copy-start.3 = (f32[1280]{0:T(1024)S(1)}, f32[1280]{0:T(1024)}, u32[]{:S(2)}) copy-start(f32[1280]{0:T(1024)} %param.25) | copy-start | bytes 15364
  6.5 82.0 %all-gather.3.cloned.1.call-start = ((), (), s32[]{:S(2)}) async-start(), calls=%async_computation.3 | async-start | bytes 13209600 | tf_op jit(solution)/shard_map/all_gather | solution.py:106
  8.3 170.0 %all-gather.5.cloned.1.call-start = ((), (), s32[]{:S(2)}) async-start(), calls=%async_computation.4 | async-start | bytes 21135360 | tf_op jit(solution)/shard_map/all_gather | solution.py:110
  14.3 172.3 %all-to-all-start = ((s32[128,1,4]{2,1,0:T(1,128)}), s32[128,1,4]{2,1,0:T(1,128)S(1)}, u32[]{:S(2)}, u32[]{:S(2)}) async-start(s32[128,1,4]{2,1,0:T(1,128)} %bitcast.4), calls=%async_computation | async-start | bytes 131072 | tf_op jit(solution)/shard_map/all_to_all | solution.py:168
  88.6 10.7 %copy-start.4 = (f32[3840]{0:T(1024)S(1)}, f32[3840]{0:T(1024)}, u32[]{:S(2)}) copy-start(f32[3840]{0:T(1024)} %param.19) | copy-start | bytes 46084
  88.6 10.7 %copy-start.5 = (f32[1280]{0:T(1024)S(1)}, f32[1280]{0:T(1024)}, u32[]{:S(2)}) copy-start(f32[1280]{0:T(1024)} %param.17) | copy-start | bytes 15364
  88.6 10.7 %copy-start.6 = (f32[1280]{0:T(1024)S(1)}, f32[1280]{0:T(1024)}, u32[]{:S(2)}) copy-start(f32[1280]{0:T(1024)} %param.16) | copy-start | bytes 15364
  151.2 8.6 %copy-start.7 = (f32[1280]{0:T(1024)S(1)}, f32[1280]{0:T(1024)}, u32[]{:S(2)}) copy-start(f32[1280]{0:T(1024)} %param.21) | copy-start | bytes 15364
  151.2 8.6 %copy-start.8 = (bf16[1280,1024]{1,0:T(8,128)(2,1)S(1)}, bf16[1280,1024]{1,0:T(8,128)(2,1)}, u32[]{:S(2)}) copy-start(bf16[1280,1024]{1,0:T(8,128)(2,1)} %shard_map.136) | copy-start | bytes 7864324
  159.8 5.1 %copy-start.1 = (f32[1280]{0:T(1024)S(1)}, f32[1280]{0:T(1024)}, u32[]{:S(2)}) copy-start(f32[1280]{0:T(1024)} %param.23) | copy-start | bytes 15364
  159.8 5.1 %copy-start.2 = (f32[1280]{0:T(1024)S(1)}, f32[1280]{0:T(1024)}, u32[]{:S(2)}) copy-start(f32[1280]{0:T(1024)} %param.22) | copy-start | bytes 15364
  186.7 22.7 %all-to-all-start.1 = ((bf16[128,4,640]{2,1,0:T(4,128)(2,1)}), bf16[128,4,640]{2,1,0:T(4,128)(2,1)S(1)}, u32[]{:S(2)}, u32[]{:S(2)}) async-start(bf16[128,4,640]{2,1,0:T(4,128)(2,1)} %reshape.210), calls=%async_computation.1 | async-start | bytes 1310720 | tf_op jit(solution)/shard_map/all_to_all | solution.py:187
  209.4 21.6 %all-to-all-start.2 = ((bf16[128,4,640]{2,1,0:T(4,128)(2,1)}), bf16[128,4,640]{2,1,0:T(4,128)(2,1)S(1)}, u32[]{:S(2)}, u32[]{:S(2)}) async-start(bf16[128,4,640]{2,1,0:T(4,128)(2,1)} %reshape.214), calls=%async_computation.2 | async-start | bytes 1310720 | tf_op jit(solution)/shard_map/all_to_all | solution.py:187
Sparse Core Ops, SparseCore 0:
  10.3 78.1 all-gather.2
  91.5 86.6 all-gather.4

commit v14 on v10

--- a/solution.py
+++ b/solution.py
@@ -147,9 +147,11 @@
         .astype(jnp.bfloat16)
         .reshape(tokens // 4, 4 * width)
     )
-    projected_padded = lax.optimization_barrier(times_rows(merged, merge_full))
-    projected = projected_padded.reshape(tokens // 4, devices, tile_rows)[:, :, :merge_rows]
-    projected = (projected.reshape(tokens // 4, width) + merge_bias).astype(jnp.bfloat16)
+    projected_padded = lax.optimization_barrier(times_rows(merge_full, merged))
+    projected_t = projected_padded.reshape(devices, tile_rows, tokens // 4)[:, :merge_rows]
+    projected_t = (projected_t.reshape(width, tokens // 4) + merge_bias[:, None]).astype(
+        jnp.bfloat16
+    )
 
     fsdp_count = lax.axis_size("fsdp")
     dp_count = lax.axis_size("dp")
@@ -172,7 +174,7 @@
     got_slots = lax.all_to_all(
         slot_sent.reshape(count_dev, capacity), axes, split_axis=0, concat_axis=0, tiled=True
     ).reshape(-1)
-    rows_out = jnp.dot(place, projected, preferred_element_type=jnp.float32).astype(jnp.bfloat16)
+    rows_out = times_rows(place, projected_t).astype(jnp.bfloat16)
     got = lax.all_to_all(
         rows_out.reshape(count_dev, capacity, width), axes, split_axis=0, concat_axis=0, tiled=True
     ).reshape(count_dev * capacity, width)

time: 232 us -> 231 us (level)
    dot_general x1 -> x2, matrix products: 11.6 us -> 12.3 us  [times_rows(): lax.dot_general(left, piece, (((1,), (1,)), ((), ())), preferred_element_...]
where the time goes in v14:
time: 231 us
  waiting for transfers between devices  87.3 us (38%)
  matrix products  50.6 us (22%)
  Pallas kernels  38.4 us (17%)
  starting transfers between devices  18.8 us (8%)
  between operations  13.6 us (6%)
  local copies, waits for them, and re-layouts  11.6 us (5%)
  other arithmetic  10.2 us (4%)
    all_gather x1, waiting for transfers between devices, per_device(): first_parts = lax.all_gather(first, axes, axis=0, tiled=True)  58 us
    pallas_call x1, Pallas kernels, attention(): pl.pallas_call(functools.partial(attention_kernel, scale), out_shape=jax....  38.4 us
    all_to_all x1, waiting for transfers between devices, per_device(): lax.all_to_all(rows_out.reshape(count_dev, capacity, width), axes, split_...  19.9 us
    dot_general x2, matrix products, pick(): jnp.einsum('ij,bjk->bik', selector(rows, offset), blocks, preferred_eleme...  19.2 us
    dot_general x1, matrix products, per_device(): lax.dot_general(qkv_full, normed, (((1,), (1,)), ((), ())), preferred_ele...  13.5 us
    dot_general x2, matrix products, times_rows(): lax.dot_general(left, piece, (((1,), (1,)), ((), ())), preferred_element_...  12.3 us
    all_to_all x1, starting transfers between devices, per_device(): lax.all_to_all(slot_sent.reshape(count_dev, capacity), axes, split_axis=0...  11.5 us
    all_gather x1, waiting for transfers between devices, per_device(): merge_parts = lax.all_gather(merge_padded, axes, axis=0, tiled=True)  9.37 us
  transfers between devices with their start and end apart: 4, of which 3 were waited for; matrix products, arithmetic and copies ran while one was open for 30% of the time, Pallas kernels for 17%

profile of v14, /device:TPU:1, one launch (start us, length us, event | category | flops | bytes accessed | tf_op | source)
XLA Modules:
  0.0 230.6 jit_solution(17668972917236661783)
XLA Ops:
  6.5 0.0 all-gather.5.cloned.1.call-start
  6.5 1.7 pad_maximum_fusion
  8.2 0.0 all-gather.5.cloned.1.call-update
  8.3 0.0 all-gather.3.cloned.1.call-start
  8.3 1.6 concatenate.6
  9.9 0.0 all-gather.3.cloned.1.call-update
  9.9 0.8 copy.22
  10.7 0.2 fusion.27
  11.0 0.9 fusion.29
  11.9 0.7 multiply_add_fusion
  12.6 0.2 fusion.21
  12.7 0.9 multiply_reduce_fusion
  13.6 0.7 select_n.59
  14.3 11.5 %all-to-all-start = ((s32[128,1,4]{2,1,0:T(1,128)}), s32[128,1,4]{2,1,0:T(1,128)S(1)}, u32[]{:S(2)}, u32[]{:S(2)}) async-start(s32[128,1,4]{2,1,0:T(1,128)} %bitcast.4), calls=%async_computation | async-start | bytes 131072 | tf_op jit(solution)/shard_map/all_to_all | solution.py:174
  25.8 1.7 copy.25.qid_ref
  27.6 2.2 convert_reduce_fusion
  29.8 0.0 copy-done
  29.8 0.8 fusion.4
  30.6 58.0 %all-gather.5.cloned.1.call-done = bf16[5120,1280]{1,0:T(8,128)(2,1)} async-done(((bf16[40,1280]{1,0:T(8,128)(2,1)}), bf16[5120,1280]{1,0:T(8,128)(2,1)}) %all-gather.5.cloned.1.call-update) | async-done | bytes 13107216 | tf_op jit(solution)/shard_map/all_gather | solution.py:106
  88.6 10.7 %convolution_convert_fusion = bf16[16,1280,240]{1,2,0:T(8,128)(2,1)S(1)} fusion(bf16[16,320,1280]{2,1,0:T(8,128)(2,1)} %bitcast.40, s32[240]{0:T(256)S(1)} %fusion.37), kind=kOutput, calls=%fused_computation.1 | convolution fusion | flops 3150720000 | bytes 22938560 | tf_op jit(solution)/shard_map/ij,bjk->bik/dot_general | solution.py:122
  99.3 0.0 copy-done.4
  99.3 0.0 copy-done.5
  99.3 0.0 copy-done.6
  99.3 13.5 %add_convert_fusion.q_ref.k_ref.v_ref = bf16[3840,1024]{1,0:T(8,128)(2,1)} fusion(bf16[3840,1280]{1,0:T(8,128)(2,1)S(1)} %bitcast.42, f32[3840]{0:T(1024)S(1)} %copy-done.4, bf16[1024,1280]{1,0:T(8,128)(2,1)S(1)} %copy-done, f32[1280]{0:T(1024)S(1)} %copy-done.5, f32[1280]{0:T(1024)S(1)} %copy-done.6, f32[1024]{0:T(1024)S(1)} %add_rsqrt_fusion.1, ...), kind=kOutput, calls=%fused_computation | convolution fusion | flops 10082058240 | bytes 20349952 | tf_op jit(solution)/shard_map/dot_general | solution.py:132
  112.8 38.4 %shard_map.136 = bf16[1280,1024]{1,0:T(8,128)(2,1)} custom-call(bf16[3840,1024]{1,0:T(8,128)(2,1)} %add_convert_fusion.q_ref.k_ref.v_ref, bf16[3840,1024]{1,0:T(8,128)(2,1)} %add_convert_fusion.q_ref.k_ref.v_ref, bf16[3840,1024]{1,0:T(8,128)(2,1)} %add_convert_fusion.q_ref.k_ref.v_ref, s32[1024,1]{1,0:T(8,128)} %copy.25.qid_ref, s32[1,1024]{1,0:T(1,128)} %bitcast.50), custom_call_target="tpu_custom_call" | custom-call | flops 5368709120 | bytes 10485760 | tf_op jit(solution)/shard_map/pallas_call | solution.py:63
  151.2 8.6 %convolution_convert_fusion.1 = bf16[16,1280,80]{1,2,0:T(8,128)(2,1)S(1)} fusion(bf16[16,320,1280]{2,1,0:T(8,128)(2,1)} %bitcast.41, s32[80]{0:T(128)S(1)} %fusion.39), kind=kOutput, calls=%fused_computation.21 | convolution fusion | flops 1050240000 | bytes 16384320 | tf_op jit(solution)/shard_map/ij,bjk->bik/dot_general | solution.py:122
  159.7 0.0 copy-done.7
  159.8 0.0 copy-done.8
  159.8 0.0 copy-start.1
  159.8 0.0 copy-start.2
  159.8 4.2 %convert_reduce_fusion.1 = (f32[1024]{0:T(1024)S(1)}, bf16[1024,1280]{1,0:T(8,128)(2,1)S(1)}) fusion(f32[1280]{0:T(1024)S(1)} %copy-done.7, bf16[1280,1024]{1,0:T(8,128)(2,1)S(1)} %copy-done.8, bf16[1280,1280]{1,0:T(8,128)(2,1)S(1)} %bitcast.43, bf16[1024,1280]{1,0:T(8,128)(2,1)S(1)} %copy-done), kind=kOutput, calls=%fused_computation.6 | convolution fusion | flops 3363306496 | bytes 11150336 | tf_op jit(solution)/shard_map/dot_general | solution.py:139
  164.0 0.8 fusion.8
  164.9 0.0 copy-done.1
  164.9 1.0 fusion.11
  165.9 2.9 %reshape.194 = bf16[256,5120]{1,0:T(8,128)(2,1)} reshape(bf16[1024,1280]{1,0:T(8,128)(2,1)S(1)} %fusion.11) | data formatting | bytes 5242880 | tf_op jit(solution)/shard_map/reshape | solution.py:148
  168.8 9.4 %all-gather.3.cloned.1.call-done = bf16[2048,5120]{1,0:T(8,128)(2,1)} async-done(((bf16[16,5120]{1,0:T(8,128)(2,1)}), bf16[2048,5120]{1,0:T(8,128)(2,1)}) %all-gather.3.cloned.1.call-update) | async-done | bytes 20971536 | tf_op jit(solution)/shard_map/all_gather | solution.py:110
  178.2 11.7 %fusion.42 = f32[2048,256]{1,0:T(8,128)} fusion(bf16[2048,5120]{1,0:T(8,128)(2,1)} %all-gather.3.cloned.1.call-done, bf16[256,5120]{1,0:T(8,128)(2,1)} %reshape.194), kind=kOutput, calls=%fused_computation.77 | convolution fusion | flops 5368709120 | bytes 25690112 | tf_op jit(solution)/shard_map/dot_general | solution.py:27
  189.9 1.6 reshape.196
  191.5 0.6 convolution_convert_fusion.2
  192.2 1.2 reshape.197
  193.4 0.0 all-to-all-done
  193.4 7.3 %all-to-all-start.1 = ((bf16[128,4,1280]{2,1,0:T(4,128)(2,1)}), bf16[128,4,1280]{2,1,0:T(4,128)(2,1)S(1)}, u32[]{:S(2)}, u32[]{:S(2)}) async-start(bf16[128,4,1280]{2,1,0:T(4,128)(2,1)} %reshape.197), calls=%async_computation.1 | async-start | bytes 2621440 | tf_op jit(solution)/shard_map/all_to_all | solution.py:178
  200.7 0.5 broadcast.200
  201.2 0.8 reduce.4
  202.0 0.1 eq.108
  202.1 19.9 %all-to-all-done.1 = bf16[128,4,1280]{2,1,0:T(4,128)(2,1)S(1)} async-done(((bf16[128,4,1280]{2,1,0:T(4,128)(2,1)}), bf16[128,4,1280]{2,1,0:T(4,128)(2,1)S(1)}, u32[]{:S(2)}, u32[]{:S(2)}) %all-to-all-start.1) | async-done | bytes 1310752 | tf_op jit(solution)/shard_map/all_to_all | solution.py:178
  222.1 0.3 reshape.198
  222.4 1.3 convolution_convert_fusion.3
  (22 shorter events, 0.1 us)
Async XLA Ops:
  6.5 23.2 %copy-start = (bf16[1024,1280]{1,0:T(8,128)(2,1)S(1)}, bf16[1024,1280]{1,0:T(8,128)(2,1)}, u32[]{:S(2)}) copy-start(bf16[1024,1280]{1,0:T(8,128)(2,1)} %param.14) | copy-start | bytes 7864324
  6.5 82.0 %all-gather.5.cloned.1.call-start = ((), (), s32[]{:S(2)}) async-start(), calls=%async_computation.3 | async-start | bytes 13209600 | tf_op jit(solution)/shard_map/all_gather | solution.py:106
  8.3 169.9 %all-gather.3.cloned.1.call-start = ((), (), s32[]{:S(2)}) async-start(), calls=%async_computation.2 | async-start | bytes 21135360 | tf_op jit(solution)/shard_map/all_gather | solution.py:110
  14.3 179.1 %all-to-all-start = ((s32[128,1,4]{2,1,0:T(1,128)}), s32[128,1,4]{2,1,0:T(1,128)S(1)}, u32[]{:S(2)}, u32[]{:S(2)}) async-start(s32[128,1,4]{2,1,0:T(1,128)} %bitcast.4), calls=%async_computation | async-start | bytes 131072 | tf_op jit(solution)/shard_map/all_to_all | solution.py:174
  88.6 10.7 %copy-start.4 = (f32[3840]{0:T(1024)S(1)}, f32[3840]{0:T(1024)}, u32[]{:S(2)}) copy-start(f32[3840]{0:T(1024)} %param.19) | copy-start | bytes 46084
  88.6 10.7 %copy-start.5 = (f32[1280]{0:T(1024)S(1)}, f32[1280]{0:T(1024)}, u32[]{:S(2)}) copy-start(f32[1280]{0:T(1024)} %param.17) | copy-start | bytes 15364
  88.6 10.7 %copy-start.6 = (f32[1280]{0:T(1024)S(1)}, f32[1280]{0:T(1024)}, u32[]{:S(2)}) copy-start(f32[1280]{0:T(1024)} %param.16) | copy-start | bytes 15364
  151.2 8.6 %copy-start.7 = (f32[1280]{0:T(1024)S(1)}, f32[1280]{0:T(1024)}, u32[]{:S(2)}) copy-start(f32[1280]{0:T(1024)} %param.21) | copy-start | bytes 15364
  151.2 8.6 %copy-start.8 = (bf16[1280,1024]{1,0:T(8,128)(2,1)S(1)}, bf16[1280,1024]{1,0:T(8,128)(2,1)}, u32[]{:S(2)}) copy-start(bf16[1280,1024]{1,0:T(8,128)(2,1)} %shard_map.136) | copy-start | bytes 7864324
  159.8 5.1 %copy-start.1 = (f32[1280]{0:T(1024)S(1)}, f32[1280]{0:T(1024)}, u32[]{:S(2)}) copy-start(f32[1280]{0:T(1024)} %param.23) | copy-start | bytes 15364
  159.8 5.1 %copy-start.2 = (f32[1280]{0:T(1024)S(1)}, f32[1280]{0:T(1024)}, u32[]{:S(2)}) copy-start(f32[1280]{0:T(1024)} %param.22) | copy-start | bytes 15364
  168.8 22.7 %copy-start.3 = (f32[1280]{0:T(1024)S(1)}, f32[1280]{0:T(1024)}, u32[]{:S(2)}) copy-start(f32[1280]{0:T(1024)} %param.25) | copy-start | bytes 15364
  193.4 28.7 %all-to-all-start.1 = ((bf16[128,4,1280]{2,1,0:T(4,128)(2,1)}), bf16[128,4,1280]{2,1,0:T(4,128)(2,1)S(1)}, u32[]{:S(2)}, u32[]{:S(2)}) async-start(bf16[128,4,1280]{2,1,0:T(4,128)(2,1)} %reshape.197), calls=%async_computation.1 | async-start | bytes 2621440 | tf_op jit(solution)/shard_map/all_to_all | solution.py:178
Sparse Core Ops, SparseCore 0:
  10.3 78.1 all-gather.4
  91.5 86.6 all-gather.2
